TPU v7x, 256 devices: a whole 4x4x8 slice. The times are simulated.
256 devices in a mesh: tm: 32 (over z, y), expert: 8 (over x, core).
Axes of the slice: x: 4, y: 4, z: 8, core: 2. Of those that a mesh axis runs over, the one named last changes fastest.
Arguments:
- frames: bfloat16 [8, 8192, 1024], P('expert', 'tm'), may hold values from -6 to 6
- utt_lengths: int32 [8, 32], P('expert'), may hold values from 1 to 512, 8192 in all within a row
- expert_ids: int32 [8, 8192, 1], P('expert', 'tm'), may hold values from 0 to 63; in each aligned block of 256 rows (0 to 255, 256 to 511, ..., all dimensions but the last counted through in order) at most 8 rows name the same one
- point_in: bfloat16 [1024, 2048], replicated, may hold values from -0.1875 to 0.1875
- depth_taps: float32 [31, 1024], replicated, may hold values from -1 to 1
- norm_scale: float32 [1024], replicated, may hold values from 0.5 to 2
- norm_shift: float32 [1024], replicated, may hold values from -3 to 3
- point_out: bfloat16 [1024, 1024], replicated, may hold values from -0.1875 to 0.1875
- router: bfloat16 [1024, 64], replicated, may hold values from -0.1875 to 0.1875
- expert_in: bfloat16 [8, 32, 1024, 1024], P('expert', 'tm'), may hold values from -0.1875 to 0.1875
- expert_out: bfloat16 [8, 32, 1024, 1024], P('expert', 'tm'), may hold values from -0.09375 to 0.09375
Outputs:
- layer_out: bfloat16 [8, 8192, 1024], P('expert', 'tm')
Inputs may be any that keep to these rules, and one draw needn't show every extreme that they name: `expert_ids`: in the 256 frames of one device (aligned blocks of a stream) no expert is named more than 8 times; in some such blocks one expert is named exactly 8 times. `utt_lengths`: the lengths of each stream sum to 8192; the longest is exactly 512.
All inputs are finite; a program needn't handle non-finite values.
Results may differ from a plain program's by a relative error of at most 0.006.
Values may be sent and summed in bfloat16 or wider, within the bound.
No kernel may reach another device: no remote copies, remote signals or barrier semaphores. Data moves between devices by JAX's collectives and lax.ppermute only.
A program may use at most 64 MiB of HBM per device.

v0:
```python
import jax
import jax.numpy as jnp
from jax import lax
from jax.sharding import PartitionSpec as P

QUARTERS = 4


def padded_2(cells, sides, width):
    for axis, dim in sides:
        count = lax.axis_size(axis)
        ends = count - 1
        head = lax.slice_in_dim(cells, 0, width, axis=dim)
        tail = lax.slice_in_dim(cells, cells.shape[dim] - width, cells.shape[dim], axis=dim)
        cells = jnp.concatenate(
            [
                lax.ppermute(tail, axis, [(i, (i + 1) % count) for i in range(ends)]),
                cells,
                lax.ppermute(head, axis, [((i + 1) % count, i) for i in range(ends)]),
            ],
            axis=dim,
        )
    return cells


def layer_norm(values):
    values = values.astype(jnp.float32)
    center = values - jnp.mean(values, axis=-1, keepdims=True)
    variance = jnp.mean(center * center, axis=-1, keepdims=True)
    return center * lax.rsqrt(variance + 1e-05)


def expert_pass(slot_block, w_in, w_out):
    slot_rows = slot_block.reshape(-1, slot_block.shape[-1])
    hidden = jax.nn.silu(jnp.dot(slot_rows, w_in, preferred_element_type=jnp.float32)).astype(
        jnp.bfloat16
    )
    partial_out = jnp.dot(hidden, w_out, preferred_element_type=jnp.float32).astype(jnp.bfloat16)
    return partial_out.reshape(slot_block.shape)


def shards(
    frames,
    utt_lengths,
    expert_ids,
    point_in,
    depth_taps,
    norm_scale,
    norm_shift,
    point_out,
    router,
    expert_in,
    expert_out,
):
    signal = frames[0]
    frame_count, model_width = signal.shape
    tap_count = depth_taps.shape[0]
    half_span = (tap_count - 1) // 2
    normed = layer_norm(signal).astype(jnp.bfloat16)
    projected = jnp.dot(normed, point_in, preferred_element_type=jnp.float32)
    gated_act = (projected[:, :model_width] * jax.nn.sigmoid(projected[:, model_width:])).astype(
        jnp.bfloat16
    )
    padded = padded_2(gated_act, (("tm", 0),), half_span)
    lengths = utt_lengths[0]
    utter_ends = jnp.cumsum(lengths, dtype=jnp.int32)
    utter_starts = utter_ends - lengths
    position = lax.axis_index("tm") * frame_count + jnp.arange(frame_count, dtype=jnp.int32)
    inside = (utter_starts[None, :] <= position[:, None]) & (
        position[:, None] < utter_ends[None, :]
    )
    first_pos = jnp.sum(jnp.where(inside, utter_starts[None, :], 0), axis=1, dtype=jnp.int32)
    last_pos = jnp.sum(jnp.where(inside, utter_ends[None, :], 0), axis=1, dtype=jnp.int32)
    depth_sum = jnp.zeros((frame_count, model_width), jnp.float32)
    for tap_index in range(tap_count):
        nearby = position + (tap_index - half_span)
        inside_tap = ((nearby >= first_pos) & (nearby < last_pos)).astype(jnp.float32)
        window = padded[tap_index : tap_index + frame_count].astype(jnp.float32)
        depth_sum = depth_sum + depth_taps[tap_index][None, :] * window * inside_tap[:, None]
    activated = jax.nn.silu(depth_sum * norm_scale[None, :] + norm_shift[None, :]).astype(
        jnp.bfloat16
    )
    mixed_res = (
        signal.astype(jnp.float32)
        + jnp.dot(activated, point_out, preferred_element_type=jnp.float32)
    ).astype(jnp.bfloat16)
    moe_in = layer_norm(mixed_res).astype(jnp.bfloat16)
    route_ids = expert_ids[0, :, 0]
    expert_count = router.shape[1]
    capacity = 2 * frame_count // expert_count
    owners = lax.axis_size("expert")
    per_owner = expert_count // owners
    labels = jnp.arange(expert_count, dtype=jnp.int32)
    onehot = (route_ids[:, None] == labels[None, :]).astype(jnp.int32)
    earlier = jnp.cumsum(onehot, axis=0, dtype=jnp.int32) - onehot
    rank_in = jnp.sum(earlier * onehot, axis=1, dtype=jnp.int32)
    logits = jnp.dot(moe_in, router, preferred_element_type=jnp.float32)
    gate_value = jax.nn.sigmoid(jnp.sum(logits * onehot.astype(jnp.float32), axis=1))
    owner_group = route_ids // per_owner
    member = route_ids % per_owner
    slot_index = (member * owners + owner_group) * capacity + rank_in
    send_buffer = (
        jnp.zeros((per_owner * owners * capacity, model_width), jnp.bfloat16)
        .at[slot_index]
        .set(moe_in)
    )
    send_buffer = send_buffer.reshape(per_owner, owners, capacity, model_width)
    w_in = expert_in[0, 0]
    w_out = expert_out[0, 0]
    copies = jnp.repeat(
        lax.all_to_all(send_buffer, "expert", split_axis=1, concat_axis=1, tiled=True),
        QUARTERS,
        axis=0,
    )
    partial_out = expert_pass(
        lax.all_to_all(copies, "tm", split_axis=0, concat_axis=0, tiled=True), w_in, w_out
    )
    returned = lax.all_to_all(partial_out, "tm", split_axis=0, concat_axis=0, tiled=True)
    by_quarter = returned.reshape(per_owner, QUARTERS, owners, returned.shape[2], model_width)
    summed = jnp.sum(by_quarter.astype(jnp.float32), axis=1).astype(jnp.bfloat16)
    results = lax.all_to_all(summed, "expert", split_axis=1, concat_axis=1, tiled=True)
    frame_moe = results.reshape(-1, model_width)[slot_index]
    layer_out = mixed_res.astype(jnp.float32) + gate_value[:, None] * frame_moe.astype(jnp.float32)
    return layer_out.astype(jnp.bfloat16)[None]


def solution(mesh):
    return jax.shard_map(
        shards,
        mesh=mesh,
        in_specs=(
            P("expert", "tm", None),
            P("expert", None),
            P("expert", "tm", None),
            P(),
            P(),
            P(),
            P(),
            P(),
            P(),
            P("expert", "tm", None, None),
            P("expert", "tm", None, None),
        ),
        out_specs=P("expert", "tm", None),
        check_vma=False,
    )
```

profile of v0, /device:TPU:1, one launch (start us, length us, event | category | flops | bytes accessed | tf_op | source)
XLA Modules:
  0.0 314.5 jit_solution(14524343699067483412)
XLA Ops:
  0.0 0.0 copy-start
  0.0 1.3 convert_reduce_fusion.1
  1.3 1.3 fusion.18
  2.7 0.0 copy-start.4
  2.7 0.0 copy-start.6
  2.7 0.0 copy-start.5
  2.7 0.0 copy-start.2
  2.7 0.0 copy-start.8
  2.7 0.0 copy-start.9
  2.8 3.8 %fusion.27 = f32[256,2048]{1,0:T(8,128)S(1)} fusion(bf16[1024,2048]{1,0:T(8,128)(2,1)} %param.14, bf16[1,256,1024]{2,1,0:T(8,128)(2,1)} %param.11, f32[256]{0:T(256)S(1)} %add_rsqrt_fusion.1, f32[256]{0:T(256)S(1)} %broadcast_multiply_fusion.1), kind=kOutput, calls=%fused_computation.64 | convolution fusion | flops 1074790400 | bytes 6817792 | tf_op jit(solution)/shard_map/dot_general | solution.py:60
  6.5 0.3 fusion.25
  6.8 0.0 copy-start.3
  6.8 0.8 copy-done.3
  7.6 4.0 %collective-permute-start = (bf16[15,1024]{1,0:T(8,128)(2,1)S(1)}, bf16[15,1024]{1,0:T(8,128)(2,1)S(1)}, u32[]{:S(2)}, u32[]{:S(2)}) collective-permute-start(bf16[15,1024]{1,0:T(8,128)(2,1)S(1)} %get-tuple-element.7), channel_id=1, source_target_pairs={{0,8},{8,16},{16,24},{24,32},{32,40},{40,48},{48,56},{56,64},{64,7... | collective-permute-start | bytes 92168 | tf_op jit(solution)/shard_map/ppermute | solution.py:17
  11.7 1.3 collective-permute-start.1
  13.0 0.0 copy-done.4
  13.0 0.1 fusion.73
  13.1 0.0 copy-done.6
  13.1 0.1 copy.31
  13.2 0.1 reduce-window.10
  13.2 0.1 reduce.2
  13.4 0.0 copy-done.5
  13.4 0.6 reduce-window.11
  14.0 0.2 slice_reduce_fusion
  14.2 0.1 select_reduce_fusion.1
  14.4 0.1 fusion.62
  14.5 0.0 collective-permute-done
  14.5 1.8 collective-permute-done.1
  16.3 0.0 copy-done.2
  16.3 0.0 copy-done.8
  16.3 0.0 copy-done.9
  16.3 22.8 %convert_reduce_fusion = (f32[256]{0:T(256)S(1)}, bf16[256,1024]{1,0:T(8,128)(2,1)S(1)}) fusion(bf16[1024,1024]{1,0:T(8,128)(2,1)} %param.18, bf16[256,1024]{1,0:T(8,128)(2,1)} %copy-done.3, bf16[15,1024]{1,0:T(8,128)(2,1)S(1)} %collective-permute-done.1, bf16[15,1024]{1,0:T(8,128)(2,1)S(1)} %collective-permute-done, f32[1024]{0:T(1024)S(1)} %copy-done.8, ...), kind=kOutput, calls=%fused_computation.39 | convolution fusion | flops 595853056 | bytes 3899392 | tf_op jit(solution)/shard_map/dot_general | solution.py:85
  39.1 0.0 copy-start.1
  39.1 0.3 fusion.16
  39.4 2.8 scatter_custom_fusion
  42.3 1.3 copy.33
  43.6 21.3 %all_to_all.20 = bf16[8,8,8,1024]{3,2,0,1:T(8,128)(2,1)S(1)} all-to-all(bf16[8,8,8,1024]{3,2,0,1:T(8,128)(2,1)S(1)} %copy.33), channel_id=1, replica_groups=mesh['tm'=32,'expert'=8] {'expert'}, dimensions={1} | all-to-all | bytes 2097152 | tf_op jit(solution)/shard_map/all_to_all | solution.py:111
  64.9 0.1 copy.34
  64.9 0.5 broadcast_in_dim.22
  65.5 106.1 %all_to_all.21 = bf16[32,8,8,1024]{3,2,1,0:T(8,128)(2,1)} all-to-all(bf16[32,8,8,1024]{3,2,1,0:T(8,128)(2,1)S(1)} %bitcast.109), channel_id=1, replica_groups=mesh['tm'=32,'expert'=8] {'tm'}, dimensions={0} | all-to-all | bytes 8388608 | tf_op jit(solution)/shard_map/all_to_all | solution.py:116
  171.6 0.0 copy-done
  171.6 13.0 %fusion.1 = bf16[2048,1024]{1,0:T(8,128)(2,1)} fusion(bf16[1,1,1024,1024]{3,2,1,0:T(8,128)(2,1)S(1)} %copy-done, bf16[2048,1024]{1,0:T(8,128)(2,1)} %bitcast.110, bf16[1,1,1024,1024]{3,2,1,0:T(8,128)(2,1)} %param.20), kind=kOutput, calls=%fused_computation.5 | convolution fusion | flops 8602517504 | bytes 12582912 | tf_op jit(solution)/shard_map/dot_general | solution.py:38
  184.6 98.6 %all_to_all.22 = bf16[32,8,8,1024]{3,2,1,0:T(8,128)(2,1)S(1)} all-to-all(bf16[32,8,8,1024]{3,2,1,0:T(8,128)(2,1)} %bitcast.111), channel_id=1, replica_groups=mesh['tm'=32,'expert'=8] {'tm'}, dimensions={0} | all-to-all | bytes 8388608 | tf_op jit(solution)/shard_map/all_to_all | solution.py:118
  283.2 0.0 copy-start.7
  283.2 0.9 bitcast_reduce_fusion
  284.2 1.1 copy.35
  285.3 8.4 %all-to-all-start.3 = ((bf16[8,8,8,1024]{3,2,0,1:T(8,128)(2,1)}), bf16[8,8,8,1024]{3,2,0,1:T(8,128)(2,1)}, u32[]{:S(2)}, u32[]{:S(2)}) async-start(bf16[8,8,8,1024]{3,2,0,1:T(8,128)(2,1)} %copy.35), calls=%async_computation.3 | async-start | bytes 2097152 | tf_op jit(solution)/shard_map/all_to_all | solution.py:121
  293.8 0.0 copy-done.1
  293.8 0.0 copy-done.7
  293.8 0.4 fusion.15
  294.2 14.8 %all-to-all-done.3 = bf16[8,8,8,1024]{3,2,0,1:T(8,128)(2,1)} async-done(((bf16[8,8,8,1024]{3,2,0,1:T(8,128)(2,1)}), bf16[8,8,8,1024]{3,2,0,1:T(8,128)(2,1)}, u32[]{:S(2)}, u32[]{:S(2)}) %all-to-all-start.3) | async-done | bytes 1048608 | tf_op jit(solution)/shard_map/all_to_all | solution.py:121
  309.0 1.3 copy.36
  310.3 2.0 gather_fusion
  312.2 2.2 fusion.26
  (15 shorter events, 0.2 us)
Async XLA Ops:
  0.0 171.6 %copy-start = (bf16[1,1,1024,1024]{3,2,1,0:T(8,128)(2,1)S(1)}, bf16[1,1,1024,1024]{3,2,1,0:T(8,128)(2,1)}, u32[]{:S(2)}) copy-start(bf16[1,1,1024,1024]{3,2,1,0:T(8,128)(2,1)} %param.21) | copy-start | bytes 6291460
  2.7 10.3 %copy-start.4 = (f32[31,1024]{1,0:T(8,128)S(1)}, f32[31,1024]{1,0:T(8,128)}, u32[]{:S(2)}) copy-start(f32[31,1024]{1,0:T(8,128)} %param.15) | copy-start | bytes 380932
  2.7 10.4 %copy-start.6 = (s32[1,32]{1,0:T(1,128)S(1)}, s32[1,32]{1,0:T(1,128)}, u32[]{:S(2)}) copy-start(s32[1,32]{1,0:T(1,128)} %param.12) | copy-start | bytes 388
  2.7 10.7 %copy-start.5 = (s32[1,256,1]{1,2,0:T(1,128)S(1)}, s32[1,256,1]{1,2,0:T(1,128)}, u32[]{:S(2)}) copy-start(s32[1,256,1]{1,2,0:T(1,128)} %param.13) | copy-start | bytes 3076
  2.7 13.6 %copy-start.2 = (bf16[1,256,1024]{2,1,0:T(8,128)(2,1)S(1)}, bf16[1,256,1024]{2,1,0:T(8,128)(2,1)}, u32[]{:S(2)}) copy-start(bf16[1,256,1024]{2,1,0:T(8,128)(2,1)} %param.11) | copy-start | bytes 1572868
  2.7 13.6 %copy-start.8 = (f32[1024]{0:T(1024)S(1)}, f32[1024]{0:T(1024)}, u32[]{:S(2)}) copy-start(f32[1024]{0:T(1024)} %param.17) | copy-start | bytes 12292
  2.7 13.6 %copy-start.9 = (f32[1024]{0:T(1024)S(1)}, f32[1024]{0:T(1024)}, u32[]{:S(2)}) copy-start(f32[1024]{0:T(1024)} %param.16) | copy-start | bytes 12292
  6.8 0.8 copy-start.3
  7.6 6.9 %collective-permute-start = (bf16[15,1024]{1,0:T(8,128)(2,1)S(1)}, bf16[15,1024]{1,0:T(8,128)(2,1)S(1)}, u32[]{:S(2)}, u32[]{:S(2)}) collective-permute-start(bf16[15,1024]{1,0:T(8,128)(2,1)S(1)} %get-tuple-element.7), channel_id=1, source_target_pairs={{0,8},{8,16},{16,24},{24,32},{32,40},{40,48},{48,56},{56,64},{64,7... | collective-permute-start | bytes 92168 | tf_op jit(solution)/shard_map/ppermute | solution.py:17
  11.7 4.7 %collective-permute-start.1 = (bf16[15,1024]{1,0:T(8,128)(2,1)S(1)}, bf16[15,1024]{1,0:T(8,128)(2,1)S(1)}, u32[]{:S(2)}, u32[]{:S(2)}) collective-permute-start(bf16[15,1024]{1,0:T(8,128)(2,1)S(1)} %get-tuple-element.8), channel_id=1, source_target_pairs={{8,0},{16,8},{24,16},{32,24},{40,32},{48,40},{56,48},{64,56},{72,6... | collective-permute-start | bytes 92168 | tf_op jit(solution)/shard_map/ppermute | solution.py:19
  39.1 254.6 %copy-start.1 = (bf16[256,1024]{1,0:T(8,128)(2,1)}, bf16[256,1024]{1,0:T(8,128)(2,1)S(1)}, u32[]{:S(2)}) copy-start(bf16[256,1024]{1,0:T(8,128)(2,1)S(1)} %get-tuple-element.72) | copy-start | bytes 1572868
  283.2 10.5 %copy-start.7 = (bf16[1024,64]{0,1:T(8,128)(2,1)S(1)}, bf16[1024,64]{0,1:T(8,128)(2,1)}, u32[]{:S(2)}) copy-start(bf16[1024,64]{0,1:T(8,128)(2,1)} %param.19) | copy-start | bytes 393220
  285.3 23.6 %all-to-all-start.3 = ((bf16[8,8,8,1024]{3,2,0,1:T(8,128)(2,1)}), bf16[8,8,8,1024]{3,2,0,1:T(8,128)(2,1)}, u32[]{:S(2)}, u32[]{:S(2)}) async-start(bf16[8,8,8,1024]{3,2,0,1:T(8,128)(2,1)} %copy.35), calls=%async_computation.3 | async-start | bytes 2097152 | tf_op jit(solution)/shard_map/all_to_all | solution.py:121
where the time goes:
time: 315 us; the launch traced here: 314 us
  blocking collectives  226 us (72%)
  matrix products  40 us (13%)
  waiting for transfers between devices  16.6 us (5%)
  starting transfers between devices  13.7 us (4%)
  other arithmetic  10.4 us (3%)
  local copies, waits for them, and re-layouts  7.54 us (2%)
    all_to_all x1, blocking collectives, shards(): lax.all_to_all(copies, 'tm', split_axis=0, concat_axis=0, tiled=True)  106 us
    all_to_all x1, blocking collectives, shards(): lax.all_to_all(partial_out, 'tm', split_axis=0, concat_axis=0, tiled=True)  98.6 us
    dot_general x1, matrix products, shards(): jnp.dot(activated, point_out, preferred_element_type=jnp.float32)  22.8 us
    all_to_all x1, blocking collectives, shards(): lax.all_to_all(send_buffer, 'expert', split_axis=1, concat_axis=1, tiled=...  21.3 us
    all_to_all x1, waiting for transfers between devices, shards(): lax.all_to_all(summed, 'expert', split_axis=1, concat_axis=1, tiled=True)  14.8 us
    dot_general x1, matrix products, expert_pass(): jnp.dot(hidden, w_out, preferred_element_type=jnp.float32)  13 us
    all_to_all x1, starting transfers between devices, shards(): lax.all_to_all(summed, 'expert', split_axis=1, concat_axis=1, tiled=True)  8.42 us
  transfers between devices with their start and end apart: 3, of which 2 were waited for; matrix products, arithmetic and copies ran while one was open for 1% of the time, Pallas kernels for 0%

commit v1 on v0

--- a/solution.py
+++ b/solution.py
@@ -1,7 +1,7 @@
 import jax
 import jax.numpy as jnp
 from jax import lax
-from jax.sharding import PartitionSpec as P
+from jax.sharding import Mesh, PartitionSpec as P
 
 QUARTERS = 4
 
@@ -61,11 +61,11 @@
     gated_act = (projected[:, :model_width] * jax.nn.sigmoid(projected[:, model_width:])).astype(
         jnp.bfloat16
     )
-    padded = padded_2(gated_act, (("tm", 0),), half_span)
+    padded = padded_2(gated_act, ((("z", "y"), 0),), half_span)
     lengths = utt_lengths[0]
     utter_ends = jnp.cumsum(lengths, dtype=jnp.int32)
     utter_starts = utter_ends - lengths
-    position = lax.axis_index("tm") * frame_count + jnp.arange(frame_count, dtype=jnp.int32)
+    position = (lax.axis_index("z") * lax.axis_size("y") + lax.axis_index("y")) * frame_count + jnp.arange(frame_count, dtype=jnp.int32)
     inside = (utter_starts[None, :] <= position[:, None]) & (
         position[:, None] < utter_ends[None, :]
     )
@@ -107,40 +107,43 @@
     send_buffer = send_buffer.reshape(per_owner, owners, capacity, model_width)
     w_in = expert_in[0, 0]
     w_out = expert_out[0, 0]
-    copies = jnp.repeat(
-        lax.all_to_all(send_buffer, "expert", split_axis=1, concat_axis=1, tiled=True),
-        QUARTERS,
-        axis=0,
-    )
-    partial_out = expert_pass(
-        lax.all_to_all(copies, "tm", split_axis=0, concat_axis=0, tiled=True), w_in, w_out
-    )
-    returned = lax.all_to_all(partial_out, "tm", split_axis=0, concat_axis=0, tiled=True)
-    by_quarter = returned.reshape(per_owner, QUARTERS, owners, returned.shape[2], model_width)
-    summed = jnp.sum(by_quarter.astype(jnp.float32), axis=1).astype(jnp.bfloat16)
-    results = lax.all_to_all(summed, "expert", split_axis=1, concat_axis=1, tiled=True)
+    by_group = lax.all_to_all(send_buffer, "expert", split_axis=1, concat_axis=1, tiled=True)
+    by_member = lax.all_to_all(by_group, "z", split_axis=0, concat_axis=0, tiled=True)
+    gathered = lax.all_gather(by_member, "y", axis=0, tiled=False)
+    partial_out = expert_pass(gathered, w_in, w_out)
+    returned = lax.all_to_all(partial_out, "y", split_axis=0, concat_axis=0, tiled=False)
+    summed = jnp.sum(returned.astype(jnp.float32), axis=0).astype(jnp.bfloat16)
+    results = lax.all_to_all(summed, "z", split_axis=0, concat_axis=0, tiled=True)
+    results = lax.all_to_all(results, "expert", split_axis=1, concat_axis=1, tiled=True)
     frame_moe = results.reshape(-1, model_width)[slot_index]
     layer_out = mixed_res.astype(jnp.float32) + gate_value[:, None] * frame_moe.astype(jnp.float32)
     return layer_out.astype(jnp.bfloat16)[None]
 
 
 def solution(mesh):
+    tm_size = mesh.shape["tm"]
+    y_size = QUARTERS
+    split_mesh = Mesh(
+        mesh.devices.reshape(tm_size // y_size, y_size, mesh.shape["expert"]), ("z", "y", "expert")
+    )
+    frames_spec = P("expert", ("z", "y"), None)
+    weights_spec = P("expert", ("z", "y"), None, None)
     return jax.shard_map(
         shards,
-        mesh=mesh,
+        mesh=split_mesh,
         in_specs=(
-            P("expert", "tm", None),
+            frames_spec,
             P("expert", None),
-            P("expert", "tm", None),
+            frames_spec,
             P(),
             P(),
             P(),
             P(),
             P(),
             P(),
-            P("expert", "tm", None, None),
-            P("expert", "tm", None, None),
+            weights_spec,
+            weights_spec,
         ),
-        out_specs=P("expert", "tm", None),
+        out_specs=frames_spec,
         check_vma=False,
     )

time: 315 us -> 297 us (0.943)
  blocking collectives: 226 us -> 144 us
  waiting for transfers between devices: 16.6 us -> 64.6 us
  between operations: 0.3 us -> 13.7 us
  other arithmetic: 10.4 us -> 13.8 us
    all_to_all x2 -> x3, blocking collectives: 205 us -> 123 us  [the longest x1 53.6 us: shards(): lax.all_to_all(partial_out, 'y', split_axis=0, concat_axis=0, tiled=False)]
    all_gather x0 -> x1, waiting for transfers between devices: none -> 48 us  [shards(): gathered = lax.all_gather(by_member, 'y', axis=0, tiled=False)]
    reduce_sum x1, other arithmetic: 0.95 us -> 4.41 us  [shards(): summed = jnp.sum(returned.astype(jnp.float32), axis=0).astype(jnp.bfloat16)]
  transfers between devices with their start and end apart: 3 -> 4, of which waited for: 2 -> 3; matrix products, arithmetic and copies ran while one was open for 1% -> 1% of each run, Pallas kernels for 0% -> 0%
where the time goes in v1:
time: 297 us; the launch traced here: 296 us
  blocking collectives  144 us (48%)
  waiting for transfers between devices  64.6 us (22%)
  matrix products  40 us (13%)
  other arithmetic  13.8 us (5%)
  between operations  13.7 us (5%)
  starting transfers between devices  13.4 us (5%)
  local copies, waits for them, and re-layouts  7.01 us (2%)
    all_to_all x1, blocking collectives, shards(): lax.all_to_all(partial_out, 'y', split_axis=0, concat_axis=0, tiled=False)  53.6 us
    all_gather x1, waiting for transfers between devices, shards(): gathered = lax.all_gather(by_member, 'y', axis=0, tiled=False)  48 us
    all_to_all x1, blocking collectives, shards(): lax.all_to_all(by_group, 'z', split_axis=0, concat_axis=0, tiled=True)  36.3 us
    all_to_all x1, blocking collectives, shards(): lax.all_to_all(summed, 'z', split_axis=0, concat_axis=0, tiled=True)  32.7 us
    dot_general x1, matrix products, shards(): jnp.dot(activated, point_out, preferred_element_type=jnp.float32)  22.8 us
    all_to_all x1, blocking collectives, shards(): lax.all_to_all(send_buffer, 'expert', split_axis=1, concat_axis=1, tiled=...  21.3 us
    all_to_all x1, waiting for transfers between devices, shards(): lax.all_to_all(results, 'expert', split_axis=1, concat_axis=1, tiled=True)  14.8 us
    dot_general x1, matrix products, expert_pass(): jnp.dot(hidden, w_out, preferred_element_type=jnp.float32)  13 us
  transfers between devices with their start and end apart: 4, of which 3 were waited for; matrix products, arithmetic and copies ran while one was open for 1% of the time, Pallas kernels for 0%

profile of v1, /device:TPU:1, one launch (start us, length us, event | category | flops | bytes accessed | tf_op | source)
XLA Modules:
  0.0 296.4 jit_solution(1995473942620025814)
XLA Ops:
  6.5 0.0 copy-start
  6.5 0.0 all-gather.3.cloned.1.call-start
  6.5 1.3 convert_reduce_fusion.1
  7.9 1.3 fusion.18
  9.2 0.0 copy-start.4
  9.2 0.0 copy-start.6
  9.2 0.0 copy-start.5
  9.3 0.0 copy-start.2
  9.3 0.0 copy-start.8
  9.3 0.0 copy-start.9
  9.3 3.8 %fusion.27 = f32[256,2048]{1,0:T(8,128)S(1)} fusion(bf16[1024,2048]{1,0:T(8,128)(2,1)} %param.14, bf16[1,256,1024]{2,1,0:T(8,128)(2,1)} %param.11, f32[256]{0:T(256)S(1)} %add_rsqrt_fusion.1, f32[256]{0:T(256)S(1)} %broadcast_multiply_fusion.1), kind=kOutput, calls=%fused_computation.63 | convolution fusion | flops 1074790400 | bytes 6817792 | tf_op jit(solution)/shard_map/dot_general | solution.py:60
  13.1 0.3 fusion.25
  13.4 0.0 copy-start.3
  13.4 0.8 copy-done.3
  14.2 4.0 %collective-permute-start = (bf16[15,1024]{1,0:T(8,128)(2,1)S(1)}, bf16[15,1024]{1,0:T(8,128)(2,1)S(1)}, u32[]{:S(2)}, u32[]{:S(2)}) collective-permute-start(bf16[15,1024]{1,0:T(8,128)(2,1)S(1)} %get-tuple-element.7), channel_id=1, source_target_pairs={{0,8},{8,16},{16,24},{24,32},{32,40},{40,48},{48,56},{56,64},{64,7... | collective-permute-start | bytes 92168 | tf_op jit(solution)/shard_map/ppermute | solution.py:17
  18.2 1.3 collective-permute-start.1
  19.5 0.0 copy-done.4
  19.5 0.1 fusion.73
  19.6 0.0 copy-done.6
  19.7 0.1 copy.31
  19.7 0.1 reduce-window.10
  19.8 0.1 reduce.2
  19.9 0.0 copy-done.5
  20.0 0.6 reduce-window.11
  20.6 0.2 slice_reduce_fusion
  20.8 0.1 select_reduce_fusion.1
  20.9 0.1 fusion.62
  21.1 0.0 collective-permute-done
  21.1 1.8 collective-permute-done.1
  22.9 0.0 copy-done.2
  22.9 0.0 copy-done.8
  22.9 0.0 copy-done.9
  22.9 22.8 %convert_reduce_fusion = (f32[256]{0:T(256)S(1)}, bf16[256,1024]{1,0:T(8,128)(2,1)S(1)}) fusion(bf16[1024,1024]{1,0:T(8,128)(2,1)} %param.18, bf16[256,1024]{1,0:T(8,128)(2,1)} %copy-done.3, bf16[15,1024]{1,0:T(8,128)(2,1)S(1)} %collective-permute-done.1, bf16[15,1024]{1,0:T(8,128)(2,1)S(1)} %collective-permute-done, f32[1024]{0:T(1024)S(1)} %copy-done.8, ...), kind=kOutput, calls=%fused_computation.38 | convolution fusion | flops 595853056 | bytes 3899392 | tf_op jit(solution)/shard_map/dot_general | solution.py:85
  45.7 0.0 copy-start.1
  45.7 0.3 fusion.16
  46.0 2.8 scatter_custom_fusion
  48.8 1.3 copy.33
  50.1 21.3 %all_to_all.25 = bf16[8,8,8,1024]{3,2,0,1:T(8,128)(2,1)S(1)} all-to-all(bf16[8,8,8,1024]{3,2,0,1:T(8,128)(2,1)S(1)} %copy.33), channel_id=1, replica_groups=mesh['z'=8,'y'=4,'expert'=8] {'expert'}, dimensions={1} | all-to-all | bytes 2097152 | tf_op jit(solution)/shard_map/all_to_all | solution.py:110
  71.4 0.1 copy.34
  71.5 36.3 %all_to_all.26 = bf16[8,8,8,1024]{3,2,1,0:T(8,128)(2,1)} all-to-all(bf16[8,8,8,1024]{3,2,1,0:T(8,128)(2,1)S(1)} %copy.34), channel_id=1, replica_groups=mesh['z'=8,'y'=4,'expert'=8] {'z'}, dimensions={0} | all-to-all | bytes 2097152 | tf_op jit(solution)/shard_map/all_to_all | solution.py:111
  107.8 0.0 all-gather.3.cloned.1.call-update
  107.8 48.0 %all-gather.3.cloned.1.call-done = bf16[32,8,8,1024]{3,2,1,0:T(8,128)(2,1)} async-done(((bf16[8,8,8,1024]{3,2,1,0:T(8,128)(2,1)}), bf16[32,8,8,1024]{3,2,1,0:T(8,128)(2,1)}) %all-gather.3.cloned.1.call-update) | async-done | bytes 4194320 | tf_op jit(solution)/shard_map/all_gather | solution.py:112
  155.9 0.0 copy-done
  155.9 13.0 %fusion.1 = bf16[2048,1024]{1,0:T(8,128)(2,1)} fusion(bf16[1,1,1024,1024]{3,2,1,0:T(8,128)(2,1)S(1)} %copy-done, bf16[2048,1024]{1,0:T(8,128)(2,1)} %bitcast.146, bf16[1,1,1024,1024]{3,2,1,0:T(8,128)(2,1)} %param.20), kind=kOutput, calls=%fused_computation.4 | convolution fusion | flops 8602517504 | bytes 12582912 | tf_op jit(solution)/shard_map/dot_general | solution.py:38
  168.9 53.6 %all_to_all.27 = bf16[4,8,8,8,1024]{4,3,2,1,0:T(8,128)(2,1)} all-to-all(bf16[4,8,8,8,1024]{4,3,2,1,0:T(8,128)(2,1)} %bitcast.106), channel_id=1, replica_groups=mesh['z'=8,'y'=4,'expert'=8] {'y'}, dimensions={0} | all-to-all | bytes 8388608 | tf_op jit(solution)/shard_map/all_to_all | solution.py:114
  222.5 4.4 %reduce_sum.95 = bf16[8,8,8,1024]{3,2,1,0:T(8,128)(2,1)} reduce(bf16[4,8,8,8,1024]{4,3,2,1,0:T(8,128)(2,1)} %all_to_all.27, bf16[]{:T(256)} %constant.125.clone.1), dimensions={0}, to_apply=%region_12.13 | reduce | flops 1572864 | bytes 5242882 | tf_op jit(solution)/shard_map/reduce_sum | solution.py:115
  226.9 0.0 copy-start.7
  226.9 32.7 %all_to_all.28 = bf16[8,8,8,1024]{3,2,1,0:T(8,128)(2,1)S(1)} all-to-all(bf16[8,8,8,1024]{3,2,1,0:T(8,128)(2,1)} %reduce_sum.95), channel_id=1, replica_groups=mesh['z'=8,'y'=4,'expert'=8] {'z'}, dimensions={0} | all-to-all | bytes 2097152 | tf_op jit(solution)/shard_map/all_to_all | solution.py:116
  259.6 1.1 copy.35
  260.8 8.1 %all-to-all-start.4 = ((bf16[8,8,8,1024]{3,2,0,1:T(8,128)(2,1)}), bf16[8,8,8,1024]{3,2,0,1:T(8,128)(2,1)}, u32[]{:S(2)}, u32[]{:S(2)}) async-start(bf16[8,8,8,1024]{3,2,0,1:T(8,128)(2,1)} %copy.35), calls=%async_computation.4 | async-start | bytes 2097152 | tf_op jit(solution)/shard_map/all_to_all | solution.py:117
  268.9 0.0 copy-done.1
  268.9 0.0 copy-done.7
  268.9 0.4 fusion.15
  269.3 14.8 %all-to-all-done.4 = bf16[8,8,8,1024]{3,2,0,1:T(8,128)(2,1)} async-done(((bf16[8,8,8,1024]{3,2,0,1:T(8,128)(2,1)}), bf16[8,8,8,1024]{3,2,0,1:T(8,128)(2,1)}, u32[]{:S(2)}, u32[]{:S(2)}) %all-to-all-start.4) | async-done | bytes 1048608 | tf_op jit(solution)/shard_map/all_to_all | solution.py:117
  284.1 1.3 copy.36
  285.4 2.0 gather_fusion
  287.4 2.2 fusion.26
  (15 shorter events, 0.2 us)
Async XLA Ops:
  6.5 149.3 %copy-start = (bf16[1,1,1024,1024]{3,2,1,0:T(8,128)(2,1)S(1)}, bf16[1,1,1024,1024]{3,2,1,0:T(8,128)(2,1)}, u32[]{:S(2)}) copy-start(bf16[1,1,1024,1024]{3,2,1,0:T(8,128)(2,1)} %param.21) | copy-start | bytes 6291460
  6.5 149.3 %all-gather.3.cloned.1.call-start = ((), (), s32[]{:S(2)}) async-start(), calls=%async_computation.5 | async-start | bytes 5242880 | tf_op jit(solution)/shard_map/all_gather | solution.py:112
  9.2 10.3 %copy-start.4 = (f32[31,1024]{1,0:T(8,128)S(1)}, f32[31,1024]{1,0:T(8,128)}, u32[]{:S(2)}) copy-start(f32[31,1024]{1,0:T(8,128)} %param.15) | copy-start | bytes 380932
  9.2 10.4 %copy-start.6 = (s32[1,32]{1,0:T(1,128)S(1)}, s32[1,32]{1,0:T(1,128)}, u32[]{:S(2)}) copy-start(s32[1,32]{1,0:T(1,128)} %param.12) | copy-start | bytes 388
  9.2 10.7 %copy-start.5 = (s32[1,256,1]{1,2,0:T(1,128)S(1)}, s32[1,256,1]{1,2,0:T(1,128)}, u32[]{:S(2)}) copy-start(s32[1,256,1]{1,2,0:T(1,128)} %param.13) | copy-start | bytes 3076
  9.3 13.6 %copy-start.2 = (bf16[1,256,1024]{2,1,0:T(8,128)(2,1)S(1)}, bf16[1,256,1024]{2,1,0:T(8,128)(2,1)}, u32[]{:S(2)}) copy-start(bf16[1,256,1024]{2,1,0:T(8,128)(2,1)} %param.11) | copy-start | bytes 1572868
  9.3 13.6 %copy-start.8 = (f32[1024]{0:T(1024)S(1)}, f32[1024]{0:T(1024)}, u32[]{:S(2)}) copy-start(f32[1024]{0:T(1024)} %param.17) | copy-start | bytes 12292
  9.3 13.6 %copy-start.9 = (f32[1024]{0:T(1024)S(1)}, f32[1024]{0:T(1024)}, u32[]{:S(2)}) copy-start(f32[1024]{0:T(1024)} %param.16) | copy-start | bytes 12292
  13.4 0.8 copy-start.3
  14.2 6.9 %collective-permute-start = (bf16[15,1024]{1,0:T(8,128)(2,1)S(1)}, bf16[15,1024]{1,0:T(8,128)(2,1)S(1)}, u32[]{:S(2)}, u32[]{:S(2)}) collective-permute-start(bf16[15,1024]{1,0:T(8,128)(2,1)S(1)} %get-tuple-element.7), channel_id=1, source_target_pairs={{0,8},{8,16},{16,24},{24,32},{32,40},{40,48},{48,56},{56,64},{64,7... | collective-permute-start | bytes 92168 | tf_op jit(solution)/shard_map/ppermute | solution.py:17
  18.2 4.7 %collective-permute-start.1 = (bf16[15,1024]{1,0:T(8,128)(2,1)S(1)}, bf16[15,1024]{1,0:T(8,128)(2,1)S(1)}, u32[]{:S(2)}, u32[]{:S(2)}) collective-permute-start(bf16[15,1024]{1,0:T(8,128)(2,1)S(1)} %get-tuple-element.8), channel_id=1, source_target_pairs={{8,0},{16,8},{24,16},{32,24},{40,32},{48,40},{56,48},{64,56},{72,6... | collective-permute-start | bytes 92168 | tf_op jit(solution)/shard_map/ppermute | solution.py:19
  45.7 223.2 %copy-start.1 = (bf16[256,1024]{1,0:T(8,128)(2,1)}, bf16[256,1024]{1,0:T(8,128)(2,1)S(1)}, u32[]{:S(2)}) copy-start(bf16[256,1024]{1,0:T(8,128)(2,1)S(1)} %get-tuple-element.72) | copy-start | bytes 1572868
  226.9 41.9 %copy-start.7 = (bf16[1024,64]{0,1:T(8,128)(2,1)S(1)}, bf16[1024,64]{0,1:T(8,128)(2,1)}, u32[]{:S(2)}) copy-start(bf16[1024,64]{0,1:T(8,128)(2,1)} %param.19) | copy-start | bytes 393220
  260.8 23.3 %all-to-all-start.4 = ((bf16[8,8,8,1024]{3,2,0,1:T(8,128)(2,1)}), bf16[8,8,8,1024]{3,2,0,1:T(8,128)(2,1)}, u32[]{:S(2)}, u32[]{:S(2)}) async-start(bf16[8,8,8,1024]{3,2,0,1:T(8,128)(2,1)} %copy.35), calls=%async_computation.4 | async-start | bytes 2097152 | tf_op jit(solution)/shard_map/all_to_all | solution.py:117
Sparse Core Ops, SparseCore 0:
  108.0 47.8 all-gather.2

commit v2 on v1

--- a/solution.py
+++ b/solution.py
@@ -21,6 +21,18 @@
             axis=dim,
         )
     return cells
+
+
+def shifted_exchange(blocks, axis, dim, back=False):
+    count = lax.axis_size(axis)
+    pieces = []
+    for shift in range(count):
+        piece = lax.index_in_dim(blocks, shift, axis=dim, keepdims=True)
+        if shift:
+            step = -shift if back else shift
+            piece = lax.ppermute(piece, axis, [(i, (i + step) % count) for i in range(count)])
+        pieces.append(piece)
+    return jnp.concatenate(pieces, axis=dim)
 
 
 def layer_norm(values):
@@ -96,8 +108,8 @@
     rank_in = jnp.sum(earlier * onehot, axis=1, dtype=jnp.int32)
     logits = jnp.dot(moe_in, router, preferred_element_type=jnp.float32)
     gate_value = jax.nn.sigmoid(jnp.sum(logits * onehot.astype(jnp.float32), axis=1))
-    owner_group = route_ids // per_owner
-    member = route_ids % per_owner
+    owner_group = (route_ids // per_owner - lax.axis_index("expert")) % owners
+    member = (route_ids % per_owner - lax.axis_index("z")) % per_owner
     slot_index = (member * owners + owner_group) * capacity + rank_in
     send_buffer = (
         jnp.zeros((per_owner * owners * capacity, model_width), jnp.bfloat16)
@@ -107,14 +119,14 @@
     send_buffer = send_buffer.reshape(per_owner, owners, capacity, model_width)
     w_in = expert_in[0, 0]
     w_out = expert_out[0, 0]
-    by_group = lax.all_to_all(send_buffer, "expert", split_axis=1, concat_axis=1, tiled=True)
-    by_member = lax.all_to_all(by_group, "z", split_axis=0, concat_axis=0, tiled=True)
+    by_group = shifted_exchange(send_buffer, "expert", 1)
+    by_member = shifted_exchange(by_group, "z", 0)
     gathered = lax.all_gather(by_member, "y", axis=0, tiled=False)
     partial_out = expert_pass(gathered, w_in, w_out)
     returned = lax.all_to_all(partial_out, "y", split_axis=0, concat_axis=0, tiled=False)
     summed = jnp.sum(returned.astype(jnp.float32), axis=0).astype(jnp.bfloat16)
-    results = lax.all_to_all(summed, "z", split_axis=0, concat_axis=0, tiled=True)
-    results = lax.all_to_all(results, "expert", split_axis=1, concat_axis=1, tiled=True)
+    results = shifted_exchange(summed, "z", 0, back=True)
+    results = shifted_exchange(results, "expert", 1, back=True)
     frame_moe = results.reshape(-1, model_width)[slot_index]
     layer_out = mixed_res.astype(jnp.float32) + gate_value[:, None] * frame_moe.astype(jnp.float32)
     return layer_out.astype(jnp.bfloat16)[None]

time: 297 us -> 292 us (0.983)
  blocking collectives: 144 us -> 0 us
  waiting for transfers between devices: 64.6 us -> 149 us
  starting transfers between devices: 13.4 us -> 63 us
  local copies, waits for them, and re-layouts: 7.01 us -> 11.5 us
    all_to_all x4 -> x0, blocking collectives: 144 us -> none  [the longest x1 53.6 us: shards(): lax.all_to_all(partial_out, 'y', split_axis=0, concat_axis=0, tiled=False)]
    ppermute x0 -> x28, starting transfers between devices: none -> 52.6 us  [shifted_exchange(): lax.ppermute(piece, axis, [(i, (i + step) % count) for i in range(count)])]
    ppermute x0 -> x28, waiting for transfers between devices: none -> 47.6 us  [shifted_exchange(): lax.ppermute(piece, axis, [(i, (i + step) % count) for i in range(count)])]
    all_to_all x1, waiting for transfers between devices: 14.8 us -> 48 us  [shards(): lax.all_to_all(partial_out, 'y', split_axis=0, concat_axis=0, tiled=False)]
    unnamed x20 -> x44, local copies, waits for them, and re-layouts: 0.84 us -> 4.98 us
    slice x1 -> x5, local copies, waits for them, and re-layouts: 0.18 us -> 3.7 us  [the longest x4 3.52 us: shifted_exchange(): piece = lax.index_in_dim(blocks, shift, axis=dim, keepdims=True)]
    all_gather x1, waiting for transfers between devices: 48 us -> 51.1 us  [shards(): gathered = lax.all_gather(by_member, 'y', axis=0, tiled=False)]
    all_to_all x1, starting transfers between devices: 8.11 us -> 5.06 us  [shards(): lax.all_to_all(partial_out, 'y', split_axis=0, concat_axis=0, tiled=False)]
  transfers between devices with their start and end apart: 4 -> 32, of which waited for: 3 -> 17; matrix products, arithmetic and copies ran while one was open for 1% -> 2% of each run, Pallas kernels for 0% -> 0%
where the time goes in v2:
time: 292 us; the launch traced here: 290 us
  waiting for transfers between devices  149 us (51%)
  starting transfers between devices  63 us (22%)
  matrix products  39.3 us (13%)
  other arithmetic  13.8 us (5%)
  between operations  13.8 us (5%)
  local copies, waits for them, and re-layouts  11.5 us (4%)
    ppermute x28, starting transfers between devices, shifted_exchange(): lax.ppermute(piece, axis, [(i, (i + step) % count) for i in range(count)])  52.6 us
    all_gather x1, waiting for transfers between devices, shards(): gathered = lax.all_gather(by_member, 'y', axis=0, tiled=False)  51.1 us
    all_to_all x1, waiting for transfers between devices, shards(): lax.all_to_all(partial_out, 'y', split_axis=0, concat_axis=0, tiled=False)  48 us
    ppermute x28, waiting for transfers between devices, shifted_exchange(): lax.ppermute(piece, axis, [(i, (i + step) % count) for i in range(count)])  47.6 us
    dot_general x1, matrix products, shards(): jnp.dot(activated, point_out, preferred_element_type=jnp.float32)  22.1 us
    dot_general x1, matrix products, expert_pass(): jnp.dot(hidden, w_out, preferred_element_type=jnp.float32)  13 us
  transfers between devices with their start and end apart: 32, of which 17 were waited for; matrix products, arithmetic and copies ran while one was open for 2% of the time, Pallas kernels for 0%

profile of v2, /device:TPU:1, one launch (start us, length us, event | category | flops | bytes accessed | tf_op | source)
XLA Modules:
  0.0 290.0 jit_solution(17592441873162428102)
XLA Ops:
  6.5 1.3 convert_reduce_fusion.1
  7.9 1.3 fusion.18
  9.3 3.8 %fusion.27 = f32[256,2048]{1,0:T(8,128)S(1)} fusion(bf16[1024,2048]{1,0:T(8,128)(2,1)} %param.14, bf16[1,256,1024]{2,1,0:T(8,128)(2,1)} %param.11, f32[256]{0:T(256)S(1)} %add_rsqrt_fusion.1, f32[256]{0:T(256)S(1)} %broadcast_multiply_fusion.1), kind=kOutput, calls=%fused_computation.63 | convolution fusion | flops 1074790400 | bytes 6817792 | tf_op jit(solution)/shard_map/dot_general | solution.py:72
  13.4 0.8 copy-done.3
  14.2 4.0 %collective-permute-start = (bf16[15,1024]{1,0:T(8,128)(2,1)S(1)}, bf16[15,1024]{1,0:T(8,128)(2,1)S(1)}, u32[]{:S(2)}, u32[]{:S(2)}) collective-permute-start(bf16[15,1024]{1,0:T(8,128)(2,1)S(1)} %get-tuple-element.39), channel_id=1, source_target_pairs={{0,8},{8,16},{16,24},{24,32},{32,40},{40,48},{48,56},{56,64},{64,7... | collective-permute-start | bytes 92168 | tf_op jit(solution)/shard_map/ppermute | solution.py:17
  18.2 1.3 collective-permute-start.1
  20.0 0.6 reduce-window.11
  21.1 1.8 collective-permute-done.1
  22.9 22.1 %convert_reduce_fusion = (f32[256]{0:T(256)S(1)}, bf16[256,1024]{1,0:T(8,128)(2,1)S(1)}) fusion(bf16[1024,1024]{1,0:T(8,128)(2,1)} %param.18, bf16[256,1024]{1,0:T(8,128)(2,1)} %copy-done.3, bf16[15,1024]{1,0:T(8,128)(2,1)S(1)} %collective-permute-done.1, bf16[15,1024]{1,0:T(8,128)(2,1)S(1)} %collective-permute-done, f32[1024]{0:T(1024)S(1)} %copy-done.8, ...), kind=kOutput, calls=%fused_computation.38 | convolution fusion | flops 595853056 | bytes 3899392 | tf_op jit(solution)/shard_map/dot_general | solution.py:97
  45.3 2.8 scatter_custom_fusion
  48.1 1.4 fusion.78
  49.5 3.2 %collective-permute-start.2 = (bf16[8,1,8,1024]{3,2,1,0:T(8,128)(2,1)S(1)}, bf16[8,1,8,1024]{3,2,1,0:T(8,128)(2,1)S(1)}, u32[]{:S(2)}, u32[]{:S(2)}) collective-permute-start(bf16[8,1,8,1024]{3,2,1,0:T(8,128)(2,1)S(1)} %get-tuple-element.37), channel_id=1, source_target_pairs={{0,1},{1,2},{2,3},{3,4},{4,5},{5,6},{6,7},{7,0},{8,9},{9,10},{10,1... | collective-permute-start | bytes 393224 | tf_op jit(solution)/shard_map/ppermute | solution.py:33
  52.7 1.2 collective-permute-start.3
  53.9 1.6 collective-permute-start.4
  56.0 1.9 collective-permute-start.6
  58.0 0.7 collective-permute-start.7
  58.6 1.4 collective-permute-done.3
  60.3 0.6 collective-permute-done.4
  61.0 5.7 %collective-permute-done.5 = bf16[8,1,8,1024]{3,2,1,0:T(8,128)(2,1)S(1)} collective-permute-done((bf16[8,1,8,1024]{3,2,1,0:T(8,128)(2,1)S(1)}, bf16[8,1,8,1024]{3,2,1,0:T(8,128)(2,1)S(1)}, u32[]{:S(2)}, u32[]{:S(2)}) %collective-permute-start.5) | collective-permute-done | bytes 131104 | tf_op jit(solution)/shard_map/ppermute | solution.py:33
  66.7 0.6 collective-permute-done.6
  67.3 0.7 collective-permute-done.8
  68.0 0.7 fusion.77
  68.7 1.9 collective-permute-start.9
  70.7 3.0 %collective-permute-start.10 = (bf16[1,8,8,1024]{3,2,1,0:T(8,128)(2,1)S(1)}, bf16[1,8,8,1024]{3,2,1,0:T(8,128)(2,1)S(1)}, u32[]{:S(2)}, u32[]{:S(2)}) collective-permute-start(bf16[1,8,8,1024]{3,2,1,0:T(8,128)(2,1)S(1)} %get-tuple-element.28), channel_id=1, source_target_pairs={{0,64},{32,96},{64,128},{96,160},{128,192},{160,224},{192,0},{224,... | collective-permute-start | bytes 393224 | tf_op jit(solution)/shard_map/ppermute | solution.py:33
  73.7 3.8 %collective-permute-start.11 = (bf16[1,8,8,1024]{3,2,1,0:T(8,128)(2,1)S(1)}, bf16[1,8,8,1024]{3,2,1,0:T(8,128)(2,1)S(1)}, u32[]{:S(2)}, u32[]{:S(2)}) collective-permute-start(bf16[1,8,8,1024]{3,2,1,0:T(8,128)(2,1)S(1)} %get-tuple-element.27), channel_id=1, source_target_pairs={{0,96},{32,128},{64,160},{96,192},{128,224},{160,0},{192,32},{224,... | collective-permute-start | bytes 393224 | tf_op jit(solution)/shard_map/ppermute | solution.py:33
  77.9 4.5 %collective-permute-start.13 = (bf16[1,8,8,1024]{3,2,1,0:T(8,128)(2,1)S(1)}, bf16[1,8,8,1024]{3,2,1,0:T(8,128)(2,1)S(1)}, u32[]{:S(2)}, u32[]{:S(2)}) collective-permute-start(bf16[1,8,8,1024]{3,2,1,0:T(8,128)(2,1)S(1)} %get-tuple-element.25), channel_id=1, source_target_pairs={{0,160},{32,192},{64,224},{96,0},{128,32},{160,64},{192,96},{224,1... | collective-permute-start | bytes 393224 | tf_op jit(solution)/shard_map/ppermute | solution.py:33
  82.3 2.9 collective-permute-start.14
  85.2 0.7 constant_dynamic-update-slice_fusion.13
  85.9 1.5 collective-permute-start.15
  87.3 0.7 constant_dynamic-update-slice_fusion.12
  88.0 7.1 %collective-permute-done.11 = bf16[1,8,8,1024]{3,2,1,0:T(8,128)(2,1)S(1)} collective-permute-done((bf16[1,8,8,1024]{3,2,1,0:T(8,128)(2,1)S(1)}, bf16[1,8,8,1024]{3,2,1,0:T(8,128)(2,1)S(1)}, u32[]{:S(2)}, u32[]{:S(2)}) %collective-permute-start.11) | collective-permute-done | bytes 131104 | tf_op jit(solution)/shard_map/ppermute | solution.py:33
  95.2 0.7 constant_dynamic-update-slice_fusion.11
  95.8 0.7 constant_dynamic-update-slice_fusion.10
  96.5 0.7 constant_dynamic-update-slice_fusion.9
  97.1 6.3 %collective-permute-done.14 = bf16[1,8,8,1024]{3,2,1,0:T(8,128)(2,1)S(1)} collective-permute-done((bf16[1,8,8,1024]{3,2,1,0:T(8,128)(2,1)S(1)}, bf16[1,8,8,1024]{3,2,1,0:T(8,128)(2,1)S(1)}, u32[]{:S(2)}, u32[]{:S(2)}) %collective-permute-start.14) | collective-permute-done | bytes 131104 | tf_op jit(solution)/shard_map/ppermute | solution.py:33
  103.4 0.7 constant_dynamic-update-slice_fusion.8
  104.1 0.6 constant_dynamic-update-slice_fusion.7
  104.8 51.1 %all-gather.3.cloned.1.call-done = bf16[32,8,8,1024]{3,2,1,0:T(8,128)(2,1)} async-done(((bf16[8,8,8,1024]{3,2,1,0:T(8,128)(2,1)}), bf16[32,8,8,1024]{3,2,1,0:T(8,128)(2,1)}) %all-gather.3.cloned.1.call-update) | async-done | bytes 4194320 | tf_op jit(solution)/shard_map/all_gather | solution.py:124
  155.9 13.0 %fusion.1 = bf16[2048,1024]{1,0:T(8,128)(2,1)} fusion(bf16[1,1,1024,1024]{3,2,1,0:T(8,128)(2,1)S(1)} %copy-done, bf16[2048,1024]{1,0:T(8,128)(2,1)} %bitcast.144, bf16[1,1,1024,1024]{3,2,1,0:T(8,128)(2,1)} %param.20), kind=kOutput, calls=%fused_computation.4 | convolution fusion | flops 8602517504 | bytes 12582912 | tf_op jit(solution)/shard_map/dot_general | solution.py:50
  168.9 5.1 %all-to-all-start = ((bf16[4,8,8,8,1024]{4,3,2,1,0:T(8,128)(2,1)}), bf16[4,8,8,8,1024]{4,3,2,1,0:T(8,128)(2,1)}, u32[]{:S(2)}, u32[]{:S(2)}) async-start(bf16[4,8,8,8,1024]{4,3,2,1,0:T(8,128)(2,1)} %bitcast.104), calls=%async_computation | async-start | bytes 8388608 | tf_op jit(solution)/shard_map/all_to_all | solution.py:126
  174.0 48.0 %all-to-all-done = bf16[4,8,8,8,1024]{4,3,2,1,0:T(8,128)(2,1)} async-done(((bf16[4,8,8,8,1024]{4,3,2,1,0:T(8,128)(2,1)}), bf16[4,8,8,8,1024]{4,3,2,1,0:T(8,128)(2,1)}, u32[]{:S(2)}, u32[]{:S(2)}) %all-to-all-start) | async-done | bytes 4194336 | tf_op jit(solution)/shard_map/all_to_all | solution.py:126
  222.1 4.4 %reduce_sum.95 = bf16[8,8,8,1024]{3,2,1,0:T(8,128)(2,1)} reduce(bf16[4,8,8,8,1024]{4,3,2,1,0:T(8,128)(2,1)} %all-to-all-done, bf16[]{:T(256)} %constant.137.clone.1), dimensions={0}, to_apply=%region_12.13 | reduce | flops 1572864 | bytes 5242882 | tf_op jit(solution)/shard_map/reduce_sum | solution.py:127
  226.5 1.4 fusion.76
  227.8 3.1 %collective-permute-start.16 = (bf16[1,8,8,1024]{3,2,1,0:T(8,128)(2,1)S(1)}, bf16[1,8,8,1024]{3,2,1,0:T(8,128)(2,1)S(1)}, u32[]{:S(2)}, u32[]{:S(2)}) collective-permute-start(bf16[1,8,8,1024]{3,2,1,0:T(8,128)(2,1)S(1)} %get-tuple-element.21), channel_id=1, source_target_pairs={{0,224},{32,0},{64,32},{96,64},{128,96},{160,128},{192,160},{224,1... | collective-permute-start | bytes 393224 | tf_op jit(solution)/shard_map/ppermute | solution.py:33
  230.9 1.9 collective-permute-start.17
  233.2 1.0 collective-permute-start.18
  234.2 3.7 %collective-permute-start.19 = (bf16[1,8,8,1024]{3,2,1,0:T(8,128)(2,1)S(1)}, bf16[1,8,8,1024]{3,2,1,0:T(8,128)(2,1)S(1)}, u32[]{:S(2)}, u32[]{:S(2)}) collective-permute-start(bf16[1,8,8,1024]{3,2,1,0:T(8,128)(2,1)S(1)} %get-tuple-element.18), channel_id=1, source_target_pairs={{0,128},{32,160},{64,192},{96,224},{128,0},{160,32},{192,64},{224,... | collective-permute-start | bytes 393224 | tf_op jit(solution)/shard_map/ppermute | solution.py:33
  237.9 3.0 %collective-permute-start.21 = (bf16[1,8,8,1024]{3,2,1,0:T(8,128)(2,1)S(1)}, bf16[1,8,8,1024]{3,2,1,0:T(8,128)(2,1)S(1)}, u32[]{:S(2)}, u32[]{:S(2)}) collective-permute-start(bf16[1,8,8,1024]{3,2,1,0:T(8,128)(2,1)S(1)} %get-tuple-element.16), channel_id=1, source_target_pairs={{0,64},{32,96},{64,128},{96,160},{128,192},{160,224},{192,0},{224,... | collective-permute-start | bytes 393224 | tf_op jit(solution)/shard_map/ppermute | solution.py:33
  240.9 1.3 collective-permute-start.22
  242.2 2.7 collective-permute-done.18
  245.0 6.3 %collective-permute-done.20 = bf16[1,8,8,1024]{3,2,1,0:T(8,128)(2,1)S(1)} collective-permute-done((bf16[1,8,8,1024]{3,2,1,0:T(8,128)(2,1)S(1)}, bf16[1,8,8,1024]{3,2,1,0:T(8,128)(2,1)S(1)}, u32[]{:S(2)}, u32[]{:S(2)}) %collective-permute-start.20) | collective-permute-done | bytes 131104 | tf_op jit(solution)/shard_map/ppermute | solution.py:33
  251.3 5.7 %collective-permute-done.21 = bf16[1,8,8,1024]{3,2,1,0:T(8,128)(2,1)S(1)} collective-permute-done((bf16[1,8,8,1024]{3,2,1,0:T(8,128)(2,1)S(1)}, bf16[1,8,8,1024]{3,2,1,0:T(8,128)(2,1)S(1)}, u32[]{:S(2)}, u32[]{:S(2)}) %collective-permute-start.21) | collective-permute-done | bytes 131104 | tf_op jit(solution)/shard_map/ppermute | solution.py:33
  257.0 4.3 %collective-permute-done.22 = bf16[1,8,8,1024]{3,2,1,0:T(8,128)(2,1)S(1)} collective-permute-done((bf16[1,8,8,1024]{3,2,1,0:T(8,128)(2,1)S(1)}, bf16[1,8,8,1024]{3,2,1,0:T(8,128)(2,1)S(1)}, u32[]{:S(2)}, u32[]{:S(2)}) %collective-permute-start.22) | collective-permute-done | bytes 131104 | tf_op jit(solution)/shard_map/ppermute | solution.py:33
  261.4 1.8 collective-permute-start.23
  263.2 2.4 collective-permute-start.24
  265.6 0.8 collective-permute-start.25
  266.4 1.2 collective-permute-start.26
  267.7 2.1 collective-permute-start.27
  269.7 0.6 collective-permute-start.28
  270.3 2.4 collective-permute-start.29
  272.8 0.6 collective-permute-done.26
  273.5 5.0 %collective-permute-done.27 = bf16[8,1,8,1024]{3,2,1,0:T(8,128)(2,1)S(1)} collective-permute-done((bf16[8,1,8,1024]{3,2,1,0:T(8,128)(2,1)S(1)}, bf16[8,1,8,1024]{3,2,1,0:T(8,128)(2,1)S(1)}, u32[]{:S(2)}, u32[]{:S(2)}) %collective-permute-start.27) | collective-permute-done | bytes 131104 | tf_op jit(solution)/shard_map/ppermute | solution.py:33
  279.0 2.0 gather_fusion
  280.9 2.2 fusion.26
  (88 shorter events, 4.0 us)
Async XLA Ops:
  6.5 149.4 %copy-start = (bf16[1,1,1024,1024]{3,2,1,0:T(8,128)(2,1)S(1)}, bf16[1,1,1024,1024]{3,2,1,0:T(8,128)(2,1)}, u32[]{:S(2)}) copy-start(bf16[1,1,1024,1024]{3,2,1,0:T(8,128)(2,1)} %param.21) | copy-start | bytes 6291460
  6.5 149.4 %all-gather.3.cloned.1.call-start = ((), (), s32[]{:S(2)}) async-start(), calls=%async_computation.1 | async-start | bytes 5242880 | tf_op jit(solution)/shard_map/all_gather | solution.py:124
  9.2 10.3 %copy-start.4 = (f32[31,1024]{1,0:T(8,128)S(1)}, f32[31,1024]{1,0:T(8,128)}, u32[]{:S(2)}) copy-start(f32[31,1024]{1,0:T(8,128)} %param.15) | copy-start | bytes 380932
  9.2 10.4 %copy-start.6 = (s32[1,32]{1,0:T(1,128)S(1)}, s32[1,32]{1,0:T(1,128)}, u32[]{:S(2)}) copy-start(s32[1,32]{1,0:T(1,128)} %param.12) | copy-start | bytes 388
  9.2 10.7 %copy-start.5 = (s32[1,256,1]{1,2,0:T(1,128)S(1)}, s32[1,256,1]{1,2,0:T(1,128)}, u32[]{:S(2)}) copy-start(s32[1,256,1]{1,2,0:T(1,128)} %param.13) | copy-start | bytes 3076
  9.3 13.6 %copy-start.2 = (bf16[1,256,1024]{2,1,0:T(8,128)(2,1)S(1)}, bf16[1,256,1024]{2,1,0:T(8,128)(2,1)}, u32[]{:S(2)}) copy-start(bf16[1,256,1024]{2,1,0:T(8,128)(2,1)} %param.11) | copy-start | bytes 1572868
  9.3 13.6 %copy-start.8 = (f32[1024]{0:T(1024)S(1)}, f32[1024]{0:T(1024)}, u32[]{:S(2)}) copy-start(f32[1024]{0:T(1024)} %param.17) | copy-start | bytes 12292
  9.3 13.6 %copy-start.9 = (f32[1024]{0:T(1024)S(1)}, f32[1024]{0:T(1024)}, u32[]{:S(2)}) copy-start(f32[1024]{0:T(1024)} %param.16) | copy-start | bytes 12292
  13.4 0.8 copy-start.3
  14.2 6.9 %collective-permute-start = (bf16[15,1024]{1,0:T(8,128)(2,1)S(1)}, bf16[15,1024]{1,0:T(8,128)(2,1)S(1)}, u32[]{:S(2)}, u32[]{:S(2)}) collective-permute-start(bf16[15,1024]{1,0:T(8,128)(2,1)S(1)} %get-tuple-element.39), channel_id=1, source_target_pairs={{0,8},{8,16},{16,24},{24,32},{32,40},{40,48},{48,56},{56,64},{64,7... | collective-permute-start | bytes 92168 | tf_op jit(solution)/shard_map/ppermute | solution.py:17
  18.2 4.7 %collective-permute-start.1 = (bf16[15,1024]{1,0:T(8,128)(2,1)S(1)}, bf16[15,1024]{1,0:T(8,128)(2,1)S(1)}, u32[]{:S(2)}, u32[]{:S(2)}) collective-permute-start(bf16[15,1024]{1,0:T(8,128)(2,1)S(1)} %get-tuple-element.40), channel_id=1, source_target_pairs={{8,0},{16,8},{24,16},{32,24},{40,32},{48,40},{56,48},{64,56},{72,6... | collective-permute-start | bytes 92168 | tf_op jit(solution)/shard_map/ppermute | solution.py:19
  45.0 187.9 %copy-start.1 = (bf16[256,1024]{1,0:T(8,128)(2,1)}, bf16[256,1024]{1,0:T(8,128)(2,1)S(1)}, u32[]{:S(2)}) copy-start(bf16[256,1024]{1,0:T(8,128)(2,1)S(1)} %get-tuple-element.104) | copy-start | bytes 1572868
  49.5 8.5 %collective-permute-start.2 = (bf16[8,1,8,1024]{3,2,1,0:T(8,128)(2,1)S(1)}, bf16[8,1,8,1024]{3,2,1,0:T(8,128)(2,1)S(1)}, u32[]{:S(2)}, u32[]{:S(2)}) collective-permute-start(bf16[8,1,8,1024]{3,2,1,0:T(8,128)(2,1)S(1)} %get-tuple-element.37), channel_id=1, source_target_pairs={{0,1},{1,2},{2,3},{3,4},{4,5},{5,6},{6,7},{7,0},{8,9},{9,10},{10,1... | collective-permute-start | bytes 393224 | tf_op jit(solution)/shard_map/ppermute | solution.py:33
  52.7 7.4 %collective-permute-start.3 = (bf16[8,1,8,1024]{3,2,1,0:T(8,128)(2,1)S(1)}, bf16[8,1,8,1024]{3,2,1,0:T(8,128)(2,1)S(1)}, u32[]{:S(2)}, u32[]{:S(2)}) collective-permute-start(bf16[8,1,8,1024]{3,2,1,0:T(8,128)(2,1)S(1)} %get-tuple-element.36), channel_id=1, source_target_pairs={{0,2},{1,3},{2,4},{3,5},{4,6},{5,7},{6,0},{7,1},{8,10},{9,11},{10,... | collective-permute-start | bytes 393224 | tf_op jit(solution)/shard_map/ppermute | solution.py:33
  53.9 7.1 %collective-permute-start.4 = (bf16[8,1,8,1024]{3,2,1,0:T(8,128)(2,1)S(1)}, bf16[8,1,8,1024]{3,2,1,0:T(8,128)(2,1)S(1)}, u32[]{:S(2)}, u32[]{:S(2)}) collective-permute-start(bf16[8,1,8,1024]{3,2,1,0:T(8,128)(2,1)S(1)} %get-tuple-element.35), channel_id=1, source_target_pairs={{0,3},{1,4},{2,5},{3,6},{4,7},{5,0},{6,1},{7,2},{8,11},{9,12},{10,... | collective-permute-start | bytes 393224 | tf_op jit(solution)/shard_map/ppermute | solution.py:33
  55.5 11.2 %collective-permute-start.5 = (bf16[8,1,8,1024]{3,2,1,0:T(8,128)(2,1)S(1)}, bf16[8,1,8,1024]{3,2,1,0:T(8,128)(2,1)S(1)}, u32[]{:S(2)}, u32[]{:S(2)}) collective-permute-start(bf16[8,1,8,1024]{3,2,1,0:T(8,128)(2,1)S(1)} %get-tuple-element.34), channel_id=1, source_target_pairs={{0,4},{1,5},{2,6},{3,7},{4,0},{5,1},{6,2},{7,3},{8,12},{9,13},{10,... | collective-permute-start | bytes 393224 | tf_op jit(solution)/shard_map/ppermute | solution.py:33
  56.0 11.3 %collective-permute-start.6 = (bf16[8,1,8,1024]{3,2,1,0:T(8,128)(2,1)S(1)}, bf16[8,1,8,1024]{3,2,1,0:T(8,128)(2,1)S(1)}, u32[]{:S(2)}, u32[]{:S(2)}) collective-permute-start(bf16[8,1,8,1024]{3,2,1,0:T(8,128)(2,1)S(1)} %get-tuple-element.33), channel_id=1, source_target_pairs={{0,5},{1,6},{2,7},{3,0},{4,1},{5,2},{6,3},{7,4},{8,13},{9,14},{10,... | collective-permute-start | bytes 393224 | tf_op jit(solution)/shard_map/ppermute | solution.py:33
  58.0 9.4 %collective-permute-start.7 = (bf16[8,1,8,1024]{3,2,1,0:T(8,128)(2,1)S(1)}, bf16[8,1,8,1024]{3,2,1,0:T(8,128)(2,1)S(1)}, u32[]{:S(2)}, u32[]{:S(2)}) collective-permute-start(bf16[8,1,8,1024]{3,2,1,0:T(8,128)(2,1)S(1)} %get-tuple-element.32), channel_id=1, source_target_pairs={{0,6},{1,7},{2,0},{3,1},{4,2},{5,3},{6,4},{7,5},{8,14},{9,15},{10,... | collective-permute-start | bytes 393224 | tf_op jit(solution)/shard_map/ppermute | solution.py:33
  60.1 7.9 %collective-permute-start.8 = (bf16[8,1,8,1024]{3,2,1,0:T(8,128)(2,1)S(1)}, bf16[8,1,8,1024]{3,2,1,0:T(8,128)(2,1)S(1)}, u32[]{:S(2)}, u32[]{:S(2)}) collective-permute-start(bf16[8,1,8,1024]{3,2,1,0:T(8,128)(2,1)S(1)} %get-tuple-element.31), channel_id=1, source_target_pairs={{0,7},{1,0},{2,1},{3,2},{4,3},{5,4},{6,5},{7,6},{8,15},{9,8},{10,9... | collective-permute-start | bytes 393224 | tf_op jit(solution)/shard_map/ppermute | solution.py:33
  68.7 13.6 %collective-permute-start.9 = (bf16[1,8,8,1024]{3,2,1,0:T(8,128)(2,1)S(1)}, bf16[1,8,8,1024]{3,2,1,0:T(8,128)(2,1)S(1)}, u32[]{:S(2)}, u32[]{:S(2)}) collective-permute-start(bf16[1,8,8,1024]{3,2,1,0:T(8,128)(2,1)S(1)} %get-tuple-element.29), channel_id=1, source_target_pairs={{0,32},{32,64},{64,96},{96,128},{128,160},{160,192},{192,224},{224... | collective-permute-start | bytes 393224 | tf_op jit(solution)/shard_map/ppermute | solution.py:33
  70.7 15.2 %collective-permute-start.10 = (bf16[1,8,8,1024]{3,2,1,0:T(8,128)(2,1)S(1)}, bf16[1,8,8,1024]{3,2,1,0:T(8,128)(2,1)S(1)}, u32[]{:S(2)}, u32[]{:S(2)}) collective-permute-start(bf16[1,8,8,1024]{3,2,1,0:T(8,128)(2,1)S(1)} %get-tuple-element.28), channel_id=1, source_target_pairs={{0,64},{32,96},{64,128},{96,160},{128,192},{160,224},{192,0},{224,... | collective-permute-start | bytes 393224 | tf_op jit(solution)/shard_map/ppermute | solution.py:33
  73.7 21.5 %collective-permute-start.11 = (bf16[1,8,8,1024]{3,2,1,0:T(8,128)(2,1)S(1)}, bf16[1,8,8,1024]{3,2,1,0:T(8,128)(2,1)S(1)}, u32[]{:S(2)}, u32[]{:S(2)}) collective-permute-start(bf16[1,8,8,1024]{3,2,1,0:T(8,128)(2,1)S(1)} %get-tuple-element.27), channel_id=1, source_target_pairs={{0,96},{32,128},{64,160},{96,192},{128,224},{160,0},{192,32},{224,... | collective-permute-start | bytes 393224 | tf_op jit(solution)/shard_map/ppermute | solution.py:33
  77.4 18.4 %collective-permute-start.12 = (bf16[1,8,8,1024]{3,2,1,0:T(8,128)(2,1)S(1)}, bf16[1,8,8,1024]{3,2,1,0:T(8,128)(2,1)S(1)}, u32[]{:S(2)}, u32[]{:S(2)}) collective-permute-start(bf16[1,8,8,1024]{3,2,1,0:T(8,128)(2,1)S(1)} %get-tuple-element.26), channel_id=1, source_target_pairs={{0,128},{32,160},{64,192},{96,224},{128,0},{160,32},{192,64},{224,... | collective-permute-start | bytes 393224 | tf_op jit(solution)/shard_map/ppermute | solution.py:33
  77.9 18.6 %collective-permute-start.13 = (bf16[1,8,8,1024]{3,2,1,0:T(8,128)(2,1)S(1)}, bf16[1,8,8,1024]{3,2,1,0:T(8,128)(2,1)S(1)}, u32[]{:S(2)}, u32[]{:S(2)}) collective-permute-start(bf16[1,8,8,1024]{3,2,1,0:T(8,128)(2,1)S(1)} %get-tuple-element.25), channel_id=1, source_target_pairs={{0,160},{32,192},{64,224},{96,0},{128,32},{160,64},{192,96},{224,1... | collective-permute-start | bytes 393224 | tf_op jit(solution)/shard_map/ppermute | solution.py:33
  82.3 21.1 %collective-permute-start.14 = (bf16[1,8,8,1024]{3,2,1,0:T(8,128)(2,1)S(1)}, bf16[1,8,8,1024]{3,2,1,0:T(8,128)(2,1)S(1)}, u32[]{:S(2)}, u32[]{:S(2)}) collective-permute-start(bf16[1,8,8,1024]{3,2,1,0:T(8,128)(2,1)S(1)} %get-tuple-element.24), channel_id=1, source_target_pairs={{0,192},{32,224},{64,0},{96,32},{128,64},{160,96},{192,128},{224,1... | collective-permute-start | bytes 393224 | tf_op jit(solution)/shard_map/ppermute | solution.py:33
  85.9 18.2 %collective-permute-start.15 = (bf16[1,8,8,1024]{3,2,1,0:T(8,128)(2,1)S(1)}, bf16[1,8,8,1024]{3,2,1,0:T(8,128)(2,1)S(1)}, u32[]{:S(2)}, u32[]{:S(2)}) collective-permute-start(bf16[1,8,8,1024]{3,2,1,0:T(8,128)(2,1)S(1)} %get-tuple-element.23), channel_id=1, source_target_pairs={{0,224},{32,0},{64,32},{96,64},{128,96},{160,128},{192,160},{224,1... | collective-permute-start | bytes 393224 | tf_op jit(solution)/shard_map/ppermute | solution.py:33
  168.9 53.1 %all-to-all-start = ((bf16[4,8,8,8,1024]{4,3,2,1,0:T(8,128)(2,1)}), bf16[4,8,8,8,1024]{4,3,2,1,0:T(8,128)(2,1)}, u32[]{:S(2)}, u32[]{:S(2)}) async-start(bf16[4,8,8,8,1024]{4,3,2,1,0:T(8,128)(2,1)} %bitcast.104), calls=%async_computation | async-start | bytes 8388608 | tf_op jit(solution)/shard_map/all_to_all | solution.py:126
  174.0 58.8 %copy-start.7 = (bf16[1024,64]{0,1:T(8,128)(2,1)S(1)}, bf16[1024,64]{0,1:T(8,128)(2,1)}, u32[]{:S(2)}) copy-start(bf16[1024,64]{0,1:T(8,128)(2,1)} %param.19) | copy-start | bytes 393220
  227.8 10.0 %collective-permute-start.16 = (bf16[1,8,8,1024]{3,2,1,0:T(8,128)(2,1)S(1)}, bf16[1,8,8,1024]{3,2,1,0:T(8,128)(2,1)S(1)}, u32[]{:S(2)}, u32[]{:S(2)}) collective-permute-start(bf16[1,8,8,1024]{3,2,1,0:T(8,128)(2,1)S(1)} %get-tuple-element.21), channel_id=1, source_target_pairs={{0,224},{32,0},{64,32},{96,64},{128,96},{160,128},{192,160},{224,1... | collective-permute-start | bytes 393224 | tf_op jit(solution)/shard_map/ppermute | solution.py:33
  230.9 10.0 %collective-permute-start.17 = (bf16[1,8,8,1024]{3,2,1,0:T(8,128)(2,1)S(1)}, bf16[1,8,8,1024]{3,2,1,0:T(8,128)(2,1)S(1)}, u32[]{:S(2)}, u32[]{:S(2)}) collective-permute-start(bf16[1,8,8,1024]{3,2,1,0:T(8,128)(2,1)S(1)} %get-tuple-element.20), channel_id=1, source_target_pairs={{0,192},{32,224},{64,0},{96,32},{128,64},{160,96},{192,128},{224,1... | collective-permute-start | bytes 393224 | tf_op jit(solution)/shard_map/ppermute | solution.py:33
  233.2 11.7 %collective-permute-start.18 = (bf16[1,8,8,1024]{3,2,1,0:T(8,128)(2,1)S(1)}, bf16[1,8,8,1024]{3,2,1,0:T(8,128)(2,1)S(1)}, u32[]{:S(2)}, u32[]{:S(2)}) collective-permute-start(bf16[1,8,8,1024]{3,2,1,0:T(8,128)(2,1)S(1)} %get-tuple-element.19), channel_id=1, source_target_pairs={{0,160},{32,192},{64,224},{96,0},{128,32},{160,64},{192,96},{224,1... | collective-permute-start | bytes 393224 | tf_op jit(solution)/shard_map/ppermute | solution.py:33
  234.2 10.8 %collective-permute-start.19 = (bf16[1,8,8,1024]{3,2,1,0:T(8,128)(2,1)S(1)}, bf16[1,8,8,1024]{3,2,1,0:T(8,128)(2,1)S(1)}, u32[]{:S(2)}, u32[]{:S(2)}) collective-permute-start(bf16[1,8,8,1024]{3,2,1,0:T(8,128)(2,1)S(1)} %get-tuple-element.18), channel_id=1, source_target_pairs={{0,128},{32,160},{64,192},{96,224},{128,0},{160,32},{192,64},{224,... | collective-permute-start | bytes 393224 | tf_op jit(solution)/shard_map/ppermute | solution.py:33
  237.9 13.4 %collective-permute-start.20 = (bf16[1,8,8,1024]{3,2,1,0:T(8,128)(2,1)S(1)}, bf16[1,8,8,1024]{3,2,1,0:T(8,128)(2,1)S(1)}, u32[]{:S(2)}, u32[]{:S(2)}) collective-permute-start(bf16[1,8,8,1024]{3,2,1,0:T(8,128)(2,1)S(1)} %get-tuple-element.17), channel_id=1, source_target_pairs={{0,96},{32,128},{64,160},{96,192},{128,224},{160,0},{192,32},{224,... | collective-permute-start | bytes 393224 | tf_op jit(solution)/shard_map/ppermute | solution.py:33
  237.9 19.1 %collective-permute-start.21 = (bf16[1,8,8,1024]{3,2,1,0:T(8,128)(2,1)S(1)}, bf16[1,8,8,1024]{3,2,1,0:T(8,128)(2,1)S(1)}, u32[]{:S(2)}, u32[]{:S(2)}) collective-permute-start(bf16[1,8,8,1024]{3,2,1,0:T(8,128)(2,1)S(1)} %get-tuple-element.16), channel_id=1, source_target_pairs={{0,64},{32,96},{64,128},{96,160},{128,192},{160,224},{192,0},{224,... | collective-permute-start | bytes 393224 | tf_op jit(solution)/shard_map/ppermute | solution.py:33
  240.9 20.4 %collective-permute-start.22 = (bf16[1,8,8,1024]{3,2,1,0:T(8,128)(2,1)S(1)}, bf16[1,8,8,1024]{3,2,1,0:T(8,128)(2,1)S(1)}, u32[]{:S(2)}, u32[]{:S(2)}) collective-permute-start(bf16[1,8,8,1024]{3,2,1,0:T(8,128)(2,1)S(1)} %get-tuple-element.15), channel_id=1, source_target_pairs={{0,32},{32,64},{64,96},{96,128},{128,160},{160,192},{192,224},{224... | collective-permute-start | bytes 393224 | tf_op jit(solution)/shard_map/ppermute | solution.py:33
  261.4 8.3 %collective-permute-start.23 = (bf16[8,1,8,1024]{3,2,1,0:T(8,128)(2,1)S(1)}, bf16[8,1,8,1024]{3,2,1,0:T(8,128)(2,1)S(1)}, u32[]{:S(2)}, u32[]{:S(2)}) collective-permute-start(bf16[8,1,8,1024]{3,2,1,0:T(8,128)(2,1)S(1)} %get-tuple-element.13), channel_id=1, source_target_pairs={{0,7},{1,0},{2,1},{3,2},{4,3},{5,4},{6,5},{7,6},{8,15},{9,8},{10,9... | collective-permute-start | bytes 393224 | tf_op jit(solution)/shard_map/ppermute | solution.py:33
  263.2 7.1 %collective-permute-start.24 = (bf16[8,1,8,1024]{3,2,1,0:T(8,128)(2,1)S(1)}, bf16[8,1,8,1024]{3,2,1,0:T(8,128)(2,1)S(1)}, u32[]{:S(2)}, u32[]{:S(2)}) collective-permute-start(bf16[8,1,8,1024]{3,2,1,0:T(8,128)(2,1)S(1)} %get-tuple-element.12), channel_id=1, source_target_pairs={{0,6},{1,7},{2,0},{3,1},{4,2},{5,3},{6,4},{7,5},{8,14},{9,15},{10,... | collective-permute-start | bytes 393224 | tf_op jit(solution)/shard_map/ppermute | solution.py:33
  265.6 7.2 %collective-permute-start.25 = (bf16[8,1,8,1024]{3,2,1,0:T(8,128)(2,1)S(1)}, bf16[8,1,8,1024]{3,2,1,0:T(8,128)(2,1)S(1)}, u32[]{:S(2)}, u32[]{:S(2)}) collective-permute-start(bf16[8,1,8,1024]{3,2,1,0:T(8,128)(2,1)S(1)} %get-tuple-element.11), channel_id=1, source_target_pairs={{0,5},{1,6},{2,7},{3,0},{4,1},{5,2},{6,3},{7,4},{8,13},{9,14},{10,... | collective-permute-start | bytes 393224 | tf_op jit(solution)/shard_map/ppermute | solution.py:33
  266.4 7.0 %collective-permute-start.26 = (bf16[8,1,8,1024]{3,2,1,0:T(8,128)(2,1)S(1)}, bf16[8,1,8,1024]{3,2,1,0:T(8,128)(2,1)S(1)}, u32[]{:S(2)}, u32[]{:S(2)}) collective-permute-start(bf16[8,1,8,1024]{3,2,1,0:T(8,128)(2,1)S(1)} %get-tuple-element.10), channel_id=1, source_target_pairs={{0,4},{1,5},{2,6},{3,7},{4,0},{5,1},{6,2},{7,3},{8,12},{9,13},{10,... | collective-permute-start | bytes 393224 | tf_op jit(solution)/shard_map/ppermute | solution.py:33
  267.7 10.8 %collective-permute-start.27 = (bf16[8,1,8,1024]{3,2,1,0:T(8,128)(2,1)S(1)}, bf16[8,1,8,1024]{3,2,1,0:T(8,128)(2,1)S(1)}, u32[]{:S(2)}, u32[]{:S(2)}) collective-permute-start(bf16[8,1,8,1024]{3,2,1,0:T(8,128)(2,1)S(1)} %get-tuple-element.9), channel_id=1, source_target_pairs={{0,3},{1,4},{2,5},{3,6},{4,7},{5,0},{6,1},{7,2},{8,11},{9,12},{10,... | collective-permute-start | bytes 393224 | tf_op jit(solution)/shard_map/ppermute | solution.py:33
  269.7 9.2 %collective-permute-start.28 = (bf16[8,1,8,1024]{3,2,1,0:T(8,128)(2,1)S(1)}, bf16[8,1,8,1024]{3,2,1,0:T(8,128)(2,1)S(1)}, u32[]{:S(2)}, u32[]{:S(2)}) collective-permute-start(bf16[8,1,8,1024]{3,2,1,0:T(8,128)(2,1)S(1)} %get-tuple-element.8), channel_id=1, source_target_pairs={{0,2},{1,3},{2,4},{3,5},{4,6},{5,7},{6,0},{7,1},{8,10},{9,11},{10,... | collective-permute-start | bytes 393224 | tf_op jit(solution)/shard_map/ppermute | solution.py:33
  270.3 8.6 %collective-permute-start.29 = (bf16[8,1,8,1024]{3,2,1,0:T(8,128)(2,1)S(1)}, bf16[8,1,8,1024]{3,2,1,0:T(8,128)(2,1)S(1)}, u32[]{:S(2)}, u32[]{:S(2)}) collective-permute-start(bf16[8,1,8,1024]{3,2,1,0:T(8,128)(2,1)S(1)} %get-tuple-element.7), channel_id=1, source_target_pairs={{0,1},{1,2},{2,3},{3,4},{4,5},{5,6},{6,7},{7,0},{8,9},{9,10},{10,1... | collective-permute-start | bytes 393224 | tf_op jit(solution)/shard_map/ppermute | solution.py:33
Sparse Core Ops, SparseCore 0:
  104.9 50.9 all-gather.2

commit v3 on v1

--- a/solution.py
+++ b/solution.py
@@ -98,23 +98,21 @@
     gate_value = jax.nn.sigmoid(jnp.sum(logits * onehot.astype(jnp.float32), axis=1))
     owner_group = route_ids // per_owner
     member = route_ids % per_owner
-    slot_index = (member * owners + owner_group) * capacity + rank_in
+    slot_index = (owner_group * per_owner + member) * capacity + rank_in
     send_buffer = (
         jnp.zeros((per_owner * owners * capacity, model_width), jnp.bfloat16)
         .at[slot_index]
         .set(moe_in)
     )
-    send_buffer = send_buffer.reshape(per_owner, owners, capacity, model_width)
+    send_buffer = send_buffer.reshape(owners * per_owner, capacity, model_width)
     w_in = expert_in[0, 0]
     w_out = expert_out[0, 0]
-    by_group = lax.all_to_all(send_buffer, "expert", split_axis=1, concat_axis=1, tiled=True)
-    by_member = lax.all_to_all(by_group, "z", split_axis=0, concat_axis=0, tiled=True)
+    by_member = lax.all_to_all(send_buffer, ("expert", "z"), split_axis=0, concat_axis=0, tiled=True)
     gathered = lax.all_gather(by_member, "y", axis=0, tiled=False)
     partial_out = expert_pass(gathered, w_in, w_out)
     returned = lax.all_to_all(partial_out, "y", split_axis=0, concat_axis=0, tiled=False)
     summed = jnp.sum(returned.astype(jnp.float32), axis=0).astype(jnp.bfloat16)
-    results = lax.all_to_all(summed, "z", split_axis=0, concat_axis=0, tiled=True)
-    results = lax.all_to_all(results, "expert", split_axis=1, concat_axis=1, tiled=True)
+    results = lax.all_to_all(summed, ("expert", "z"), split_axis=0, concat_axis=0, tiled=True)
     frame_moe = results.reshape(-1, model_width)[slot_index]
     layer_out = mixed_res.astype(jnp.float32) + gate_value[:, None] * frame_moe.astype(jnp.float32)
     return layer_out.astype(jnp.bfloat16)[None]

time: 297 us -> 264 us (0.89)
  blocking collectives: 144 us -> 96.9 us
  waiting for transfers between devices: 64.6 us -> 77.4 us
  local copies, waits for them, and re-layouts: 7.01 us -> 3.18 us
  starting transfers between devices: 13.4 us -> 17.1 us
    all_to_all x3 -> x1, blocking collectives: 90.3 us -> 43.3 us  [shards(): lax.all_to_all(send_buffer, ('expert', 'z'), split_axis=0, concat_axis=0,...]
    all_to_all x1, waiting for transfers between devices: 14.8 us -> 26.6 us  [shards(): lax.all_to_all(summed, ('expert', 'z'), split_axis=0, concat_axis=0, tile...]
    all_to_all x1, starting transfers between devices: 8.11 us -> 11.8 us  [shards(): lax.all_to_all(summed, ('expert', 'z'), split_axis=0, concat_axis=0, tile...]
where the time goes in v3:
time: 264 us; the launch traced here: 263 us
  blocking collectives  96.9 us (37%)
  waiting for transfers between devices  77.4 us (29%)
  matrix products  41 us (16%)
  starting transfers between devices  17.1 us (6%)
  other arithmetic  13.8 us (5%)
  between operations  13.7 us (5%)
  local copies, waits for them, and re-layouts  3.18 us (1%)
    all_to_all x1, blocking collectives, shards(): lax.all_to_all(partial_out, 'y', split_axis=0, concat_axis=0, tiled=False)  53.6 us
    all_gather x1, waiting for transfers between devices, shards(): gathered = lax.all_gather(by_member, 'y', axis=0, tiled=False)  48.9 us
    all_to_all x1, blocking collectives, shards(): lax.all_to_all(send_buffer, ('expert', 'z'), split_axis=0, concat_axis=0,...  43.3 us
    all_to_all x1, waiting for transfers between devices, shards(): lax.all_to_all(summed, ('expert', 'z'), split_axis=0, concat_axis=0, tile...  26.6 us
    dot_general x1, matrix products, shards(): jnp.dot(activated, point_out, preferred_element_type=jnp.float32)  22.8 us
    dot_general x1, matrix products, expert_pass(): jnp.dot(hidden, w_out, preferred_element_type=jnp.float32)  13 us
    all_to_all x1, starting transfers between devices, shards(): lax.all_to_all(summed, ('expert', 'z'), split_axis=0, concat_axis=0, tile...  11.8 us
  transfers between devices with their start and end apart: 4, of which 3 were waited for; matrix products, arithmetic and copies ran while one was open for 1% of the time, Pallas kernels for 0%

profile of v3, /device:TPU:1, one launch (start us, length us, event | category | flops | bytes accessed | tf_op | source)
XLA Modules:
  0.0 263.0 jit_solution(13125398151709000320)
XLA Ops:
  6.5 0.0 copy-start
  6.5 0.0 all-gather.3.cloned.1.call-start
  6.5 1.3 convert_reduce_fusion.1
  7.9 1.3 fusion.20
  9.2 0.0 copy-start.4
  9.2 0.0 copy-start.6
  9.2 0.0 copy-start.5
  9.3 0.0 copy-start.2
  9.3 0.0 copy-start.8
  9.3 0.0 copy-start.9
  9.3 3.8 %fusion.29 = f32[256,2048]{1,0:T(8,128)S(1)} fusion(bf16[1024,2048]{1,0:T(8,128)(2,1)} %param.14, bf16[1,256,1024]{2,1,0:T(8,128)(2,1)} %param.11, f32[256]{0:T(256)S(1)} %add_rsqrt_fusion.1, f32[256]{0:T(256)S(1)} %broadcast_multiply_fusion.1), kind=kOutput, calls=%fused_computation.64 | convolution fusion | flops 1074790400 | bytes 6817792 | tf_op jit(solution)/shard_map/dot_general | solution.py:60
  13.1 0.3 fusion.27
  13.4 0.0 copy-start.3
  13.4 0.8 copy-done.3
  14.2 4.0 %collective-permute-start = (bf16[15,1024]{1,0:T(8,128)(2,1)S(1)}, bf16[15,1024]{1,0:T(8,128)(2,1)S(1)}, u32[]{:S(2)}, u32[]{:S(2)}) collective-permute-start(bf16[15,1024]{1,0:T(8,128)(2,1)S(1)} %get-tuple-element.7), channel_id=1, source_target_pairs={{0,8},{8,16},{16,24},{24,32},{32,40},{40,48},{48,56},{56,64},{64,7... | collective-permute-start | bytes 92168 | tf_op jit(solution)/shard_map/ppermute | solution.py:17
  18.2 1.3 collective-permute-start.1
  19.5 0.0 copy-done.4
  19.5 0.1 fusion.74
  19.6 0.0 copy-done.6
  19.7 0.1 copy.18
  19.7 0.1 reduce-window.10
  19.8 0.1 reduce.2
  19.9 0.0 copy-done.5
  20.0 0.6 reduce-window.11
  20.6 0.2 slice_reduce_fusion
  20.8 0.1 select_reduce_fusion.1
  20.9 0.1 fusion.64
  21.1 0.0 collective-permute-done
  21.1 1.8 collective-permute-done.1
  22.9 0.0 copy-done.2
  22.9 0.0 copy-done.8
  22.9 0.0 copy-done.9
  22.9 22.8 %convert_reduce_fusion = (f32[256]{0:T(256)S(1)}, bf16[256,1024]{1,0:T(8,128)(2,1)S(1)}) fusion(bf16[1024,1024]{1,0:T(8,128)(2,1)} %param.18, bf16[256,1024]{1,0:T(8,128)(2,1)} %copy-done.3, bf16[15,1024]{1,0:T(8,128)(2,1)S(1)} %collective-permute-done.1, bf16[15,1024]{1,0:T(8,128)(2,1)S(1)} %collective-permute-done, f32[1024]{0:T(1024)S(1)} %copy-done.8, ...), kind=kOutput, calls=%fused_computation.39 | convolution fusion | flops 595853056 | bytes 3899392 | tf_op jit(solution)/shard_map/dot_general | solution.py:85
  45.7 0.0 copy-start.1
  45.7 0.3 fusion.18
  46.0 2.8 %scatter_custom_fusion = bf16[512,1024]{1,0:T(8,128)(2,1)} fusion(s32[256]{0:T(256)S(1)} %bitcast.143, bf16[]{:T(256)} %constant.125.clone.1, bf16[256,1024]{1,0:T(8,128)(2,1)S(1)} %get-tuple-element.72, f32[256]{0:T(256)S(1)} %add_rsqrt_fusion, f32[256]{0:T(256)S(1)} %broadcast_multiply_fusion), kind=kCustom, calls=%fused_computation.112 | custom fusion | flops 1048576 | bytes 1574914 | tf_op jit(solution)/shard_map/scatter | solution.py:105
  48.8 43.3 %all_to_all.15 = bf16[64,8,1024]{2,1,0:T(8,128)(2,1)} all-to-all(bf16[64,8,1024]{2,1,0:T(8,128)(2,1)} %bitcast.107), channel_id=1, replica_groups=mesh['z'=8,'y'=4,'expert'=8] {'expert','z'}, dimensions={0} | all-to-all | bytes 2097152 | tf_op jit(solution)/shard_map/all_to_all | solution.py:110
  92.1 0.0 all-gather.3.cloned.1.call-update
  92.1 48.9 %all-gather.3.cloned.1.call-done = bf16[256,8,1024]{2,1,0:T(8,128)(2,1)} async-done(((bf16[64,8,1024]{2,1,0:T(8,128)(2,1)}), bf16[256,8,1024]{2,1,0:T(8,128)(2,1)}) %all-gather.3.cloned.1.call-update) | async-done | bytes 4194320 | tf_op jit(solution)/shard_map/all_gather | solution.py:111
  141.0 0.0 copy-done
  141.0 13.0 %fusion.3 = bf16[2048,1024]{1,0:T(8,128)(2,1)} fusion(bf16[256,8,1024]{2,1,0:T(8,128)(2,1)} %all-gather.3.cloned.1.call-done, bf16[1,1,1024,1024]{3,2,1,0:T(8,128)(2,1)S(1)} %copy-done, bf16[1,1,1024,1024]{3,2,1,0:T(8,128)(2,1)} %param.20), kind=kOutput, calls=%fused_computation.6 | convolution fusion | flops 8602517504 | bytes 12582912 | tf_op jit(solution)/shard_map/dot_general | solution.py:38
  154.1 0.0 copy-done.1
  154.1 53.6 %all_to_all.16 = bf16[4,64,8,1024]{3,2,1,0:T(8,128)(2,1)} all-to-all(bf16[4,64,8,1024]{3,2,1,0:T(8,128)(2,1)} %bitcast.106), channel_id=1, replica_groups=mesh['z'=8,'y'=4,'expert'=8] {'y'}, dimensions={0} | all-to-all | bytes 8388608 | tf_op jit(solution)/shard_map/all_to_all | solution.py:113
  207.7 0.0 copy-start.7
  207.7 4.4 %reduce_sum.95 = bf16[64,8,1024]{2,1,0:T(8,128)(2,1)} reduce(bf16[4,64,8,1024]{3,2,1,0:T(8,128)(2,1)} %all_to_all.16, bf16[]{:T(256)} %constant.125.clone.1), dimensions={0}, to_apply=%region_12.13 | reduce | flops 1572864 | bytes 5242882 | tf_op jit(solution)/shard_map/reduce_sum | solution.py:114
  212.1 11.8 %all-to-all-start.2 = ((bf16[64,8,1024]{2,1,0:T(8,128)(2,1)}), bf16[64,8,1024]{2,1,0:T(8,128)(2,1)S(1)}, u32[]{:S(2)}, u32[]{:S(2)}) async-start(bf16[64,8,1024]{2,1,0:T(8,128)(2,1)} %reduce_sum.95), calls=%async_computation.2 | async-start | bytes 2097152 | tf_op jit(solution)/shard_map/all_to_all | solution.py:115
  223.9 0.0 copy-done.7
  224.0 1.4 fusion.17
  225.4 26.6 %all-to-all-done.2 = bf16[64,8,1024]{2,1,0:T(8,128)(2,1)S(1)} async-done(((bf16[64,8,1024]{2,1,0:T(8,128)(2,1)}), bf16[64,8,1024]{2,1,0:T(8,128)(2,1)S(1)}, u32[]{:S(2)}, u32[]{:S(2)}) %all-to-all-start.2) | async-done | bytes 1048608 | tf_op jit(solution)/shard_map/all_to_all | solution.py:115
  252.0 2.0 gather_fusion
  254.0 2.2 fusion.28
  (15 shorter events, 0.2 us)
Async XLA Ops:
  6.5 134.5 %copy-start = (bf16[1,1,1024,1024]{3,2,1,0:T(8,128)(2,1)S(1)}, bf16[1,1,1024,1024]{3,2,1,0:T(8,128)(2,1)}, u32[]{:S(2)}) copy-start(bf16[1,1,1024,1024]{3,2,1,0:T(8,128)(2,1)} %param.21) | copy-start | bytes 6291460
  6.5 134.5 %all-gather.3.cloned.1.call-start = ((), (), s32[]{:S(2)}) async-start(), calls=%async_computation.3 | async-start | bytes 5242880 | tf_op jit(solution)/shard_map/all_gather | solution.py:111
  9.2 10.3 %copy-start.4 = (f32[31,1024]{1,0:T(8,128)S(1)}, f32[31,1024]{1,0:T(8,128)}, u32[]{:S(2)}) copy-start(f32[31,1024]{1,0:T(8,128)} %param.15) | copy-start | bytes 380932
  9.2 10.4 %copy-start.6 = (s32[1,32]{1,0:T(1,128)S(1)}, s32[1,32]{1,0:T(1,128)}, u32[]{:S(2)}) copy-start(s32[1,32]{1,0:T(1,128)} %param.12) | copy-start | bytes 388
  9.2 10.7 %copy-start.5 = (s32[1,256,1]{1,2,0:T(1,128)S(1)}, s32[1,256,1]{1,2,0:T(1,128)}, u32[]{:S(2)}) copy-start(s32[1,256,1]{1,2,0:T(1,128)} %param.13) | copy-start | bytes 3076
  9.3 13.6 %copy-start.2 = (bf16[1,256,1024]{2,1,0:T(8,128)(2,1)S(1)}, bf16[1,256,1024]{2,1,0:T(8,128)(2,1)}, u32[]{:S(2)}) copy-start(bf16[1,256,1024]{2,1,0:T(8,128)(2,1)} %param.11) | copy-start | bytes 1572868
  9.3 13.6 %copy-start.8 = (f32[1024]{0:T(1024)S(1)}, f32[1024]{0:T(1024)}, u32[]{:S(2)}) copy-start(f32[1024]{0:T(1024)} %param.17) | copy-start | bytes 12292
  9.3 13.6 %copy-start.9 = (f32[1024]{0:T(1024)S(1)}, f32[1024]{0:T(1024)}, u32[]{:S(2)}) copy-start(f32[1024]{0:T(1024)} %param.16) | copy-start | bytes 12292
  13.4 0.8 copy-start.3
  14.2 6.9 %collective-permute-start = (bf16[15,1024]{1,0:T(8,128)(2,1)S(1)}, bf16[15,1024]{1,0:T(8,128)(2,1)S(1)}, u32[]{:S(2)}, u32[]{:S(2)}) collective-permute-start(bf16[15,1024]{1,0:T(8,128)(2,1)S(1)} %get-tuple-element.7), channel_id=1, source_target_pairs={{0,8},{8,16},{16,24},{24,32},{32,40},{40,48},{48,56},{56,64},{64,7... | collective-permute-start | bytes 92168 | tf_op jit(solution)/shard_map/ppermute | solution.py:17
  18.2 4.7 %collective-permute-start.1 = (bf16[15,1024]{1,0:T(8,128)(2,1)S(1)}, bf16[15,1024]{1,0:T(8,128)(2,1)S(1)}, u32[]{:S(2)}, u32[]{:S(2)}) collective-permute-start(bf16[15,1024]{1,0:T(8,128)(2,1)S(1)} %get-tuple-element.8), channel_id=1, source_target_pairs={{8,0},{16,8},{24,16},{32,24},{40,32},{48,40},{56,48},{64,56},{72,6... | collective-permute-start | bytes 92168 | tf_op jit(solution)/shard_map/ppermute | solution.py:19
  45.7 108.4 %copy-start.1 = (bf16[256,1024]{1,0:T(8,128)(2,1)}, bf16[256,1024]{1,0:T(8,128)(2,1)S(1)}, u32[]{:S(2)}) copy-start(bf16[256,1024]{1,0:T(8,128)(2,1)S(1)} %get-tuple-element.72) | copy-start | bytes 1572868
  207.7 16.2 %copy-start.7 = (bf16[1024,64]{0,1:T(8,128)(2,1)S(1)}, bf16[1024,64]{0,1:T(8,128)(2,1)}, u32[]{:S(2)}) copy-start(bf16[1024,64]{0,1:T(8,128)(2,1)} %param.19) | copy-start | bytes 393220
  212.1 39.9 %all-to-all-start.2 = ((bf16[64,8,1024]{2,1,0:T(8,128)(2,1)}), bf16[64,8,1024]{2,1,0:T(8,128)(2,1)S(1)}, u32[]{:S(2)}, u32[]{:S(2)}) async-start(bf16[64,8,1024]{2,1,0:T(8,128)(2,1)} %reduce_sum.95), calls=%async_computation.2 | async-start | bytes 2097152 | tf_op jit(solution)/shard_map/all_to_all | solution.py:115
Sparse Core Ops, SparseCore 0:
  92.2 48.7 all-gather.2

commit v4 on v3

--- a/solution.py
+++ b/solution.py
@@ -110,8 +110,7 @@
     by_member = lax.all_to_all(send_buffer, ("expert", "z"), split_axis=0, concat_axis=0, tiled=True)
     gathered = lax.all_gather(by_member, "y", axis=0, tiled=False)
     partial_out = expert_pass(gathered, w_in, w_out)
-    returned = lax.all_to_all(partial_out, "y", split_axis=0, concat_axis=0, tiled=False)
-    summed = jnp.sum(returned.astype(jnp.float32), axis=0).astype(jnp.bfloat16)
+    summed = lax.psum_scatter(partial_out, "y", scatter_dimension=0, tiled=False)
     results = lax.all_to_all(summed, ("expert", "z"), split_axis=0, concat_axis=0, tiled=True)
     frame_moe = results.reshape(-1, model_width)[slot_index]
     layer_out = mixed_res.astype(jnp.float32) + gate_value[:, None] * frame_moe.astype(jnp.float32)

time: 264 us -> 253 us (0.958)
  blocking collectives: 96.9 us -> 43.3 us
  waiting for transfers between devices: 77.4 us -> 127 us
  other arithmetic: 13.8 us -> 9.41 us
    all_to_all x1 -> x0, blocking collectives: 53.6 us -> none  [shards(): lax.all_to_all(partial_out, 'y', split_axis=0, concat_axis=0, tiled=False)]
    reduce_scatter x0 -> x1, waiting for transfers between devices: none -> 49.9 us  [shards(): lax.psum_scatter(partial_out, 'y', scatter_dimension=0, tiled=False)]
    reduce_sum x1 -> x0, other arithmetic: 4.39 us -> none  [shards(): summed = jnp.sum(returned.astype(jnp.float32), axis=0).astype(jnp.bfloat16)]
  transfers between devices with their start and end apart: 4 -> 5, of which waited for: 3 -> 4; matrix products, arithmetic and copies ran while one was open for 1% -> 1% of each run, Pallas kernels for 0% -> 0%
where the time goes in v4:
time: 253 us
  waiting for transfers between devices  127 us (50%)
  blocking collectives  43.3 us (17%)
  matrix products  40.3 us (16%)
  starting transfers between devices  16.2 us (6%)
  between operations  13.7 us (5%)
  other arithmetic  9.41 us (4%)
  local copies, waits for them, and re-layouts  3.18 us (1%)
    reduce_scatter x1, waiting for transfers between devices, shards(): lax.psum_scatter(partial_out, 'y', scatter_dimension=0, tiled=False)  49.9 us
    all_gather x1, waiting for transfers between devices, shards(): gathered = lax.all_gather(by_member, 'y', axis=0, tiled=False)  48.7 us
    all_to_all x1, blocking collectives, shards(): lax.all_to_all(send_buffer, ('expert', 'z'), split_axis=0, concat_axis=0,...  43.3 us
    all_to_all x1, waiting for transfers between devices, shards(): lax.all_to_all(summed, ('expert', 'z'), split_axis=0, concat_axis=0, tile...  26.6 us
    dot_general x1, matrix products, shards(): jnp.dot(activated, point_out, preferred_element_type=jnp.float32)  22.1 us
    dot_general x1, matrix products, expert_pass(): jnp.dot(hidden, w_out, preferred_element_type=jnp.float32)  13 us
    all_to_all x1, starting transfers between devices, shards(): lax.all_to_all(summed, ('expert', 'z'), split_axis=0, concat_axis=0, tile...  10.6 us
  transfers between devices with their start and end apart: 5, of which 4 were waited for; matrix products, arithmetic and copies ran while one was open for 1% of the time, Pallas kernels for 0%

profile of v4, /device:TPU:1, one launch (start us, length us, event | category | flops | bytes accessed | tf_op | source)
XLA Modules:
  0.0 253.1 jit_solution(11349083587405739717)
XLA Ops:
  6.5 0.0 copy-start
  6.5 0.0 all-gather.3.cloned.1.call-start
  6.5 1.3 convert_reduce_fusion.1
  7.9 1.3 fusion.20
  9.2 0.0 copy-start.4
  9.2 0.0 copy-start.6
  9.2 0.0 copy-start.5
  9.3 0.0 copy-start.2
  9.3 0.0 copy-start.8
  9.3 0.0 copy-start.9
  9.3 3.8 %fusion.29 = f32[256,2048]{1,0:T(8,128)S(1)} fusion(bf16[1024,2048]{1,0:T(8,128)(2,1)} %param.14, bf16[1,256,1024]{2,1,0:T(8,128)(2,1)} %param.11, f32[256]{0:T(256)S(1)} %add_rsqrt_fusion.1, f32[256]{0:T(256)S(1)} %broadcast_multiply_fusion.1), kind=kOutput, calls=%fused_computation.64 | convolution fusion | flops 1074790400 | bytes 6817792 | tf_op jit(solution)/shard_map/dot_general | solution.py:60
  13.1 0.3 fusion.27
  13.4 0.0 copy-start.3
  13.4 0.8 copy-done.3
  14.2 4.0 %collective-permute-start = (bf16[15,1024]{1,0:T(8,128)(2,1)S(1)}, bf16[15,1024]{1,0:T(8,128)(2,1)S(1)}, u32[]{:S(2)}, u32[]{:S(2)}) collective-permute-start(bf16[15,1024]{1,0:T(8,128)(2,1)S(1)} %get-tuple-element.7), channel_id=1, source_target_pairs={{0,8},{8,16},{16,24},{24,32},{32,40},{40,48},{48,56},{56,64},{64,7... | collective-permute-start | bytes 92168 | tf_op jit(solution)/shard_map/ppermute | solution.py:17
  18.2 1.3 collective-permute-start.1
  19.5 0.0 copy-done.4
  19.5 0.1 fusion.74
  19.6 0.0 copy-done.6
  19.7 0.1 copy.18
  19.7 0.1 reduce-window.10
  19.8 0.1 reduce.1
  19.9 0.0 copy-done.5
  19.9 0.6 reduce-window.11
  20.6 0.2 slice_reduce_fusion
  20.8 0.1 select_reduce_fusion.1
  20.9 0.1 fusion.64
  21.1 0.0 collective-permute-done
  21.1 1.8 collective-permute-done.1
  22.9 0.0 copy-done.2
  22.9 0.0 copy-done.8
  22.9 0.0 copy-done.9
  22.9 22.1 %convert_reduce_fusion = (f32[256]{0:T(256)S(1)}, bf16[256,1024]{1,0:T(8,128)(2,1)S(1)}) fusion(bf16[1024,1024]{1,0:T(8,128)(2,1)} %param.18, bf16[256,1024]{1,0:T(8,128)(2,1)} %copy-done.3, bf16[15,1024]{1,0:T(8,128)(2,1)S(1)} %collective-permute-done.1, bf16[15,1024]{1,0:T(8,128)(2,1)S(1)} %collective-permute-done, f32[1024]{0:T(1024)S(1)} %copy-done.8, ...), kind=kOutput, calls=%fused_computation.39 | convolution fusion | flops 595853056 | bytes 3899392 | tf_op jit(solution)/shard_map/dot_general | solution.py:85
  45.0 0.0 copy-start.1
  45.0 0.3 fusion.18
  45.3 2.8 %scatter_custom_fusion = bf16[512,1024]{1,0:T(8,128)(2,1)} fusion(s32[256]{0:T(256)S(1)} %bitcast.145, bf16[]{:T(256)} %constant.124.clone.1, bf16[256,1024]{1,0:T(8,128)(2,1)S(1)} %get-tuple-element.72, f32[256]{0:T(256)S(1)} %add_rsqrt_fusion, f32[256]{0:T(256)S(1)} %broadcast_multiply_fusion), kind=kCustom, calls=%fused_computation.112 | custom fusion | flops 1048576 | bytes 1574914 | tf_op jit(solution)/shard_map/scatter | solution.py:105
  48.1 43.3 %all_to_all.10 = bf16[64,8,1024]{2,1,0:T(8,128)(2,1)} all-to-all(bf16[64,8,1024]{2,1,0:T(8,128)(2,1)} %bitcast.108), channel_id=1, replica_groups=mesh['z'=8,'y'=4,'expert'=8] {'expert','z'}, dimensions={0} | all-to-all | bytes 2097152 | tf_op jit(solution)/shard_map/all_to_all | solution.py:110
  91.4 0.0 all-gather.3.cloned.1.call-update
  91.4 0.2 reduce-scatter.2.cloned.1.call-start
  91.6 48.7 %all-gather.3.cloned.1.call-done = bf16[256,8,1024]{2,1,0:T(8,128)(2,1)} async-done(((bf16[64,8,1024]{2,1,0:T(8,128)(2,1)}), bf16[256,8,1024]{2,1,0:T(8,128)(2,1)}) %all-gather.3.cloned.1.call-update) | async-done | bytes 4194320 | tf_op jit(solution)/shard_map/all_gather | solution.py:111
  140.3 0.0 copy-done
  140.3 13.0 %fusion.3 = bf16[2048,1024]{1,0:T(8,128)(2,1)} fusion(bf16[256,8,1024]{2,1,0:T(8,128)(2,1)} %all-gather.3.cloned.1.call-done, bf16[1,1,1024,1024]{3,2,1,0:T(8,128)(2,1)S(1)} %copy-done, bf16[1,1,1024,1024]{3,2,1,0:T(8,128)(2,1)} %param.20), kind=kOutput, calls=%fused_computation.6 | convolution fusion | flops 8602517504 | bytes 12582912 | tf_op jit(solution)/shard_map/dot_general | solution.py:38
  153.4 0.0 copy-done.1
  153.4 0.0 copy-start.7
  153.4 0.0 reduce-scatter.2.cloned.1.call-update
  153.4 49.9 %reduce-scatter.2.cloned.1.call-done = bf16[1,64,8,1024]{3,2,1,0:T(8,128)(2,1)} async-done(((bf16[4,64,8,1024]{3,2,1,0:T(8,128)(2,1)}), bf16[1,64,8,1024]{3,2,1,0:T(8,128)(2,1)}) %reduce-scatter.2.cloned.1.call-update) | async-done | bytes 1048592 | tf_op jit(solution)/shard_map/reduce_scatter | solution.py:113
  203.4 10.6 %all-to-all-start.1 = ((bf16[64,8,1024]{2,1,0:T(8,128)(2,1)}), bf16[64,8,1024]{2,1,0:T(8,128)(2,1)S(1)}, u32[]{:S(2)}, u32[]{:S(2)}) async-start(bf16[64,8,1024]{2,1,0:T(8,128)(2,1)} %bitcast.109), calls=%async_computation.2 | async-start | bytes 2097152 | tf_op jit(solution)/shard_map/all_to_all | solution.py:114
  214.0 0.0 copy-done.7
  214.0 1.4 fusion.17
  215.4 26.6 %all-to-all-done.1 = bf16[64,8,1024]{2,1,0:T(8,128)(2,1)S(1)} async-done(((bf16[64,8,1024]{2,1,0:T(8,128)(2,1)}), bf16[64,8,1024]{2,1,0:T(8,128)(2,1)S(1)}, u32[]{:S(2)}, u32[]{:S(2)}) %all-to-all-start.1) | async-done | bytes 1048608 | tf_op jit(solution)/shard_map/all_to_all | solution.py:114
  242.0 2.0 gather_fusion
  244.0 2.2 fusion.28
  (15 shorter events, 0.2 us)
Async XLA Ops:
  6.5 133.8 %copy-start = (bf16[1,1,1024,1024]{3,2,1,0:T(8,128)(2,1)S(1)}, bf16[1,1,1024,1024]{3,2,1,0:T(8,128)(2,1)}, u32[]{:S(2)}) copy-start(bf16[1,1,1024,1024]{3,2,1,0:T(8,128)(2,1)} %param.21) | copy-start | bytes 6291460
  6.5 133.8 %all-gather.3.cloned.1.call-start = ((), (), s32[]{:S(2)}) async-start(), calls=%async_computation.4 | async-start | bytes 5242880 | tf_op jit(solution)/shard_map/all_gather | solution.py:111
  9.2 10.3 %copy-start.4 = (f32[31,1024]{1,0:T(8,128)S(1)}, f32[31,1024]{1,0:T(8,128)}, u32[]{:S(2)}) copy-start(f32[31,1024]{1,0:T(8,128)} %param.15) | copy-start | bytes 380932
  9.2 10.4 %copy-start.6 = (s32[1,32]{1,0:T(1,128)S(1)}, s32[1,32]{1,0:T(1,128)}, u32[]{:S(2)}) copy-start(s32[1,32]{1,0:T(1,128)} %param.12) | copy-start | bytes 388
  9.2 10.7 %copy-start.5 = (s32[1,256,1]{1,2,0:T(1,128)S(1)}, s32[1,256,1]{1,2,0:T(1,128)}, u32[]{:S(2)}) copy-start(s32[1,256,1]{1,2,0:T(1,128)} %param.13) | copy-start | bytes 3076
  9.3 13.6 %copy-start.2 = (bf16[1,256,1024]{2,1,0:T(8,128)(2,1)S(1)}, bf16[1,256,1024]{2,1,0:T(8,128)(2,1)}, u32[]{:S(2)}) copy-start(bf16[1,256,1024]{2,1,0:T(8,128)(2,1)} %param.11) | copy-start | bytes 1572868
  9.3 13.6 %copy-start.8 = (f32[1024]{0:T(1024)S(1)}, f32[1024]{0:T(1024)}, u32[]{:S(2)}) copy-start(f32[1024]{0:T(1024)} %param.17) | copy-start | bytes 12292
  9.3 13.6 %copy-start.9 = (f32[1024]{0:T(1024)S(1)}, f32[1024]{0:T(1024)}, u32[]{:S(2)}) copy-start(f32[1024]{0:T(1024)} %param.16) | copy-start | bytes 12292
  13.4 0.8 copy-start.3
  14.2 6.9 %collective-permute-start = (bf16[15,1024]{1,0:T(8,128)(2,1)S(1)}, bf16[15,1024]{1,0:T(8,128)(2,1)S(1)}, u32[]{:S(2)}, u32[]{:S(2)}) collective-permute-start(bf16[15,1024]{1,0:T(8,128)(2,1)S(1)} %get-tuple-element.7), channel_id=1, source_target_pairs={{0,8},{8,16},{16,24},{24,32},{32,40},{40,48},{48,56},{56,64},{64,7... | collective-permute-start | bytes 92168 | tf_op jit(solution)/shard_map/ppermute | solution.py:17
  18.2 4.7 %collective-permute-start.1 = (bf16[15,1024]{1,0:T(8,128)(2,1)S(1)}, bf16[15,1024]{1,0:T(8,128)(2,1)S(1)}, u32[]{:S(2)}, u32[]{:S(2)}) collective-permute-start(bf16[15,1024]{1,0:T(8,128)(2,1)S(1)} %get-tuple-element.8), channel_id=1, source_target_pairs={{8,0},{16,8},{24,16},{32,24},{40,32},{48,40},{56,48},{64,56},{72,6... | collective-permute-start | bytes 92168 | tf_op jit(solution)/shard_map/ppermute | solution.py:19
  45.0 108.4 %copy-start.1 = (bf16[256,1024]{1,0:T(8,128)(2,1)}, bf16[256,1024]{1,0:T(8,128)(2,1)S(1)}, u32[]{:S(2)}) copy-start(bf16[256,1024]{1,0:T(8,128)(2,1)S(1)} %get-tuple-element.72) | copy-start | bytes 1572868
  91.4 112.0 %reduce-scatter.2.cloned.1.call-start = ((), (), s32[]{:S(2)}) async-start(), calls=%async_computation.3 | async-start | bytes 5242880 | tf_op jit(solution)/shard_map/reduce_scatter | solution.py:113
  153.4 60.6 %copy-start.7 = (bf16[1024,64]{0,1:T(8,128)(2,1)S(1)}, bf16[1024,64]{0,1:T(8,128)(2,1)}, u32[]{:S(2)}) copy-start(bf16[1024,64]{0,1:T(8,128)(2,1)} %param.19) | copy-start | bytes 393220
  203.4 38.7 %all-to-all-start.1 = ((bf16[64,8,1024]{2,1,0:T(8,128)(2,1)}), bf16[64,8,1024]{2,1,0:T(8,128)(2,1)S(1)}, u32[]{:S(2)}, u32[]{:S(2)}) async-start(bf16[64,8,1024]{2,1,0:T(8,128)(2,1)} %bitcast.109), calls=%async_computation.2 | async-start | bytes 2097152 | tf_op jit(solution)/shard_map/all_to_all | solution.py:114
Sparse Core Ops, SparseCore 0:
  91.5 48.7 all-gather.2
  153.5 49.7 reduce-scatter.1

commit v5 on v4

--- a/solution.py
+++ b/solution.py
@@ -4,6 +4,7 @@
 from jax.sharding import Mesh, PartitionSpec as P
 
 QUARTERS = 4
+CHUNKS = 2
 
 
 def padded_2(cells, sides, width):
@@ -107,11 +108,16 @@
     send_buffer = send_buffer.reshape(owners * per_owner, capacity, model_width)
     w_in = expert_in[0, 0]
     w_out = expert_out[0, 0]
-    by_member = lax.all_to_all(send_buffer, ("expert", "z"), split_axis=0, concat_axis=0, tiled=True)
-    gathered = lax.all_gather(by_member, "y", axis=0, tiled=False)
-    partial_out = expert_pass(gathered, w_in, w_out)
-    summed = lax.psum_scatter(partial_out, "y", scatter_dimension=0, tiled=False)
-    results = lax.all_to_all(summed, ("expert", "z"), split_axis=0, concat_axis=0, tiled=True)
+    chunk_results = []
+    for chunk in jnp.split(send_buffer, CHUNKS, axis=1):
+        by_member = lax.all_to_all(chunk, ("expert", "z"), split_axis=0, concat_axis=0, tiled=True)
+        gathered = lax.all_gather(by_member, "y", axis=0, tiled=False)
+        partial_out = expert_pass(gathered, w_in, w_out)
+        summed = lax.psum_scatter(partial_out, "y", scatter_dimension=0, tiled=False)
+        chunk_results.append(
+            lax.all_to_all(summed, ("expert", "z"), split_axis=0, concat_axis=0, tiled=True)
+        )
+    results = jnp.concatenate(chunk_results, axis=1)
     frame_moe = results.reshape(-1, model_width)[slot_index]
     layer_out = mixed_res.astype(jnp.float32) + gate_value[:, None] * frame_moe.astype(jnp.float32)
     return layer_out.astype(jnp.bfloat16)[None]

time: 253 us -> 262 us (1.036)
  waiting for transfers between devices: 127 us -> 77.9 us
  local copies, waits for them, and re-layouts: 3.18 us -> 33.1 us
  blocking collectives: 43.3 us -> 55.7 us
  starting transfers between devices: 16.2 us -> 26.9 us
    all_gather x1 -> x2, waiting for transfers between devices: 48.7 us -> 22.9 us  [shards(): gathered = lax.all_gather(by_member, 'y', axis=0, tiled=False)]
    reshape x1 -> x7, local copies, waits for them, and re-layouts: 0.09 us -> 23.4 us  [the longest x4 15.4 us: expert_pass(): return partial_out.reshape(slot_block.shape)]
    reduce_scatter x1 -> x2, waiting for transfers between devices: 49.9 us -> 36.6 us  [shards(): lax.psum_scatter(partial_out, 'y', scatter_dimension=0, tiled=False)]
    all_to_all x1 -> x2, blocking collectives: 43.3 us -> 55.7 us  [shards(): lax.all_to_all(chunk, ('expert', 'z'), split_axis=0, concat_axis=0, tiled...]
    all_to_all x1 -> x2, starting transfers between devices: 10.6 us -> 21.4 us  [shards(): lax.all_to_all(summed, ('expert', 'z'), split_axis=0, concat_axis=0, tile...]
    all_to_all x1 -> x2, waiting for transfers between devices: 26.6 us -> 16.6 us  [shards(): lax.all_to_all(summed, ('expert', 'z'), split_axis=0, concat_axis=0, tile...]
    reduce_scatter x0 -> x2, local copies, waits for them, and re-layouts: none -> 4.54 us  [shards(): lax.psum_scatter(partial_out, 'y', scatter_dimension=0, tiled=False)]
    dot_general x1 -> x2, matrix products: 13 us -> 16.5 us  [expert_pass(): jnp.dot(hidden, w_out, preferred_element_type=jnp.float32)]
  transfers between devices with their start and end apart: 5 -> 8, of which waited for: 4 -> 6; matrix products, arithmetic and copies ran while one was open for 1% -> 18% of each run, Pallas kernels for 0% -> 0%
where the time goes in v5:
time: 262 us; the launch traced here: 261 us
  waiting for transfers between devices  77.9 us (30%)
  blocking collectives  55.7 us (21%)
  matrix products  42.7 us (16%)
  local copies, waits for them, and re-layouts  33.1 us (13%)
  starting transfers between devices  26.9 us (10%)
  between operations  13.4 us (5%)
  other arithmetic  11.1 us (4%)
    all_to_all x2, blocking collectives, shards(): lax.all_to_all(chunk, ('expert', 'z'), split_axis=0, concat_axis=0, tiled...  55.7 us
    reduce_scatter x2, waiting for transfers between devices, shards(): lax.psum_scatter(partial_out, 'y', scatter_dimension=0, tiled=False)  36.6 us
    all_gather x2, waiting for transfers between devices, shards(): gathered = lax.all_gather(by_member, 'y', axis=0, tiled=False)  22.9 us
    dot_general x1, matrix products, shards(): jnp.dot(activated, point_out, preferred_element_type=jnp.float32)  22.1 us
    all_to_all x2, starting transfers between devices, shards(): lax.all_to_all(summed, ('expert', 'z'), split_axis=0, concat_axis=0, tile...  21.4 us
    all_to_all x2, waiting for transfers between devices, shards(): lax.all_to_all(summed, ('expert', 'z'), split_axis=0, concat_axis=0, tile...  16.6 us
    dot_general x2, matrix products, expert_pass(): jnp.dot(hidden, w_out, preferred_element_type=jnp.float32)  16.5 us
    reshape x4, local copies, waits for them, and re-layouts, expert_pass(): return partial_out.reshape(slot_block.shape)  15.4 us
  transfers between devices with their start and end apart: 8, of which 6 were waited for; matrix products, arithmetic and copies ran while one was open for 18% of the time, Pallas kernels for 0%

profile of v5, /device:TPU:1, one launch (start us, length us, event | category | flops | bytes accessed | tf_op | source)
XLA Modules:
  0.0 260.7 jit_solution(4549084353983346662)
XLA Ops:
  6.5 0.0 copy-start
  6.5 0.0 all-gather.5.cloned.1.call-start
  6.5 1.3 convert_reduce_fusion.1
  7.9 1.3 fusion.31
  9.2 3.7 %fusion.40 = f32[256,2048]{1,0:T(8,128)S(1)} fusion(bf16[1024,2048]{1,0:T(8,128)(2,1)} %param.14, bf16[1,256,1024]{2,1,0:T(8,128)(2,1)} %param.11, f32[256]{0:T(256)S(1)} %add_rsqrt_fusion.1, f32[256]{0:T(256)S(1)} %broadcast_multiply_fusion.1), kind=kOutput, calls=%fused_computation.70 | convolution fusion | flops 1074790400 | bytes 6817792 | tf_op jit(solution)/shard_map/dot_general | solution.py:61
  12.9 0.0 copy-start.5
  12.9 0.0 copy-start.7
  13.0 0.0 copy-start.6
  13.0 0.0 copy-start.2
  13.0 0.0 copy-start.9
  13.0 0.0 copy-start.10
  13.0 0.3 fusion.38
  13.3 0.0 copy-start.4
  13.3 0.8 copy-done.4
  14.1 4.0 %collective-permute-start = (bf16[15,1024]{1,0:T(8,128)(2,1)S(1)}, bf16[15,1024]{1,0:T(8,128)(2,1)S(1)}, u32[]{:S(2)}, u32[]{:S(2)}) collective-permute-start(bf16[15,1024]{1,0:T(8,128)(2,1)S(1)} %get-tuple-element.9), channel_id=1, source_target_pairs={{0,8},{8,16},{16,24},{24,32},{32,40},{40,48},{48,56},{56,64},{64,7... | collective-permute-start | bytes 92168 | tf_op jit(solution)/shard_map/ppermute | solution.py:18
  18.1 1.3 collective-permute-start.1
  19.4 0.0 copy-done.5
  19.4 0.1 fusion.87
  19.6 0.0 copy-done.7
  19.6 0.1 copy.27
  19.7 0.1 reduce-window.10
  19.7 0.1 reduce.1
  19.9 0.6 reduce-window.11
  20.5 0.2 slice_reduce_fusion
  20.7 0.1 select_reduce_fusion.1
  20.9 0.1 fusion.75
  21.0 0.0 collective-permute-done
  21.0 1.8 collective-permute-done.1
  22.8 22.1 %convert_reduce_fusion = (f32[256]{0:T(256)S(1)}, bf16[256,1024]{1,0:T(8,128)(2,1)S(1)}) fusion(bf16[1024,1024]{1,0:T(8,128)(2,1)} %param.18, bf16[256,1024]{1,0:T(8,128)(2,1)} %copy-done.4, bf16[15,1024]{1,0:T(8,128)(2,1)S(1)} %collective-permute-done.1, bf16[15,1024]{1,0:T(8,128)(2,1)S(1)} %collective-permute-done, f32[1024]{0:T(1024)S(1)} %copy-done.9, ...), kind=kOutput, calls=%fused_computation.44 | convolution fusion | flops 595853056 | bytes 3899392 | tf_op jit(solution)/shard_map/dot_general | solution.py:86
  44.9 0.0 copy-start.1
  44.9 0.3 fusion.29
  45.2 2.8 %scatter_custom_fusion = bf16[512,1024]{1,0:T(8,128)(2,1)} fusion(s32[256]{0:T(256)S(1)} %bitcast.155, bf16[]{:T(256)} %constant.125.clone.1, bf16[256,1024]{1,0:T(8,128)(2,1)S(1)} %get-tuple-element.74, f32[256]{0:T(256)S(1)} %add_rsqrt_fusion, f32[256]{0:T(256)S(1)} %broadcast_multiply_fusion), kind=kCustom, calls=%fused_computation.118 | custom fusion | flops 1048576 | bytes 1574914 | tf_op jit(solution)/shard_map/scatter | solution.py:106
  48.0 2.0 fusion.85
  50.0 32.1 %all_to_all.20 = bf16[64,4,1024]{2,1,0:T(4,128)(2,1)} all-to-all(bf16[64,4,1024]{2,1,0:T(4,128)(2,1)S(1)} %get-tuple-element.7), channel_id=1, replica_groups=mesh['z'=8,'y'=4,'expert'=8] {'expert','z'}, dimensions={0} | all-to-all | bytes 1048576 | tf_op jit(solution)/shard_map/all_to_all | solution.py:113
  82.1 0.0 all-gather.5.cloned.1.call-update
  82.2 0.0 all-gather.7.cloned.1.call-start
  82.2 23.6 %all_to_all.21 = bf16[64,4,1024]{2,1,0:T(4,128)(2,1)} all-to-all(bf16[64,4,1024]{2,1,0:T(4,128)(2,1)S(1)} %get-tuple-element.8), channel_id=1, replica_groups=mesh['z'=8,'y'=4,'expert'=8] {'expert','z'}, dimensions={0} | all-to-all | bytes 1048576 | tf_op jit(solution)/shard_map/all_to_all | solution.py:113
  105.8 0.0 all-gather.7.cloned.1.call-update
  105.8 0.0 reduce-scatter.3.cloned.1.call-start
  105.9 7.6 %all-gather.5.cloned.1.call-done = bf16[256,4,1024]{2,1,0:T(4,128)(2,1)} async-done(((bf16[64,4,1024]{2,1,0:T(4,128)(2,1)}), bf16[256,4,1024]{2,1,0:T(4,128)(2,1)}) %all-gather.5.cloned.1.call-update) | async-done | bytes 2097168 | tf_op jit(solution)/shard_map/all_gather | solution.py:114
  113.4 4.0 %reshape.546 = bf16[1024,1024]{1,0:T(8,128)(2,1)} reshape(bf16[256,4,1024]{2,1,0:T(4,128)(2,1)} %all-gather.5.cloned.1.call-done) | data formatting | bytes 4194304 | tf_op jit(solution)/shard_map/reshape | solution.py:35
  117.4 8.2 %fusion.8 = bf16[1024,1024]{1,0:T(8,128)(2,1)} fusion(bf16[1,1,1024,1024]{3,2,1,0:T(8,128)(2,1)S(1)} %copy-done, bf16[1024,1024]{1,0:T(8,128)(2,1)} %reshape.546, bf16[1,1,1024,1024]{3,2,1,0:T(8,128)(2,1)} %param.20), kind=kOutput, calls=%fused_computation.40 | convolution fusion | flops 4301258752 | bytes 8388608 | tf_op jit(solution)/shard_map/dot_general | solution.py:39
  125.6 4.2 %reshape.547 = bf16[4,64,4,1024]{3,2,1,0:T(4,128)(2,1)} reshape(bf16[1024,1024]{1,0:T(8,128)(2,1)} %fusion.8) | data formatting | bytes 4194304 | tf_op jit(solution)/shard_map/reshape | solution.py:40
  129.8 3.5 %copy.29 = bf16[4,64,4,1024]{3,1,2,0:T(8,128)(2,1)} copy(bf16[4,64,4,1024]{3,2,1,0:T(4,128)(2,1)} %reshape.547) | data formatting | bytes 4194304 | tf_op jit(solution)/shard_map/reshape | solution.py:40
  133.3 0.0 reduce-scatter.3.cloned.1.call-update
  133.4 0.0 reduce-scatter.5.cloned.1.call-start
  133.4 15.3 %all-gather.7.cloned.1.call-done = bf16[256,4,1024]{2,1,0:T(4,128)(2,1)} async-done(((bf16[64,4,1024]{2,1,0:T(4,128)(2,1)}), bf16[256,4,1024]{2,1,0:T(4,128)(2,1)}) %all-gather.7.cloned.1.call-update) | async-done | bytes 2097168 | tf_op jit(solution)/shard_map/all_gather | solution.py:114
  148.7 4.0 %reshape.548 = bf16[1024,1024]{1,0:T(8,128)(2,1)} reshape(bf16[256,4,1024]{2,1,0:T(4,128)(2,1)} %all-gather.7.cloned.1.call-done) | data formatting | bytes 4194304 | tf_op jit(solution)/shard_map/reshape | solution.py:35
  152.7 8.3 %fusion.11 = bf16[1024,1024]{1,0:T(8,128)(2,1)} fusion(bf16[1,1,1024,1024]{3,2,1,0:T(8,128)(2,1)S(1)} %copy-done, bf16[1024,1024]{1,0:T(8,128)(2,1)} %reshape.548, bf16[1,1,1024,1024]{3,2,1,0:T(8,128)(2,1)} %param.20), kind=kOutput, calls=%fused_computation.41 | convolution fusion | flops 4301258752 | bytes 8388608 | tf_op jit(solution)/shard_map/dot_general | solution.py:39
  161.0 4.1 %reshape.549 = bf16[4,64,4,1024]{3,2,1,0:T(4,128)(2,1)} reshape(bf16[1024,1024]{1,0:T(8,128)(2,1)} %fusion.11) | data formatting | bytes 4194304 | tf_op jit(solution)/shard_map/reshape | solution.py:40
  165.1 3.6 %copy.31 = bf16[4,64,4,1024]{3,1,2,0:T(8,128)(2,1)} copy(bf16[4,64,4,1024]{3,2,1,0:T(4,128)(2,1)} %reshape.549) | data formatting | bytes 4194304 | tf_op jit(solution)/shard_map/reshape | solution.py:40
  168.7 0.0 reduce-scatter.5.cloned.1.call-update
  168.7 14.9 %reduce-scatter.3.cloned.1.call-done = bf16[1,64,4,1024]{3,1,2,0:T(8,128)(2,1)} async-done(((bf16[4,64,4,1024]{3,1,2,0:T(8,128)(2,1)}), bf16[1,64,4,1024]{3,1,2,0:T(8,128)(2,1)}) %reduce-scatter.3.cloned.1.call-update) | async-done | bytes 524304 | tf_op jit(solution)/shard_map/reduce_scatter | solution.py:116
  183.6 2.3 copy.30
  185.9 10.6 %all-to-all-start.1 = ((bf16[64,4,1024]{2,1,0:T(4,128)(2,1)}), bf16[64,4,1024]{2,1,0:T(4,128)(2,1)S(1)}, u32[]{:S(2)}, u32[]{:S(2)}) async-start(bf16[64,4,1024]{2,1,0:T(4,128)(2,1)} %copy.30), calls=%async_computation.2 | async-start | bytes 1048576 | tf_op jit(solution)/shard_map/all_to_all | solution.py:118
  196.6 21.7 %reduce-scatter.5.cloned.1.call-done = bf16[1,64,4,1024]{3,1,2,0:T(8,128)(2,1)} async-done(((bf16[4,64,4,1024]{3,1,2,0:T(8,128)(2,1)}), bf16[1,64,4,1024]{3,1,2,0:T(8,128)(2,1)}) %reduce-scatter.5.cloned.1.call-update) | async-done | bytes 524304 | tf_op jit(solution)/shard_map/reduce_scatter | solution.py:116
  218.2 2.2 copy.32
  220.5 0.0 all-to-all-done.1
  220.5 10.8 %all-to-all-start.3 = ((bf16[64,4,1024]{2,1,0:T(4,128)(2,1)}), bf16[64,4,1024]{2,1,0:T(4,128)(2,1)}, u32[]{:S(2)}, u32[]{:S(2)}) async-start(bf16[64,4,1024]{2,1,0:T(4,128)(2,1)} %copy.32), calls=%async_computation.5 | async-start | bytes 1048576 | tf_op jit(solution)/shard_map/all_to_all | solution.py:118
  231.3 0.4 fusion.28
  231.7 16.6 %all-to-all-done.3 = bf16[64,4,1024]{2,1,0:T(4,128)(2,1)} async-done(((bf16[64,4,1024]{2,1,0:T(4,128)(2,1)}), bf16[64,4,1024]{2,1,0:T(4,128)(2,1)}, u32[]{:S(2)}, u32[]{:S(2)}) %all-to-all-start.3) | async-done | bytes 524320 | tf_op jit(solution)/shard_map/all_to_all | solution.py:118
  248.3 1.7 maximum_bitcast_fusion
  250.0 2.0 gather_fusion
  252.0 2.2 fusion.39
  (25 shorter events, 0.2 us)
Async XLA Ops:
  6.5 110.9 %copy-start = (bf16[1,1,1024,1024]{3,2,1,0:T(8,128)(2,1)S(1)}, bf16[1,1,1024,1024]{3,2,1,0:T(8,128)(2,1)}, u32[]{:S(2)}) copy-start(bf16[1,1,1024,1024]{3,2,1,0:T(8,128)(2,1)} %param.21) | copy-start | bytes 6291460
  6.5 106.9 %all-gather.5.cloned.1.call-start = ((), (), s32[]{:S(2)}) async-start(), calls=%async_computation.8 | async-start | bytes 2621440 | tf_op jit(solution)/shard_map/all_gather | solution.py:114
  12.9 6.5 %copy-start.5 = (f32[31,1024]{1,0:T(8,128)S(1)}, f32[31,1024]{1,0:T(8,128)}, u32[]{:S(2)}) copy-start(f32[31,1024]{1,0:T(8,128)} %param.15) | copy-start | bytes 380932
  12.9 6.6 %copy-start.7 = (s32[1,32]{1,0:T(1,128)S(1)}, s32[1,32]{1,0:T(1,128)}, u32[]{:S(2)}) copy-start(s32[1,32]{1,0:T(1,128)} %param.12) | copy-start | bytes 388
  13.0 6.9 %copy-start.6 = (s32[1,256,1]{1,2,0:T(1,128)S(1)}, s32[1,256,1]{1,2,0:T(1,128)}, u32[]{:S(2)}) copy-start(s32[1,256,1]{1,2,0:T(1,128)} %param.13) | copy-start | bytes 3076
  13.0 9.8 %copy-start.2 = (bf16[1,256,1024]{2,1,0:T(8,128)(2,1)S(1)}, bf16[1,256,1024]{2,1,0:T(8,128)(2,1)}, u32[]{:S(2)}) copy-start(bf16[1,256,1024]{2,1,0:T(8,128)(2,1)} %param.11) | copy-start | bytes 1572868
  13.0 9.8 %copy-start.9 = (f32[1024]{0:T(1024)S(1)}, f32[1024]{0:T(1024)}, u32[]{:S(2)}) copy-start(f32[1024]{0:T(1024)} %param.17) | copy-start | bytes 12292
  13.0 9.8 %copy-start.10 = (f32[1024]{0:T(1024)S(1)}, f32[1024]{0:T(1024)}, u32[]{:S(2)}) copy-start(f32[1024]{0:T(1024)} %param.16) | copy-start | bytes 12292
  13.3 0.8 copy-start.4
  14.1 6.9 %collective-permute-start = (bf16[15,1024]{1,0:T(8,128)(2,1)S(1)}, bf16[15,1024]{1,0:T(8,128)(2,1)S(1)}, u32[]{:S(2)}, u32[]{:S(2)}) collective-permute-start(bf16[15,1024]{1,0:T(8,128)(2,1)S(1)} %get-tuple-element.9), channel_id=1, source_target_pairs={{0,8},{8,16},{16,24},{24,32},{32,40},{40,48},{48,56},{56,64},{64,7... | collective-permute-start | bytes 92168 | tf_op jit(solution)/shard_map/ppermute | solution.py:18
  18.1 4.7 %collective-permute-start.1 = (bf16[15,1024]{1,0:T(8,128)(2,1)S(1)}, bf16[15,1024]{1,0:T(8,128)(2,1)S(1)}, u32[]{:S(2)}, u32[]{:S(2)}) collective-permute-start(bf16[15,1024]{1,0:T(8,128)(2,1)S(1)} %get-tuple-element.10), channel_id=1, source_target_pairs={{8,0},{16,8},{24,16},{32,24},{40,32},{48,40},{56,48},{64,56},{72,6... | collective-permute-start | bytes 92168 | tf_op jit(solution)/shard_map/ppermute | solution.py:20
  44.9 186.4 %copy-start.1 = (bf16[256,1024]{1,0:T(8,128)(2,1)}, bf16[256,1024]{1,0:T(8,128)(2,1)S(1)}, u32[]{:S(2)}) copy-start(bf16[256,1024]{1,0:T(8,128)(2,1)S(1)} %get-tuple-element.74) | copy-start | bytes 1572868
  82.2 66.5 %all-gather.7.cloned.1.call-start = ((), (), s32[]{:S(2)}) async-start(), calls=%async_computation.9 | async-start | bytes 2621440 | tf_op jit(solution)/shard_map/all_gather | solution.py:114
  105.8 77.8 %reduce-scatter.3.cloned.1.call-start = ((), (), s32[]{:S(2)}) async-start(), calls=%async_computation.6 | async-start | bytes 2621440 | tf_op jit(solution)/shard_map/reduce_scatter | solution.py:116
  133.4 84.9 %reduce-scatter.5.cloned.1.call-start = ((), (), s32[]{:S(2)}) async-start(), calls=%async_computation.7 | async-start | bytes 2621440 | tf_op jit(solution)/shard_map/reduce_scatter | solution.py:116
  183.6 47.7 %copy-start.8 = (bf16[1024,64]{0,1:T(8,128)(2,1)S(1)}, bf16[1024,64]{0,1:T(8,128)(2,1)}, u32[]{:S(2)}) copy-start(bf16[1024,64]{0,1:T(8,128)(2,1)} %param.19) | copy-start | bytes 393220
  185.9 34.5 %all-to-all-start.1 = ((bf16[64,4,1024]{2,1,0:T(4,128)(2,1)}), bf16[64,4,1024]{2,1,0:T(4,128)(2,1)S(1)}, u32[]{:S(2)}, u32[]{:S(2)}) async-start(bf16[64,4,1024]{2,1,0:T(4,128)(2,1)} %copy.30), calls=%async_computation.2 | async-start | bytes 1048576 | tf_op jit(solution)/shard_map/all_to_all | solution.py:118
  220.5 11.2 %copy-start.3 = (bf16[64,4,1024]{2,1,0:T(4,128)(2,1)}, bf16[64,4,1024]{2,1,0:T(4,128)(2,1)S(1)}, u32[]{:S(2)}) copy-start(bf16[64,4,1024]{2,1,0:T(4,128)(2,1)S(1)} %all-to-all-done.1) | copy-start | bytes 1572868
  220.5 27.8 %all-to-all-start.3 = ((bf16[64,4,1024]{2,1,0:T(4,128)(2,1)}), bf16[64,4,1024]{2,1,0:T(4,128)(2,1)}, u32[]{:S(2)}, u32[]{:S(2)}) async-start(bf16[64,4,1024]{2,1,0:T(4,128)(2,1)} %copy.32), calls=%async_computation.5 | async-start | bytes 1048576 | tf_op jit(solution)/shard_map/all_to_all | solution.py:118
Sparse Core Ops, SparseCore 0:
  82.3 31.0 all-gather.4
  115.2 33.4 all-gather.6
  151.3 32.3 reduce-scatter.2
  186.2 31.9 reduce-scatter.4

commit v6 on v4

--- a/solution.py
+++ b/solution.py
@@ -1,9 +1,52 @@
 import jax
 import jax.numpy as jnp
 from jax import lax
+from jax.experimental import pallas as pl
+from jax.experimental.pallas import tpu as pltpu
 from jax.sharding import Mesh, PartitionSpec as P
 
 QUARTERS = 4
+ROW_BLOCK = 64
+LANE_BLOCK = 128
+
+
+def depthwise_kernel(pad_ref, taps_ref, first_ref, last_ref, scale_ref, shift_ref, out_ref, wide_ref):
+    frame_count = out_ref.shape[0]
+    tap_count = taps_ref.shape[0]
+    half_span = (tap_count - 1) // 2
+    wide_ref[...] = pad_ref[...].astype(jnp.float32)
+    for row in range(0, frame_count, ROW_BLOCK):
+        first_rel = first_ref[row : row + ROW_BLOCK, :]
+        last_rel = last_ref[row : row + ROW_BLOCK, :]
+        acc = jnp.zeros((ROW_BLOCK, out_ref.shape[1]), jnp.float32)
+        for tap in range(tap_count):
+            offset = tap - half_span
+            valid = (first_rel <= offset) & (offset < last_rel)
+            window = wide_ref[row + tap : row + tap + ROW_BLOCK, :]
+            acc = acc + taps_ref[tap : tap + 1, :] * jnp.where(valid, window, 0.0)
+        value = acc * scale_ref[...] + shift_ref[...]
+        out_ref[row : row + ROW_BLOCK, :] = (value * jax.nn.sigmoid(value)).astype(out_ref.dtype)
+
+
+def depthwise_silu(padded, taps, first_rel, last_rel, scale, shift):
+    rows, width = padded.shape
+    tap_count = taps.shape[0]
+    frame_count = rows - (tap_count - 1)
+    return pl.pallas_call(
+        depthwise_kernel,
+        grid=(width // LANE_BLOCK,),
+        in_specs=[
+            pl.BlockSpec((rows, LANE_BLOCK), lambda c: (0, c)),
+            pl.BlockSpec((tap_count, LANE_BLOCK), lambda c: (0, c)),
+            pl.BlockSpec((frame_count, 1), lambda c: (0, 0)),
+            pl.BlockSpec((frame_count, 1), lambda c: (0, 0)),
+            pl.BlockSpec((1, LANE_BLOCK), lambda c: (0, c)),
+            pl.BlockSpec((1, LANE_BLOCK), lambda c: (0, c)),
+        ],
+        out_specs=pl.BlockSpec((frame_count, LANE_BLOCK), lambda c: (0, c)),
+        out_shape=jax.ShapeDtypeStruct((frame_count, width), jnp.bfloat16),
+        scratch_shapes=[pltpu.VMEM((rows, LANE_BLOCK), jnp.float32)],
+    )(padded, taps, first_rel, last_rel, scale.reshape(1, -1), shift.reshape(1, -1))
 
 
 def padded_2(cells, sides, width):
@@ -71,14 +114,13 @@
     )
     first_pos = jnp.sum(jnp.where(inside, utter_starts[None, :], 0), axis=1, dtype=jnp.int32)
     last_pos = jnp.sum(jnp.where(inside, utter_ends[None, :], 0), axis=1, dtype=jnp.int32)
-    depth_sum = jnp.zeros((frame_count, model_width), jnp.float32)
-    for tap_index in range(tap_count):
-        nearby = position + (tap_index - half_span)
-        inside_tap = ((nearby >= first_pos) & (nearby < last_pos)).astype(jnp.float32)
-        window = padded[tap_index : tap_index + frame_count].astype(jnp.float32)
-        depth_sum = depth_sum + depth_taps[tap_index][None, :] * window * inside_tap[:, None]
-    activated = jax.nn.silu(depth_sum * norm_scale[None, :] + norm_shift[None, :]).astype(
-        jnp.bfloat16
+    activated = depthwise_silu(
+        padded,
+        depth_taps,
+        (first_pos - position)[:, None],
+        (last_pos - position)[:, None],
+        norm_scale,
+        norm_shift,
     )
     mixed_res = (
         signal.astype(jnp.float32)

time: 253 us -> 247 us (0.976)
  matrix products: 40.3 us -> 20.7 us
  Pallas kernels: 0 us -> 11 us
    dot_general x1, matrix products: 22.1 us -> 2.56 us  [shards(): jnp.dot(activated, point_out, preferred_element_type=jnp.float32)]
    pallas_call x0 -> x1, Pallas kernels: none -> 11 us  [depthwise_silu(): pl.pallas_call(depthwise_kernel, grid=(width // LANE_BLOCK,), in_specs=[p...]
  transfers between devices with their start and end apart: 5 -> 5, of which waited for: 4 -> 4; matrix products, arithmetic and copies ran while one was open for 1% -> 2% of each run, Pallas kernels for 0% -> 0%
where the time goes in v6:
time: 247 us; the launch traced here: 246 us
  waiting for transfers between devices  126 us (51%)
  blocking collectives  43.2 us (17%)
  matrix products  20.7 us (8%)
  starting transfers between devices  16.6 us (7%)
  between operations  13.6 us (6%)
  other arithmetic  11.8 us (5%)
  Pallas kernels  11 us (4%)
  local copies, waits for them, and re-layouts  3.18 us (1%)
    reduce_scatter x1, waiting for transfers between devices, shards(): lax.psum_scatter(partial_out, 'y', scatter_dimension=0, tiled=False)  49.9 us
    all_gather x1, waiting for transfers between devices, shards(): gathered = lax.all_gather(by_member, 'y', axis=0, tiled=False)  48.4 us
    all_to_all x1, blocking collectives, shards(): lax.all_to_all(send_buffer, ('expert', 'z'), split_axis=0, concat_axis=0,...  43.2 us
    all_to_all x1, waiting for transfers between devices, shards(): lax.all_to_all(summed, ('expert', 'z'), split_axis=0, concat_axis=0, tile...  26.6 us
    dot_general x1, matrix products, expert_pass(): jnp.dot(hidden, w_out, preferred_element_type=jnp.float32)  13 us
    pallas_call x1, Pallas kernels, depthwise_silu(): pl.pallas_call(depthwise_kernel, grid=(width // LANE_BLOCK,), in_specs=[p...  11 us
    all_to_all x1, starting transfers between devices, shards(): lax.all_to_all(summed, ('expert', 'z'), split_axis=0, concat_axis=0, tile...  10.6 us
  transfers between devices with their start and end apart: 5, of which 4 were waited for; matrix products, arithmetic and copies ran while one was open for 2% of the time, Pallas kernels for 0%

profile of v6, /device:TPU:1, one launch (start us, length us, event | category | flops | bytes accessed | tf_op | source)
XLA Modules:
  0.0 246.3 jit_solution(10113607358521003725)
XLA Ops:
  6.5 0.0 copy-start
  6.5 0.0 all-gather.3.cloned.1.call-start
  6.5 1.3 convert_reduce_fusion.1
  7.9 1.3 fusion.20
  9.2 0.0 copy-start.4
  9.2 0.0 copy-start.3
  9.2 3.7 %fusion.29 = f32[256,2048]{1,0:T(8,128)S(1)} fusion(bf16[1024,2048]{1,0:T(8,128)(2,1)} %param.14, bf16[1,256,1024]{2,1,0:T(8,128)(2,1)} %param.11, f32[256]{0:T(256)S(1)} %add_rsqrt_fusion.1, f32[256]{0:T(256)S(1)} %broadcast_multiply_fusion.1), kind=kOutput, calls=%fused_computation.36 | convolution fusion | flops 1074790400 | bytes 6817792 | tf_op jit(solution)/shard_map/dot_general | solution.py:103
  13.0 0.0 copy-start.2
  13.0 0.3 fusion.27
  13.3 0.6 fusion.45
  13.9 4.6 %collective-permute-start = (bf16[15,1024]{1,0:T(8,128)(2,1)}, bf16[15,1024]{1,0:T(8,128)(2,1)}, u32[]{:S(2)}, u32[]{:S(2)}) collective-permute-start(bf16[15,1024]{1,0:T(8,128)(2,1)} %get-tuple-element.7), channel_id=1, source_target_pairs={{0,8},{8,16},{16,24},{24,32},{32,40},{40,48},{48,56},{56,64},{64,7... | collective-permute-start | bytes 92168 | tf_op jit(solution)/shard_map/ppermute | solution.py:60
  18.5 1.3 collective-permute-start.1
  19.8 0.0 copy-done.4
  19.8 0.1 copy.26
  19.9 0.1 reduce-window.10
  20.0 0.1 reduce.1
  20.1 0.1 select_reduce_fusion
  20.2 0.1 copy.28
  20.3 0.1 copy.29
  20.5 0.0 copy-done.3
  20.5 0.6 reduce-window.11
  21.1 0.2 slice_reduce_fusion
  21.4 0.7 fusion.35
  22.1 0.1 fusion.38
  22.2 0.0 collective-permute-done
  22.2 1.3 collective-permute-done.1
  23.5 1.7 pad_maximum_fusion.pad_ref
  25.2 11.0 %shard_map.109 = bf16[256,1024]{1,0:T(8,128)(2,1)} custom-call(bf16[286,1024]{1,0:T(8,128)(2,1)} %pad_maximum_fusion.pad_ref, f32[31,1024]{1,0:T(8,128)} %taps_ref.1, s32[256,1]{1,0:T(8,128)} %get-tuple-element.12.first_ref, s32[256,1]{1,0:T(8,128)} %get-tuple-element.11.last_ref, f32[1,1024]{1,0:T(1,128)} %bitcast.87, f32[1,1024]{1,0:T(1,128)} %bitcast.88), custom_call_target="tpu_custom_call" | custom-call | tf_op jit(solution)/shard_map/pallas_call | solution.py:35
  36.2 0.0 copy-done.2
  36.2 2.6 %convert_reduce_fusion = (f32[256]{0:T(256)S(1)}, bf16[256,1024]{1,0:T(8,128)(2,1)S(1)}) fusion(bf16[256,1024]{1,0:T(8,128)(2,1)} %shard_map.109, bf16[1024,1024]{1,0:T(8,128)(2,1)} %param.18, bf16[1,256,1024]{2,1,0:T(8,128)(2,1)S(1)} %copy-done.2), kind=kOutput, calls=%fused_computation.11 | convolution fusion | flops 538181376 | bytes 3671040 | tf_op jit(solution)/shard_map/dot_general | solution.py:127
  38.8 0.0 copy-start.1
  38.8 0.3 fusion.18
  39.1 2.8 %scatter_custom_fusion = bf16[512,1024]{1,0:T(8,128)(2,1)} fusion(s32[256]{0:T(256)S(1)} %bitcast.92, bf16[]{:T(256)} %constant.64.clone.1, bf16[256,1024]{1,0:T(8,128)(2,1)S(1)} %get-tuple-element.10, f32[256]{0:T(256)S(1)} %add_rsqrt_fusion, f32[256]{0:T(256)S(1)} %broadcast_multiply_fusion), kind=kCustom, calls=%fused_computation.37 | custom fusion | flops 1048576 | bytes 1574914 | tf_op jit(solution)/shard_map/scatter | solution.py:147
  41.9 43.2 %all_to_all.10 = bf16[64,8,1024]{2,1,0:T(8,128)(2,1)} all-to-all(bf16[64,8,1024]{2,1,0:T(8,128)(2,1)} %bitcast.82), channel_id=1, replica_groups=mesh['z'=8,'y'=4,'expert'=8] {'expert','z'}, dimensions={0} | all-to-all | bytes 2097152 | tf_op jit(solution)/shard_map/all_to_all | solution.py:152
  85.1 0.0 all-gather.3.cloned.1.call-update
  85.1 0.0 reduce-scatter.2.cloned.1.call-start
  85.2 48.4 %all-gather.3.cloned.1.call-done = bf16[256,8,1024]{2,1,0:T(8,128)(2,1)} async-done(((bf16[64,8,1024]{2,1,0:T(8,128)(2,1)}), bf16[256,8,1024]{2,1,0:T(8,128)(2,1)}) %all-gather.3.cloned.1.call-update) | async-done | bytes 4194320 | tf_op jit(solution)/shard_map/all_gather | solution.py:153
  133.6 0.0 copy-done
  133.6 13.0 %fusion.3 = bf16[2048,1024]{1,0:T(8,128)(2,1)} fusion(bf16[256,8,1024]{2,1,0:T(8,128)(2,1)} %all-gather.3.cloned.1.call-done, bf16[1,1,1024,1024]{3,2,1,0:T(8,128)(2,1)S(1)} %copy-done, bf16[1,1,1024,1024]{3,2,1,0:T(8,128)(2,1)} %param.20), kind=kOutput, calls=%fused_computation.6 | convolution fusion | flops 8602517504 | bytes 12582912 | tf_op jit(solution)/shard_map/dot_general | solution.py:81
  146.6 0.0 copy-done.1
  146.6 0.0 copy-start.5
  146.6 0.0 reduce-scatter.2.cloned.1.call-update
  146.7 49.9 %reduce-scatter.2.cloned.1.call-done = bf16[1,64,8,1024]{3,2,1,0:T(8,128)(2,1)} async-done(((bf16[4,64,8,1024]{3,2,1,0:T(8,128)(2,1)}), bf16[1,64,8,1024]{3,2,1,0:T(8,128)(2,1)}) %reduce-scatter.2.cloned.1.call-update) | async-done | bytes 1048592 | tf_op jit(solution)/shard_map/reduce_scatter | solution.py:155
  196.6 10.6 %all-to-all-start.1 = ((bf16[64,8,1024]{2,1,0:T(8,128)(2,1)}), bf16[64,8,1024]{2,1,0:T(8,128)(2,1)S(1)}, u32[]{:S(2)}, u32[]{:S(2)}) async-start(bf16[64,8,1024]{2,1,0:T(8,128)(2,1)} %bitcast.83), calls=%async_computation.2 | async-start | bytes 2097152 | tf_op jit(solution)/shard_map/all_to_all | solution.py:156
  207.2 0.0 copy-done.5
  207.2 1.4 fusion.17
  208.7 26.6 %all-to-all-done.1 = bf16[64,8,1024]{2,1,0:T(8,128)(2,1)S(1)} async-done(((bf16[64,8,1024]{2,1,0:T(8,128)(2,1)}), bf16[64,8,1024]{2,1,0:T(8,128)(2,1)S(1)}, u32[]{:S(2)}, u32[]{:S(2)}) %all-to-all-start.1) | async-done | bytes 1048608 | tf_op jit(solution)/shard_map/all_to_all | solution.py:156
  235.3 2.0 gather_fusion
  237.2 2.2 fusion.28
  (12 shorter events, 0.1 us)
Async XLA Ops:
  6.5 127.1 %copy-start = (bf16[1,1,1024,1024]{3,2,1,0:T(8,128)(2,1)S(1)}, bf16[1,1,1024,1024]{3,2,1,0:T(8,128)(2,1)}, u32[]{:S(2)}) copy-start(bf16[1,1,1024,1024]{3,2,1,0:T(8,128)(2,1)} %param.21) | copy-start | bytes 6291460
  6.5 127.0 %all-gather.3.cloned.1.call-start = ((), (), s32[]{:S(2)}) async-start(), calls=%async_computation.4 | async-start | bytes 5242880 | tf_op jit(solution)/shard_map/all_gather | solution.py:153
  9.2 10.6 %copy-start.4 = (s32[1,32]{1,0:T(1,128)S(1)}, s32[1,32]{1,0:T(1,128)}, u32[]{:S(2)}) copy-start(s32[1,32]{1,0:T(1,128)} %param.12) | copy-start | bytes 388
  9.2 11.3 %copy-start.3 = (s32[1,256,1]{1,2,0:T(1,128)S(1)}, s32[1,256,1]{1,2,0:T(1,128)}, u32[]{:S(2)}) copy-start(s32[1,256,1]{1,2,0:T(1,128)} %param.13) | copy-start | bytes 3076
  13.0 23.3 %copy-start.2 = (bf16[1,256,1024]{2,1,0:T(8,128)(2,1)S(1)}, bf16[1,256,1024]{2,1,0:T(8,128)(2,1)}, u32[]{:S(2)}) copy-start(bf16[1,256,1024]{2,1,0:T(8,128)(2,1)} %param.11) | copy-start | bytes 1572868
  13.9 8.3 %collective-permute-start = (bf16[15,1024]{1,0:T(8,128)(2,1)}, bf16[15,1024]{1,0:T(8,128)(2,1)}, u32[]{:S(2)}, u32[]{:S(2)}) collective-permute-start(bf16[15,1024]{1,0:T(8,128)(2,1)} %get-tuple-element.7), channel_id=1, source_target_pairs={{0,8},{8,16},{16,24},{24,32},{32,40},{40,48},{48,56},{56,64},{64,7... | collective-permute-start | bytes 92168 | tf_op jit(solution)/shard_map/ppermute | solution.py:60
  18.5 5.0 %collective-permute-start.1 = (bf16[15,1024]{1,0:T(8,128)(2,1)}, bf16[15,1024]{1,0:T(8,128)(2,1)}, u32[]{:S(2)}, u32[]{:S(2)}) collective-permute-start(bf16[15,1024]{1,0:T(8,128)(2,1)} %get-tuple-element.8), channel_id=1, source_target_pairs={{8,0},{16,8},{24,16},{32,24},{40,32},{48,40},{56,48},{64,56},{72,6... | collective-permute-start | bytes 92168 | tf_op jit(solution)/shard_map/ppermute | solution.py:62
  38.8 107.8 %copy-start.1 = (bf16[256,1024]{1,0:T(8,128)(2,1)}, bf16[256,1024]{1,0:T(8,128)(2,1)S(1)}, u32[]{:S(2)}) copy-start(bf16[256,1024]{1,0:T(8,128)(2,1)S(1)} %get-tuple-element.10) | copy-start | bytes 1572868
  85.1 111.5 %reduce-scatter.2.cloned.1.call-start = ((), (), s32[]{:S(2)}) async-start(), calls=%async_computation.3 | async-start | bytes 5242880 | tf_op jit(solution)/shard_map/reduce_scatter | solution.py:155
  146.6 60.6 %copy-start.5 = (bf16[1024,64]{0,1:T(8,128)(2,1)S(1)}, bf16[1024,64]{0,1:T(8,128)(2,1)}, u32[]{:S(2)}) copy-start(bf16[1024,64]{0,1:T(8,128)(2,1)} %param.19) | copy-start | bytes 393220
  196.6 38.7 %all-to-all-start.1 = ((bf16[64,8,1024]{2,1,0:T(8,128)(2,1)}), bf16[64,8,1024]{2,1,0:T(8,128)(2,1)S(1)}, u32[]{:S(2)}, u32[]{:S(2)}) async-start(bf16[64,8,1024]{2,1,0:T(8,128)(2,1)} %bitcast.83), calls=%async_computation.2 | async-start | bytes 2097152 | tf_op jit(solution)/shard_map/all_to_all | solution.py:156
Sparse Core Ops, SparseCore 0:
  85.3 48.2 all-gather.2
  146.8 49.7 reduce-scatter.1

commit v7 on v6

--- a/solution.py
+++ b/solution.py
@@ -6,6 +6,7 @@
 from jax.sharding import Mesh, PartitionSpec as P
 
 QUARTERS = 4
+CHUNKS = 2
 ROW_BLOCK = 64
 LANE_BLOCK = 128
 
@@ -140,20 +141,25 @@
     gate_value = jax.nn.sigmoid(jnp.sum(logits * onehot.astype(jnp.float32), axis=1))
     owner_group = route_ids // per_owner
     member = route_ids % per_owner
-    slot_index = (owner_group * per_owner + member) * capacity + rank_in
+    slot_index = rank_in * expert_count + owner_group * per_owner + member
     send_buffer = (
         jnp.zeros((per_owner * owners * capacity, model_width), jnp.bfloat16)
         .at[slot_index]
         .set(moe_in)
     )
-    send_buffer = send_buffer.reshape(owners * per_owner, capacity, model_width)
+    send_buffer = send_buffer.reshape(capacity, expert_count, model_width)
     w_in = expert_in[0, 0]
     w_out = expert_out[0, 0]
-    by_member = lax.all_to_all(send_buffer, ("expert", "z"), split_axis=0, concat_axis=0, tiled=True)
-    gathered = lax.all_gather(by_member, "y", axis=0, tiled=False)
-    partial_out = expert_pass(gathered, w_in, w_out)
-    summed = lax.psum_scatter(partial_out, "y", scatter_dimension=0, tiled=False)
-    results = lax.all_to_all(summed, ("expert", "z"), split_axis=0, concat_axis=0, tiled=True)
+    chunk_results = []
+    for chunk in jnp.split(send_buffer, CHUNKS, axis=0):
+        by_member = lax.all_to_all(chunk, ("expert", "z"), split_axis=1, concat_axis=1, tiled=True)
+        gathered = lax.all_gather(by_member, "y", axis=0, tiled=False)
+        partial_out = expert_pass(gathered, w_in, w_out)
+        summed = lax.psum_scatter(partial_out, "y", scatter_dimension=0, tiled=False)
+        chunk_results.append(
+            lax.all_to_all(summed, ("expert", "z"), split_axis=1, concat_axis=1, tiled=True)
+        )
+    results = jnp.concatenate(chunk_results, axis=0)
     frame_moe = results.reshape(-1, model_width)[slot_index]
     layer_out = mixed_res.astype(jnp.float32) + gate_value[:, None] * frame_moe.astype(jnp.float32)
     return layer_out.astype(jnp.bfloat16)[None]

time: 247 us -> 256 us (1.036)
  waiting for transfers between devices: 126 us -> 98.8 us
  blocking collectives: 43.2 us -> 55.4 us
  starting transfers between devices: 16.6 us -> 27.6 us
  local copies, waits for them, and re-layouts: 3.18 us -> 12.3 us
    all_gather x1 -> x2, waiting for transfers between devices: 48.4 us -> 32.5 us  [shards(): gathered = lax.all_gather(by_member, 'y', axis=0, tiled=False)]
    all_to_all x1 -> x2, blocking collectives: 43.2 us -> 55.4 us  [shards(): lax.all_to_all(chunk, ('expert', 'z'), split_axis=1, concat_axis=1, tiled...]
    all_to_all x1 -> x2, starting transfers between devices: 10.6 us -> 21.4 us  [shards(): lax.all_to_all(summed, ('expert', 'z'), split_axis=1, concat_axis=1, tile...]
    all_to_all x1 -> x2, waiting for transfers between devices: 26.6 us -> 16.6 us  [shards(): lax.all_to_all(summed, ('expert', 'z'), split_axis=1, concat_axis=1, tile...]
    reduce_scatter x0 -> x2, local copies, waits for them, and re-layouts: none -> 4.53 us  [shards(): lax.psum_scatter(partial_out, 'y', scatter_dimension=0, tiled=False)]
    dot_general x1 -> x2, matrix products: 13 us -> 16.5 us  [expert_pass(): jnp.dot(hidden, w_out, preferred_element_type=jnp.float32)]
    reduce_scatter x1 -> x2, waiting for transfers between devices: 49.9 us -> 48.3 us  [shards(): lax.psum_scatter(partial_out, 'y', scatter_dimension=0, tiled=False)]
  transfers between devices with their start and end apart: 5 -> 8, of which waited for: 4 -> 6; matrix products, arithmetic and copies ran while one was open for 2% -> 10% of each run, Pallas kernels for 0% -> 0%
where the time goes in v7:
time: 256 us; the launch traced here: 255 us
  waiting for transfers between devices  98.8 us (39%)
  blocking collectives  55.4 us (22%)
  starting transfers between devices  27.6 us (11%)
  matrix products  23.2 us (9%)
  other arithmetic  13.4 us (5%)
  between operations  13.4 us (5%)
  local copies, waits for them, and re-layouts  12.3 us (5%)
  Pallas kernels  11 us (4%)
    all_to_all x2, blocking collectives, shards(): lax.all_to_all(chunk, ('expert', 'z'), split_axis=1, concat_axis=1, tiled...  55.4 us
    reduce_scatter x2, waiting for transfers between devices, shards(): lax.psum_scatter(partial_out, 'y', scatter_dimension=0, tiled=False)  48.3 us
    all_gather x2, waiting for transfers between devices, shards(): gathered = lax.all_gather(by_member, 'y', axis=0, tiled=False)  32.5 us
    all_to_all x2, starting transfers between devices, shards(): lax.all_to_all(summed, ('expert', 'z'), split_axis=1, concat_axis=1, tile...  21.4 us
    all_to_all x2, waiting for transfers between devices, shards(): lax.all_to_all(summed, ('expert', 'z'), split_axis=1, concat_axis=1, tile...  16.6 us
    dot_general x2, matrix products, expert_pass(): jnp.dot(hidden, w_out, preferred_element_type=jnp.float32)  16.5 us
    pallas_call x1, Pallas kernels, depthwise_silu(): pl.pallas_call(depthwise_kernel, grid=(width // LANE_BLOCK,), in_specs=[p...  11 us
  transfers between devices with their start and end apart: 8, of which 6 were waited for; matrix products, arithmetic and copies ran while one was open for 10% of the time, Pallas kernels for 0%

profile of v7, /device:TPU:1, one launch (start us, length us, event | category | flops | bytes accessed | tf_op | source)
XLA Modules:
  0.0 255.0 jit_solution(3378585908442709584)
XLA Ops:
  6.5 0.0 copy-start
  6.5 0.0 all-gather.5.cloned.1.call-start
  6.5 1.3 convert_reduce_fusion.1
  7.9 1.3 fusion.31
  9.2 3.7 %fusion.40 = f32[256,2048]{1,0:T(8,128)S(1)} fusion(bf16[1024,2048]{1,0:T(8,128)(2,1)} %param.14, bf16[1,256,1024]{2,1,0:T(8,128)(2,1)} %param.11, f32[256]{0:T(256)S(1)} %add_rsqrt_fusion.1, f32[256]{0:T(256)S(1)} %broadcast_multiply_fusion.2), kind=kOutput, calls=%fused_computation.42 | convolution fusion | flops 1074790400 | bytes 6817792 | tf_op jit(solution)/shard_map/dot_general | solution.py:104
  12.9 0.0 copy-start.4
  12.9 0.0 copy-start.3
  13.0 0.3 fusion.38
  13.2 0.0 copy-start.2
  13.3 0.6 fusion.58
  13.9 4.6 %collective-permute-start = (bf16[15,1024]{1,0:T(8,128)(2,1)}, bf16[15,1024]{1,0:T(8,128)(2,1)}, u32[]{:S(2)}, u32[]{:S(2)}) collective-permute-start(bf16[15,1024]{1,0:T(8,128)(2,1)} %get-tuple-element.9), channel_id=1, source_target_pairs={{0,8},{8,16},{16,24},{24,32},{32,40},{40,48},{48,56},{56,64},{64,7... | collective-permute-start | bytes 92168 | tf_op jit(solution)/shard_map/ppermute | solution.py:61
  18.5 1.3 collective-permute-start.1
  19.8 0.0 copy-done.4
  19.8 0.1 copy.60
  19.9 0.1 reduce-window.10
  20.0 0.1 reduce.1
  20.1 0.1 select_reduce_fusion
  20.2 0.1 copy.62
  20.3 0.1 copy.63
  20.5 0.0 copy-done.3
  20.5 0.6 reduce-window.11
  21.1 0.2 slice_reduce_fusion
  21.4 0.1 fusion.49
  21.5 0.7 fusion.46
  22.2 0.0 collective-permute-done
  22.2 1.3 collective-permute-done.1
  23.5 1.7 pad_maximum_fusion.1.pad_ref
  25.2 11.0 %shard_map.109 = bf16[256,1024]{1,0:T(8,128)(2,1)} custom-call(bf16[286,1024]{1,0:T(8,128)(2,1)} %pad_maximum_fusion.1.pad_ref, f32[31,1024]{1,0:T(8,128)} %taps_ref.1, s32[256,1]{1,0:T(8,128)} %get-tuple-element.14.first_ref, s32[256,1]{1,0:T(8,128)} %get-tuple-element.13.last_ref, f32[1,1024]{1,0:T(1,128)} %bitcast.107, f32[1,1024]{1,0:T(1,128)} %bitcast.108), custom_call_target="tpu_custom_call" | custom-call | tf_op jit(solution)/shard_map/pallas_call | solution.py:36
  36.2 0.0 copy-done.2
  36.2 2.6 %convert_reduce_fusion = (f32[256]{0:T(256)S(1)}, bf16[256,1024]{1,0:T(8,128)(2,1)S(1)}) fusion(bf16[256,1024]{1,0:T(8,128)(2,1)} %shard_map.109, bf16[1024,1024]{1,0:T(8,128)(2,1)} %param.18, bf16[1,256,1024]{2,1,0:T(8,128)(2,1)S(1)} %copy-done.2), kind=kOutput, calls=%fused_computation.16 | convolution fusion | flops 538181376 | bytes 3671040 | tf_op jit(solution)/shard_map/dot_general | solution.py:128
  38.8 0.3 fusion.29
  39.1 2.8 %scatter_custom_fusion = bf16[512,1024]{1,0:T(8,128)(2,1)} fusion(s32[256]{0:T(256)S(1)} %bitcast.111, bf16[]{:T(256)} %constant.66.clone.1, bf16[256,1024]{1,0:T(8,128)(2,1)S(1)} %get-tuple-element.12, f32[256]{0:T(256)S(1)} %add_rsqrt_fusion, f32[256]{0:T(256)S(1)} %broadcast_multiply_fusion.1), kind=kCustom, calls=%fused_computation.43 | custom fusion | flops 1048576 | bytes 1574914 | tf_op jit(solution)/shard_map/scatter | solution.py:148
  41.9 1.3 fusion.57
  43.2 0.4 copy.65
  43.6 31.9 %all_to_all.20 = bf16[4,64,1024]{2,0,1:T(4,128)(2,1)S(1)} all-to-all(bf16[4,64,1024]{2,0,1:T(4,128)(2,1)S(1)} %copy.65), channel_id=1, replica_groups=mesh['z'=8,'y'=4,'expert'=8] {'expert','z'}, dimensions={1} | all-to-all | bytes 1048576 | tf_op jit(solution)/shard_map/all_to_all | solution.py:155
  75.5 1.0 copy.66
  76.5 0.0 all-gather.5.cloned.1.call-update
  76.5 0.0 all-gather.7.cloned.1.call-start
  76.6 0.4 copy.68
  77.0 23.5 %all_to_all.21 = bf16[4,64,1024]{2,0,1:T(4,128)(2,1)S(1)} all-to-all(bf16[4,64,1024]{2,0,1:T(4,128)(2,1)S(1)} %copy.68), channel_id=1, replica_groups=mesh['z'=8,'y'=4,'expert'=8] {'expert','z'}, dimensions={1} | all-to-all | bytes 1048576 | tf_op jit(solution)/shard_map/all_to_all | solution.py:155
  100.4 1.0 copy.69
  101.4 0.0 all-gather.7.cloned.1.call-update
  101.4 0.2 reduce-scatter.3.cloned.1.call-start
  101.7 5.6 %all-gather.5.cloned.1.call-done = bf16[16,64,1024]{2,1,0:T(8,128)(2,1)} async-done(((bf16[4,64,1024]{2,1,0:T(8,128)(2,1)}), bf16[16,64,1024]{2,1,0:T(8,128)(2,1)}) %all-gather.5.cloned.1.call-update) | async-done | bytes 2097168 | tf_op jit(solution)/shard_map/all_gather | solution.py:156
  107.3 0.0 copy-done
  107.3 8.3 %fusion.8 = bf16[1024,1024]{1,0:T(8,128)(2,1)} fusion(bf16[1,1,1024,1024]{3,2,1,0:T(8,128)(2,1)S(1)} %copy-done, bf16[1024,1024]{1,0:T(8,128)(2,1)} %bitcast.115, bf16[1,1,1024,1024]{3,2,1,0:T(8,128)(2,1)} %param.20), kind=kOutput, calls=%fused_computation.12 | convolution fusion | flops 4301258752 | bytes 8388608 | tf_op jit(solution)/shard_map/dot_general | solution.py:82
  115.5 0.0 reduce-scatter.3.cloned.1.call-update
  115.6 0.0 reduce-scatter.5.cloned.1.call-start
  115.6 26.9 %all-gather.7.cloned.1.call-done = bf16[16,64,1024]{2,1,0:T(8,128)(2,1)} async-done(((bf16[4,64,1024]{2,1,0:T(8,128)(2,1)}), bf16[16,64,1024]{2,1,0:T(8,128)(2,1)}) %all-gather.7.cloned.1.call-update) | async-done | bytes 2097168 | tf_op jit(solution)/shard_map/all_gather | solution.py:156
  142.5 8.3 %fusion.11 = bf16[1024,1024]{1,0:T(8,128)(2,1)} fusion(bf16[1,1,1024,1024]{3,2,1,0:T(8,128)(2,1)S(1)} %copy-done, bf16[1024,1024]{1,0:T(8,128)(2,1)} %bitcast.116, bf16[1,1,1024,1024]{3,2,1,0:T(8,128)(2,1)} %param.20), kind=kOutput, calls=%fused_computation.13 | convolution fusion | flops 4301258752 | bytes 8388608 | tf_op jit(solution)/shard_map/dot_general | solution.py:82
  150.8 0.0 reduce-scatter.5.cloned.1.call-update
  150.8 26.7 %reduce-scatter.3.cloned.1.call-done = bf16[1,4,64,1024]{3,2,1,0:T(8,128)(2,1)} async-done(((bf16[4,4,64,1024]{3,2,1,0:T(8,128)(2,1)}), bf16[1,4,64,1024]{3,2,1,0:T(8,128)(2,1)}) %reduce-scatter.3.cloned.1.call-update) | async-done | bytes 524304 | tf_op jit(solution)/shard_map/reduce_scatter | solution.py:158
  177.5 2.3 copy.67
  179.8 10.6 %all-to-all-start.1 = ((bf16[4,64,1024]{2,0,1:T(4,128)(2,1)}), bf16[4,64,1024]{2,0,1:T(4,128)(2,1)S(1)}, u32[]{:S(2)}, u32[]{:S(2)}) async-start(bf16[4,64,1024]{2,0,1:T(4,128)(2,1)} %copy.67), calls=%async_computation.2 | async-start | bytes 1048576 | tf_op jit(solution)/shard_map/all_to_all | solution.py:160
  190.4 21.7 %reduce-scatter.5.cloned.1.call-done = bf16[1,4,64,1024]{3,2,1,0:T(8,128)(2,1)} async-done(((bf16[4,4,64,1024]{3,2,1,0:T(8,128)(2,1)}), bf16[1,4,64,1024]{3,2,1,0:T(8,128)(2,1)}) %reduce-scatter.5.cloned.1.call-update) | async-done | bytes 524304 | tf_op jit(solution)/shard_map/reduce_scatter | solution.py:158
  212.1 2.2 copy.70
  214.3 0.0 all-to-all-done.1
  214.3 10.8 %all-to-all-start.3 = ((bf16[4,64,1024]{2,0,1:T(4,128)(2,1)}), bf16[4,64,1024]{2,0,1:T(4,128)(2,1)}, u32[]{:S(2)}, u32[]{:S(2)}) async-start(bf16[4,64,1024]{2,0,1:T(4,128)(2,1)} %copy.70), calls=%async_computation.5 | async-start | bytes 1048576 | tf_op jit(solution)/shard_map/all_to_all | solution.py:160
  225.1 0.4 fusion.28
  225.5 16.6 %all-to-all-done.3 = bf16[4,64,1024]{2,0,1:T(4,128)(2,1)} async-done(((bf16[4,64,1024]{2,0,1:T(4,128)(2,1)}), bf16[4,64,1024]{2,0,1:T(4,128)(2,1)}, u32[]{:S(2)}, u32[]{:S(2)}) %all-to-all-start.3) | async-done | bytes 524320 | tf_op jit(solution)/shard_map/all_to_all | solution.py:160
  242.1 1.6 pad_maximum_fusion
  243.7 0.6 copy.71
  244.3 2.0 gather_fusion
  246.2 2.2 fusion.39
  (17 shorter events, 0.1 us)
Async XLA Ops:
  6.5 100.7 %copy-start = (bf16[1,1,1024,1024]{3,2,1,0:T(8,128)(2,1)S(1)}, bf16[1,1,1024,1024]{3,2,1,0:T(8,128)(2,1)}, u32[]{:S(2)}) copy-start(bf16[1,1,1024,1024]{3,2,1,0:T(8,128)(2,1)} %param.21) | copy-start | bytes 6291460
  6.5 100.7 %all-gather.5.cloned.1.call-start = ((), (), s32[]{:S(2)}) async-start(), calls=%async_computation.8 | async-start | bytes 2621440 | tf_op jit(solution)/shard_map/all_gather | solution.py:156
  12.9 6.9 %copy-start.4 = (s32[1,32]{1,0:T(1,128)S(1)}, s32[1,32]{1,0:T(1,128)}, u32[]{:S(2)}) copy-start(s32[1,32]{1,0:T(1,128)} %param.12) | copy-start | bytes 388
  12.9 7.5 %copy-start.3 = (s32[1,256,1]{1,2,0:T(1,128)S(1)}, s32[1,256,1]{1,2,0:T(1,128)}, u32[]{:S(2)}) copy-start(s32[1,256,1]{1,2,0:T(1,128)} %param.13) | copy-start | bytes 3076
  13.2 23.0 %copy-start.2 = (bf16[1,256,1024]{2,1,0:T(8,128)(2,1)S(1)}, bf16[1,256,1024]{2,1,0:T(8,128)(2,1)}, u32[]{:S(2)}) copy-start(bf16[1,256,1024]{2,1,0:T(8,128)(2,1)} %param.11) | copy-start | bytes 1572868
  13.9 8.3 %collective-permute-start = (bf16[15,1024]{1,0:T(8,128)(2,1)}, bf16[15,1024]{1,0:T(8,128)(2,1)}, u32[]{:S(2)}, u32[]{:S(2)}) collective-permute-start(bf16[15,1024]{1,0:T(8,128)(2,1)} %get-tuple-element.9), channel_id=1, source_target_pairs={{0,8},{8,16},{16,24},{24,32},{32,40},{40,48},{48,56},{56,64},{64,7... | collective-permute-start | bytes 92168 | tf_op jit(solution)/shard_map/ppermute | solution.py:61
  18.5 5.0 %collective-permute-start.1 = (bf16[15,1024]{1,0:T(8,128)(2,1)}, bf16[15,1024]{1,0:T(8,128)(2,1)}, u32[]{:S(2)}, u32[]{:S(2)}) collective-permute-start(bf16[15,1024]{1,0:T(8,128)(2,1)} %get-tuple-element.10), channel_id=1, source_target_pairs={{8,0},{16,8},{24,16},{32,24},{40,32},{48,40},{56,48},{64,56},{72,6... | collective-permute-start | bytes 92168 | tf_op jit(solution)/shard_map/ppermute | solution.py:63
  38.8 186.3 %copy-start.1 = (bf16[256,1024]{1,0:T(8,128)(2,1)}, bf16[256,1024]{1,0:T(8,128)(2,1)S(1)}, u32[]{:S(2)}) copy-start(bf16[256,1024]{1,0:T(8,128)(2,1)S(1)} %get-tuple-element.12) | copy-start | bytes 1572868
  76.5 66.0 %all-gather.7.cloned.1.call-start = ((), (), s32[]{:S(2)}) async-start(), calls=%async_computation.9 | async-start | bytes 2621440 | tf_op jit(solution)/shard_map/all_gather | solution.py:156
  101.4 76.0 %reduce-scatter.3.cloned.1.call-start = ((), (), s32[]{:S(2)}) async-start(), calls=%async_computation.6 | async-start | bytes 2621440 | tf_op jit(solution)/shard_map/reduce_scatter | solution.py:158
  115.6 96.5 %reduce-scatter.5.cloned.1.call-start = ((), (), s32[]{:S(2)}) async-start(), calls=%async_computation.7 | async-start | bytes 2621440 | tf_op jit(solution)/shard_map/reduce_scatter | solution.py:158
  177.5 47.6 %copy-start.5 = (bf16[1024,64]{0,1:T(8,128)(2,1)S(1)}, bf16[1024,64]{0,1:T(8,128)(2,1)}, u32[]{:S(2)}) copy-start(bf16[1024,64]{0,1:T(8,128)(2,1)} %param.19) | copy-start | bytes 393220
  179.8 34.5 %all-to-all-start.1 = ((bf16[4,64,1024]{2,0,1:T(4,128)(2,1)}), bf16[4,64,1024]{2,0,1:T(4,128)(2,1)S(1)}, u32[]{:S(2)}, u32[]{:S(2)}) async-start(bf16[4,64,1024]{2,0,1:T(4,128)(2,1)} %copy.67), calls=%async_computation.2 | async-start | bytes 1048576 | tf_op jit(solution)/shard_map/all_to_all | solution.py:160
  214.3 27.8 %all-to-all-start.3 = ((bf16[4,64,1024]{2,0,1:T(4,128)(2,1)}), bf16[4,64,1024]{2,0,1:T(4,128)(2,1)}, u32[]{:S(2)}, u32[]{:S(2)}) async-start(bf16[4,64,1024]{2,0,1:T(4,128)(2,1)} %copy.70), calls=%async_computation.5 | async-start | bytes 1048576 | tf_op jit(solution)/shard_map/all_to_all | solution.py:160
Sparse Core Ops, SparseCore 0:
  76.6 30.5 all-gather.4
  109.1 33.4 all-gather.6
  145.1 32.3 reduce-scatter.2
  180.0 31.9 reduce-scatter.4

commit v8 on v6

--- a/solution.py
+++ b/solution.py
@@ -49,21 +49,27 @@
     )(padded, taps, first_rel, last_rel, scale.reshape(1, -1), shift.reshape(1, -1))
 
 
-def padded_2(cells, sides, width):
-    for axis, dim in sides:
-        count = lax.axis_size(axis)
-        ends = count - 1
-        head = lax.slice_in_dim(cells, 0, width, axis=dim)
-        tail = lax.slice_in_dim(cells, cells.shape[dim] - width, cells.shape[dim], axis=dim)
-        cells = jnp.concatenate(
-            [
-                lax.ppermute(tail, axis, [(i, (i + 1) % count) for i in range(ends)]),
-                cells,
-                lax.ppermute(head, axis, [((i + 1) % count, i) for i in range(ends)]),
-            ],
-            axis=dim,
-        )
-    return cells
+def halo_rows(cells, axis, width):
+    count = lax.axis_size(axis)
+    ends = count - 1
+    head = cells[:width]
+    tail = cells[cells.shape[0] - width :]
+    return jnp.concatenate(
+        [
+            lax.ppermute(tail, axis, [(i, (i + 1) % count) for i in range(ends)]),
+            lax.ppermute(head, axis, [((i + 1) % count, i) for i in range(ends)]),
+        ],
+        axis=0,
+    )
+
+
+def gated_unit(rows, point_in):
+    model_width = rows.shape[1]
+    normed = layer_norm(rows).astype(jnp.bfloat16)
+    projected = jnp.dot(normed, point_in, preferred_element_type=jnp.float32)
+    return (projected[:, :model_width] * jax.nn.sigmoid(projected[:, model_width:])).astype(
+        jnp.bfloat16
+    )
 
 
 def layer_norm(values):
@@ -99,12 +105,12 @@
     frame_count, model_width = signal.shape
     tap_count = depth_taps.shape[0]
     half_span = (tap_count - 1) // 2
-    normed = layer_norm(signal).astype(jnp.bfloat16)
-    projected = jnp.dot(normed, point_in, preferred_element_type=jnp.float32)
-    gated_act = (projected[:, :model_width] * jax.nn.sigmoid(projected[:, model_width:])).astype(
-        jnp.bfloat16
+    halo = halo_rows(signal, ("z", "y"), half_span)
+    gated_act = gated_unit(signal, point_in)
+    gated_halo = gated_unit(halo, point_in)
+    padded = jnp.concatenate(
+        [gated_halo[:half_span], gated_act, gated_halo[half_span:]], axis=0
     )
-    padded = padded_2(gated_act, ((("z", "y"), 0),), half_span)
     lengths = utt_lengths[0]
     utter_ends = jnp.cumsum(lengths, dtype=jnp.int32)
     utter_starts = utter_ends - lengths

time: 247 us -> 248 us (level)
  matrix products: 20.7 us -> 23.8 us
  waiting for transfers between devices: 126 us -> 123 us
    dot_general x1 -> x2, matrix products: 3.7 us -> 6.75 us  [gated_unit(): projected = jnp.dot(normed, point_in, preferred_element_type=jnp.float32)]
  transfers between devices with their start and end apart: 5 -> 5, of which waited for: 4 -> 3; matrix products, arithmetic and copies ran while one was open for 2% -> 4% of each run, Pallas kernels for 0% -> 0%
where the time goes in v8:
time: 248 us; the launch traced here: 247 us
  waiting for transfers between devices  123 us (50%)
  blocking collectives  45 us (18%)
  matrix products  23.8 us (10%)
  starting transfers between devices  16 us (6%)
  between operations  13.6 us (5%)
  other arithmetic  11.3 us (5%)
  Pallas kernels  11 us (4%)
  local copies, waits for them, and re-layouts  4.11 us (2%)
    reduce_scatter x1, waiting for transfers between devices, shards(): lax.psum_scatter(partial_out, 'y', scatter_dimension=0, tiled=False)  49.9 us
    all_gather x1, waiting for transfers between devices, shards(): gathered = lax.all_gather(by_member, 'y', axis=0, tiled=False)  46 us
    all_to_all x1, blocking collectives, shards(): lax.all_to_all(send_buffer, ('expert', 'z'), split_axis=0, concat_axis=0,...  45 us
    all_to_all x1, waiting for transfers between devices, shards(): lax.all_to_all(summed, ('expert', 'z'), split_axis=0, concat_axis=0, tile...  26.6 us
    dot_general x1, matrix products, expert_pass(): jnp.dot(hidden, w_out, preferred_element_type=jnp.float32)  13 us
    pallas_call x1, Pallas kernels, depthwise_silu(): pl.pallas_call(depthwise_kernel, grid=(width // LANE_BLOCK,), in_specs=[p...  11 us
    all_to_all x1, starting transfers between devices, shards(): lax.all_to_all(summed, ('expert', 'z'), split_axis=0, concat_axis=0, tile...  10.6 us
    dot_general x2, matrix products, gated_unit(): projected = jnp.dot(normed, point_in, preferred_element_type=jnp.float32)  6.75 us
  transfers between devices with their start and end apart: 5, of which 3 were waited for; matrix products, arithmetic and copies ran while one was open for 4% of the time, Pallas kernels for 0%

profile of v8, /device:TPU:1, one launch (start us, length us, event | category | flops | bytes accessed | tf_op | source)
XLA Modules:
  0.0 247.3 jit_solution(11233597519819309413)
XLA Ops:
  6.5 0.0 copy-start
  6.5 0.0 all-gather.3.cloned.1.call-start
  6.5 1.6 slice_bitcast_fusion.1
  8.1 4.0 %collective-permute-start = (bf16[15,1024]{1,0:T(8,128)(2,1)}, bf16[15,1024]{1,0:T(8,128)(2,1)S(1)}, u32[]{:S(2)}, u32[]{:S(2)}) collective-permute-start(bf16[15,1024]{1,0:T(8,128)(2,1)} %get-tuple-element.7), channel_id=1, source_target_pairs={{0,8},{8,16},{16,24},{24,32},{32,40},{40,48},{48,56},{56,64},{64,7... | collective-permute-start | bytes 92168 | tf_op jit(solution)/shard_map/ppermute | solution.py:59
  12.1 1.3 collective-permute-start.1
  13.4 1.2 convert_reduce_fusion.1
  14.6 1.3 fusion.20
  16.0 0.0 copy-start.4
  16.0 0.0 copy-start.3
  16.0 3.7 %fusion.29 = f32[256,2048]{1,0:T(8,128)S(1)} fusion(bf16[1024,2048]{1,0:T(8,128)(2,1)} %param.14, bf16[1,256,1024]{2,1,0:T(8,128)(2,1)} %param.11, f32[256]{0:T(256)S(1)} %add_rsqrt_fusion.1, f32[256]{0:T(256)S(1)} %broadcast_multiply_fusion.1), kind=kOutput, calls=%fused_computation.36 | convolution fusion | flops 1074790400 | bytes 6817792 | tf_op jit(solution)/shard_map/dot_general | solution.py:69
  19.7 0.3 fusion.27
  20.0 0.0 copy-done.4
  20.0 0.1 copy.26
  20.1 0.1 reduce-window.10
  20.2 0.1 reduce.1
  20.3 0.1 select_reduce_fusion
  20.4 0.1 copy.28
  20.5 0.1 copy.29
  20.7 0.0 copy-done.3
  20.7 0.6 reduce-window.11
  21.3 0.2 slice_reduce_fusion
  21.5 0.0 copy-start.2
  21.5 0.7 fusion.43
  22.3 0.1 fusion.47
  22.4 0.0 collective-permute-done
  22.4 0.0 collective-permute-done.1
  22.4 0.1 convert_reduce_fusion.2
  22.5 0.2 fusion.37
  22.7 3.1 %fusion.48 = f32[30,2048]{1,0:T(8,128)S(1)} fusion(bf16[1024,2048]{1,0:T(8,128)(2,1)} %param.14, f32[30]{0:T(128)S(1)} %add_rsqrt_fusion.2, f32[30]{0:T(128)S(1)} %broadcast_multiply_fusion.2, bf16[15,1024]{1,0:T(8,128)(2,1)S(1)} %collective-permute-done.1, bf16[15,1024]{1,0:T(8,128)(2,1)S(1)} %collective-permute-done), kind=kOutput, calls=%fused_computation.60 | convolution fusion | flops 126044160 | bytes 4501744 | tf_op jit(solution)/shard_map/dot_general | solution.py:69
  25.9 1.0 pad_maximum_fusion.pad_ref
  26.8 11.0 %shard_map.109 = bf16[256,1024]{1,0:T(8,128)(2,1)} custom-call(bf16[286,1024]{1,0:T(8,128)(2,1)} %pad_maximum_fusion.pad_ref, f32[31,1024]{1,0:T(8,128)} %taps_ref.1, s32[256,1]{1,0:T(8,128)} %get-tuple-element.14.first_ref, s32[256,1]{1,0:T(8,128)} %get-tuple-element.13.last_ref, f32[1,1024]{1,0:T(1,128)} %bitcast.92, f32[1,1024]{1,0:T(1,128)} %bitcast.93), custom_call_target="tpu_custom_call" | custom-call | tf_op jit(solution)/shard_map/pallas_call | solution.py:35
  37.8 0.0 copy-done.2
  37.8 2.6 %convert_reduce_fusion = (f32[256]{0:T(256)S(1)}, bf16[256,1024]{1,0:T(8,128)(2,1)S(1)}) fusion(bf16[256,1024]{1,0:T(8,128)(2,1)} %shard_map.109, bf16[1024,1024]{1,0:T(8,128)(2,1)} %param.18, bf16[1,256,1024]{2,1,0:T(8,128)(2,1)S(1)} %copy-done.2), kind=kOutput, calls=%fused_computation.11 | convolution fusion | flops 538181376 | bytes 3671040 | tf_op jit(solution)/shard_map/dot_general | solution.py:133
  40.4 0.0 copy-start.1
  40.4 0.3 fusion.18
  40.7 2.8 %scatter_custom_fusion = bf16[512,1024]{1,0:T(8,128)(2,1)} fusion(s32[256]{0:T(256)S(1)} %bitcast.97, bf16[]{:T(256)} %constant.69.clone.1, bf16[256,1024]{1,0:T(8,128)(2,1)S(1)} %get-tuple-element.12, f32[256]{0:T(256)S(1)} %add_rsqrt_fusion, f32[256]{0:T(256)S(1)} %broadcast_multiply_fusion), kind=kCustom, calls=%fused_computation.37 | custom fusion | flops 1048576 | bytes 1574914 | tf_op jit(solution)/shard_map/scatter | solution.py:153
  43.6 45.0 %all_to_all.10 = bf16[64,8,1024]{2,1,0:T(8,128)(2,1)} all-to-all(bf16[64,8,1024]{2,1,0:T(8,128)(2,1)} %bitcast.87), channel_id=1, replica_groups=mesh['z'=8,'y'=4,'expert'=8] {'expert','z'}, dimensions={0} | all-to-all | bytes 2097152 | tf_op jit(solution)/shard_map/all_to_all | solution.py:158
  88.6 0.0 all-gather.3.cloned.1.call-update
  88.6 0.0 reduce-scatter.2.cloned.1.call-start
  88.6 46.0 %all-gather.3.cloned.1.call-done = bf16[256,8,1024]{2,1,0:T(8,128)(2,1)} async-done(((bf16[64,8,1024]{2,1,0:T(8,128)(2,1)}), bf16[256,8,1024]{2,1,0:T(8,128)(2,1)}) %all-gather.3.cloned.1.call-update) | async-done | bytes 4194320 | tf_op jit(solution)/shard_map/all_gather | solution.py:159
  134.6 0.0 copy-done
  134.6 13.0 %fusion.3 = bf16[2048,1024]{1,0:T(8,128)(2,1)} fusion(bf16[256,8,1024]{2,1,0:T(8,128)(2,1)} %all-gather.3.cloned.1.call-done, bf16[1,1,1024,1024]{3,2,1,0:T(8,128)(2,1)S(1)} %copy-done, bf16[1,1,1024,1024]{3,2,1,0:T(8,128)(2,1)} %param.20), kind=kOutput, calls=%fused_computation.6 | convolution fusion | flops 8602517504 | bytes 12582912 | tf_op jit(solution)/shard_map/dot_general | solution.py:87
  147.7 0.0 copy-done.1
  147.7 0.0 copy-start.5
  147.7 0.0 reduce-scatter.2.cloned.1.call-update
  147.7 49.9 %reduce-scatter.2.cloned.1.call-done = bf16[1,64,8,1024]{3,2,1,0:T(8,128)(2,1)} async-done(((bf16[4,64,8,1024]{3,2,1,0:T(8,128)(2,1)}), bf16[1,64,8,1024]{3,2,1,0:T(8,128)(2,1)}) %reduce-scatter.2.cloned.1.call-update) | async-done | bytes 1048592 | tf_op jit(solution)/shard_map/reduce_scatter | solution.py:161
  197.6 10.6 %all-to-all-start.1 = ((bf16[64,8,1024]{2,1,0:T(8,128)(2,1)}), bf16[64,8,1024]{2,1,0:T(8,128)(2,1)S(1)}, u32[]{:S(2)}, u32[]{:S(2)}) async-start(bf16[64,8,1024]{2,1,0:T(8,128)(2,1)} %bitcast.88), calls=%async_computation.2 | async-start | bytes 2097152 | tf_op jit(solution)/shard_map/all_to_all | solution.py:162
  208.2 0.0 copy-done.5
  208.3 1.4 fusion.17
  209.7 26.6 %all-to-all-done.1 = bf16[64,8,1024]{2,1,0:T(8,128)(2,1)S(1)} async-done(((bf16[64,8,1024]{2,1,0:T(8,128)(2,1)}), bf16[64,8,1024]{2,1,0:T(8,128)(2,1)S(1)}, u32[]{:S(2)}, u32[]{:S(2)}) %all-to-all-start.1) | async-done | bytes 1048608 | tf_op jit(solution)/shard_map/all_to_all | solution.py:162
  236.3 2.0 gather_fusion
  238.3 2.2 fusion.28
  (16 shorter events, 0.2 us)
Async XLA Ops:
  6.5 128.1 %copy-start = (bf16[1,1,1024,1024]{3,2,1,0:T(8,128)(2,1)S(1)}, bf16[1,1,1024,1024]{3,2,1,0:T(8,128)(2,1)}, u32[]{:S(2)}) copy-start(bf16[1,1,1024,1024]{3,2,1,0:T(8,128)(2,1)} %param.21) | copy-start | bytes 6291460
  6.5 128.1 %all-gather.3.cloned.1.call-start = ((), (), s32[]{:S(2)}) async-start(), calls=%async_computation.4 | async-start | bytes 5242880 | tf_op jit(solution)/shard_map/all_gather | solution.py:159
  8.1 14.3 %collective-permute-start = (bf16[15,1024]{1,0:T(8,128)(2,1)}, bf16[15,1024]{1,0:T(8,128)(2,1)S(1)}, u32[]{:S(2)}, u32[]{:S(2)}) collective-permute-start(bf16[15,1024]{1,0:T(8,128)(2,1)} %get-tuple-element.7), channel_id=1, source_target_pairs={{0,8},{8,16},{16,24},{24,32},{32,40},{40,48},{48,56},{56,64},{64,7... | collective-permute-start | bytes 92168 | tf_op jit(solution)/shard_map/ppermute | solution.py:59
  12.1 10.3 %collective-permute-start.1 = (bf16[15,1024]{1,0:T(8,128)(2,1)}, bf16[15,1024]{1,0:T(8,128)(2,1)S(1)}, u32[]{:S(2)}, u32[]{:S(2)}) collective-permute-start(bf16[15,1024]{1,0:T(8,128)(2,1)} %get-tuple-element.8), channel_id=1, source_target_pairs={{8,0},{16,8},{24,16},{32,24},{40,32},{48,40},{56,48},{64,56},{72,6... | collective-permute-start | bytes 92168 | tf_op jit(solution)/shard_map/ppermute | solution.py:60
  16.0 4.0 %copy-start.4 = (s32[1,32]{1,0:T(1,128)S(1)}, s32[1,32]{1,0:T(1,128)}, u32[]{:S(2)}) copy-start(s32[1,32]{1,0:T(1,128)} %param.12) | copy-start | bytes 388
  16.0 4.7 %copy-start.3 = (s32[1,256,1]{1,2,0:T(1,128)S(1)}, s32[1,256,1]{1,2,0:T(1,128)}, u32[]{:S(2)}) copy-start(s32[1,256,1]{1,2,0:T(1,128)} %param.13) | copy-start | bytes 3076
  21.5 16.3 %copy-start.2 = (bf16[1,256,1024]{2,1,0:T(8,128)(2,1)S(1)}, bf16[1,256,1024]{2,1,0:T(8,128)(2,1)}, u32[]{:S(2)}) copy-start(bf16[1,256,1024]{2,1,0:T(8,128)(2,1)} %param.11) | copy-start | bytes 1572868
  40.4 107.3 %copy-start.1 = (bf16[256,1024]{1,0:T(8,128)(2,1)}, bf16[256,1024]{1,0:T(8,128)(2,1)S(1)}, u32[]{:S(2)}) copy-start(bf16[256,1024]{1,0:T(8,128)(2,1)S(1)} %get-tuple-element.12) | copy-start | bytes 1572868
  88.6 109.0 %reduce-scatter.2.cloned.1.call-start = ((), (), s32[]{:S(2)}) async-start(), calls=%async_computation.3 | async-start | bytes 5242880 | tf_op jit(solution)/shard_map/reduce_scatter | solution.py:161
  147.7 60.6 %copy-start.5 = (bf16[1024,64]{0,1:T(8,128)(2,1)S(1)}, bf16[1024,64]{0,1:T(8,128)(2,1)}, u32[]{:S(2)}) copy-start(bf16[1024,64]{0,1:T(8,128)(2,1)} %param.19) | copy-start | bytes 393220
  197.6 38.7 %all-to-all-start.1 = ((bf16[64,8,1024]{2,1,0:T(8,128)(2,1)}), bf16[64,8,1024]{2,1,0:T(8,128)(2,1)S(1)}, u32[]{:S(2)}, u32[]{:S(2)}) async-start(bf16[64,8,1024]{2,1,0:T(8,128)(2,1)} %bitcast.88), calls=%async_computation.2 | async-start | bytes 2097152 | tf_op jit(solution)/shard_map/all_to_all | solution.py:162
Sparse Core Ops, SparseCore 0:
  88.7 45.8 all-gather.2
  147.8 49.7 reduce-scatter.1

commit v9 on v6

--- a/solution.py
+++ b/solution.py
@@ -6,24 +6,30 @@
 from jax.sharding import Mesh, PartitionSpec as P
 
 QUARTERS = 4
-ROW_BLOCK = 64
-LANE_BLOCK = 128
+ROW_BLOCK = 32
+LANE_BLOCK = 512
 
 
-def depthwise_kernel(pad_ref, taps_ref, first_ref, last_ref, scale_ref, shift_ref, out_ref, wide_ref):
+def depthwise_kernel(pad_ref, taps_ref, first_ref, last_ref, scale_ref, shift_ref, out_ref, shifted_ref):
     frame_count = out_ref.shape[0]
     tap_count = taps_ref.shape[0]
     half_span = (tap_count - 1) // 2
-    wide_ref[...] = pad_ref[...].astype(jnp.float32)
+    phases = 8
+    span = shifted_ref.shape[1]
+    for phase in range(phases):
+        count = min(span, pad_ref.shape[0] - phase)
+        shifted_ref[phase, :count, :] = pad_ref[phase : phase + count, :].astype(jnp.float32)
     for row in range(0, frame_count, ROW_BLOCK):
         first_rel = first_ref[row : row + ROW_BLOCK, :]
         last_rel = last_ref[row : row + ROW_BLOCK, :]
         acc = jnp.zeros((ROW_BLOCK, out_ref.shape[1]), jnp.float32)
         for tap in range(tap_count):
             offset = tap - half_span
+            phase, base = tap % phases, tap - tap % phases
+            window = shifted_ref[phase, row + base : row + base + ROW_BLOCK, :]
             valid = (first_rel <= offset) & (offset < last_rel)
-            window = wide_ref[row + tap : row + tap + ROW_BLOCK, :]
-            acc = acc + taps_ref[tap : tap + 1, :] * jnp.where(valid, window, 0.0)
+            window = jnp.where(valid, window, 0.0)
+            acc = acc + taps_ref[tap : tap + 1, :] * window
         value = acc * scale_ref[...] + shift_ref[...]
         out_ref[row : row + ROW_BLOCK, :] = (value * jax.nn.sigmoid(value)).astype(out_ref.dtype)
 
@@ -32,6 +38,7 @@
     rows, width = padded.shape
     tap_count = taps.shape[0]
     frame_count = rows - (tap_count - 1)
+    span = frame_count + 24
     return pl.pallas_call(
         depthwise_kernel,
         grid=(width // LANE_BLOCK,),
@@ -45,7 +52,7 @@
         ],
         out_specs=pl.BlockSpec((frame_count, LANE_BLOCK), lambda c: (0, c)),
         out_shape=jax.ShapeDtypeStruct((frame_count, width), jnp.bfloat16),
-        scratch_shapes=[pltpu.VMEM((rows, LANE_BLOCK), jnp.float32)],
+        scratch_shapes=[pltpu.VMEM((8, span, LANE_BLOCK), jnp.float32)],
     )(padded, taps, first_rel, last_rel, scale.reshape(1, -1), shift.reshape(1, -1))
 
 

time: 247 us -> 243 us (0.984)
  Pallas kernels: 11 us -> 7.35 us
    pallas_call x1, Pallas kernels: 11 us -> 7.35 us  [depthwise_silu(): pl.pallas_call(depthwise_kernel, grid=(width // LANE_BLOCK,), in_specs=[p...]
where the time goes in v9:
time: 243 us
  waiting for transfers between devices  126 us (52%)
  blocking collectives  43.2 us (18%)
  matrix products  20.7 us (9%)
  starting transfers between devices  16.7 us (7%)
  between operations  13.6 us (6%)
  other arithmetic  11.8 us (5%)
  Pallas kernels  7.35 us (3%)
  local copies, waits for them, and re-layouts  3.18 us (1%)
    reduce_scatter x1, waiting for transfers between devices, shards(): lax.psum_scatter(partial_out, 'y', scatter_dimension=0, tiled=False)  49.9 us
    all_gather x1, waiting for transfers between devices, shards(): gathered = lax.all_gather(by_member, 'y', axis=0, tiled=False)  48.2 us
    all_to_all x1, blocking collectives, shards(): lax.all_to_all(send_buffer, ('expert', 'z'), split_axis=0, concat_axis=0,...  43.2 us
    all_to_all x1, waiting for transfers between devices, shards(): lax.all_to_all(summed, ('expert', 'z'), split_axis=0, concat_axis=0, tile...  26.6 us
    dot_general x1, matrix products, expert_pass(): jnp.dot(hidden, w_out, preferred_element_type=jnp.float32)  13 us
    all_to_all x1, starting transfers between devices, shards(): lax.all_to_all(summed, ('expert', 'z'), split_axis=0, concat_axis=0, tile...  10.6 us
    pallas_call x1, Pallas kernels, depthwise_silu(): pl.pallas_call(depthwise_kernel, grid=(width // LANE_BLOCK,), in_specs=[p...  7.35 us
  transfers between devices with their start and end apart: 5, of which 4 were waited for; matrix products, arithmetic and copies ran while one was open for 2% of the time, Pallas kernels for 0%

profile of v9, /device:TPU:1, one launch (start us, length us, event | category | flops | bytes accessed | tf_op | source)
XLA Modules:
  0.0 242.6 jit_solution(17251052078869919172)
XLA Ops:
  6.5 0.0 copy-start
  6.5 0.0 all-gather.3.cloned.1.call-start
  6.5 1.3 convert_reduce_fusion.1
  7.9 1.3 fusion.20
  9.2 0.0 copy-start.4
  9.2 0.0 copy-start.3
  9.2 3.7 %fusion.29 = f32[256,2048]{1,0:T(8,128)S(1)} fusion(bf16[1024,2048]{1,0:T(8,128)(2,1)} %param.14, bf16[1,256,1024]{2,1,0:T(8,128)(2,1)} %param.11, f32[256]{0:T(256)S(1)} %add_rsqrt_fusion.1, f32[256]{0:T(256)S(1)} %broadcast_multiply_fusion.1), kind=kOutput, calls=%fused_computation.36 | convolution fusion | flops 1074790400 | bytes 6817792 | tf_op jit(solution)/shard_map/dot_general | solution.py:110
  13.0 0.0 copy-start.2
  13.0 0.3 fusion.27
  13.3 0.6 fusion.45
  13.9 4.6 %collective-permute-start = (bf16[15,1024]{1,0:T(8,128)(2,1)}, bf16[15,1024]{1,0:T(8,128)(2,1)}, u32[]{:S(2)}, u32[]{:S(2)}) collective-permute-start(bf16[15,1024]{1,0:T(8,128)(2,1)} %get-tuple-element.7), channel_id=1, source_target_pairs={{0,8},{8,16},{16,24},{24,32},{32,40},{40,48},{48,56},{56,64},{64,7... | collective-permute-start | bytes 92168 | tf_op jit(solution)/shard_map/ppermute | solution.py:67
  18.5 1.3 collective-permute-start.1
  19.8 0.0 copy-done.4
  19.8 0.1 copy.26
  19.9 0.1 reduce-window.10
  20.0 0.1 reduce.1
  20.1 0.1 select_reduce_fusion
  20.2 0.1 copy.28
  20.3 0.1 copy.29
  20.5 0.0 copy-done.3
  20.5 0.6 reduce-window.11
  21.1 0.2 slice_reduce_fusion
  21.4 0.7 fusion.35
  22.1 0.1 fusion.38
  22.2 0.0 collective-permute-done
  22.2 1.3 collective-permute-done.1
  23.5 1.7 pad_maximum_fusion.pad_ref
  25.2 7.4 %shard_map.109 = bf16[256,1024]{1,0:T(8,128)(2,1)} custom-call(bf16[286,1024]{1,0:T(8,128)(2,1)} %pad_maximum_fusion.pad_ref, f32[31,1024]{1,0:T(8,128)} %taps_ref.1, s32[256,1]{1,0:T(8,128)} %get-tuple-element.12.first_ref, s32[256,1]{1,0:T(8,128)} %get-tuple-element.11.last_ref, f32[1,1024]{1,0:T(1,128)} %bitcast.87, f32[1,1024]{1,0:T(1,128)} %bitcast.88), custom_call_target="tpu_custom_call" | custom-call | tf_op jit(solution)/shard_map/pallas_call | solution.py:42
  32.6 0.0 copy-done.2
  32.6 2.6 %convert_reduce_fusion = (f32[256]{0:T(256)S(1)}, bf16[256,1024]{1,0:T(8,128)(2,1)S(1)}) fusion(bf16[256,1024]{1,0:T(8,128)(2,1)} %shard_map.109, bf16[1024,1024]{1,0:T(8,128)(2,1)} %param.18, bf16[1,256,1024]{2,1,0:T(8,128)(2,1)S(1)} %copy-done.2), kind=kOutput, calls=%fused_computation.11 | convolution fusion | flops 538181376 | bytes 3671040 | tf_op jit(solution)/shard_map/dot_general | solution.py:134
  35.1 0.0 copy-start.1
  35.2 0.3 fusion.18
  35.4 2.8 %scatter_custom_fusion = bf16[512,1024]{1,0:T(8,128)(2,1)} fusion(s32[256]{0:T(256)S(1)} %bitcast.92, bf16[]{:T(256)} %constant.64.clone.1, bf16[256,1024]{1,0:T(8,128)(2,1)S(1)} %get-tuple-element.10, f32[256]{0:T(256)S(1)} %add_rsqrt_fusion, f32[256]{0:T(256)S(1)} %broadcast_multiply_fusion), kind=kCustom, calls=%fused_computation.37 | custom fusion | flops 1048576 | bytes 1574914 | tf_op jit(solution)/shard_map/scatter | solution.py:154
  38.3 43.2 %all_to_all.10 = bf16[64,8,1024]{2,1,0:T(8,128)(2,1)} all-to-all(bf16[64,8,1024]{2,1,0:T(8,128)(2,1)} %bitcast.82), channel_id=1, replica_groups=mesh['z'=8,'y'=4,'expert'=8] {'expert','z'}, dimensions={0} | all-to-all | bytes 2097152 | tf_op jit(solution)/shard_map/all_to_all | solution.py:159
  81.5 0.0 all-gather.3.cloned.1.call-update
  81.5 0.2 reduce-scatter.2.cloned.1.call-start
  81.7 48.2 %all-gather.3.cloned.1.call-done = bf16[256,8,1024]{2,1,0:T(8,128)(2,1)} async-done(((bf16[64,8,1024]{2,1,0:T(8,128)(2,1)}), bf16[256,8,1024]{2,1,0:T(8,128)(2,1)}) %all-gather.3.cloned.1.call-update) | async-done | bytes 4194320 | tf_op jit(solution)/shard_map/all_gather | solution.py:160
  129.9 0.0 copy-done
  129.9 13.0 %fusion.3 = bf16[2048,1024]{1,0:T(8,128)(2,1)} fusion(bf16[256,8,1024]{2,1,0:T(8,128)(2,1)} %all-gather.3.cloned.1.call-done, bf16[1,1,1024,1024]{3,2,1,0:T(8,128)(2,1)S(1)} %copy-done, bf16[1,1,1024,1024]{3,2,1,0:T(8,128)(2,1)} %param.20), kind=kOutput, calls=%fused_computation.6 | convolution fusion | flops 8602517504 | bytes 12582912 | tf_op jit(solution)/shard_map/dot_general | solution.py:88
  143.0 0.0 copy-done.1
  143.0 0.0 copy-start.5
  143.0 0.0 reduce-scatter.2.cloned.1.call-update
  143.0 49.9 %reduce-scatter.2.cloned.1.call-done = bf16[1,64,8,1024]{3,2,1,0:T(8,128)(2,1)} async-done(((bf16[4,64,8,1024]{3,2,1,0:T(8,128)(2,1)}), bf16[1,64,8,1024]{3,2,1,0:T(8,128)(2,1)}) %reduce-scatter.2.cloned.1.call-update) | async-done | bytes 1048592 | tf_op jit(solution)/shard_map/reduce_scatter | solution.py:162
  192.9 10.6 %all-to-all-start.1 = ((bf16[64,8,1024]{2,1,0:T(8,128)(2,1)}), bf16[64,8,1024]{2,1,0:T(8,128)(2,1)S(1)}, u32[]{:S(2)}, u32[]{:S(2)}) async-start(bf16[64,8,1024]{2,1,0:T(8,128)(2,1)} %bitcast.83), calls=%async_computation.2 | async-start | bytes 2097152 | tf_op jit(solution)/shard_map/all_to_all | solution.py:163
  203.6 0.0 copy-done.5
  203.6 1.4 fusion.17
  205.0 26.6 %all-to-all-done.1 = bf16[64,8,1024]{2,1,0:T(8,128)(2,1)S(1)} async-done(((bf16[64,8,1024]{2,1,0:T(8,128)(2,1)}), bf16[64,8,1024]{2,1,0:T(8,128)(2,1)S(1)}, u32[]{:S(2)}, u32[]{:S(2)}) %all-to-all-start.1) | async-done | bytes 1048608 | tf_op jit(solution)/shard_map/all_to_all | solution.py:163
  231.6 2.0 gather_fusion
  233.6 2.2 fusion.28
  (12 shorter events, 0.1 us)
Async XLA Ops:
  6.5 123.4 %copy-start = (bf16[1,1,1024,1024]{3,2,1,0:T(8,128)(2,1)S(1)}, bf16[1,1,1024,1024]{3,2,1,0:T(8,128)(2,1)}, u32[]{:S(2)}) copy-start(bf16[1,1,1024,1024]{3,2,1,0:T(8,128)(2,1)} %param.21) | copy-start | bytes 6291460
  6.5 123.4 %all-gather.3.cloned.1.call-start = ((), (), s32[]{:S(2)}) async-start(), calls=%async_computation.4 | async-start | bytes 5242880 | tf_op jit(solution)/shard_map/all_gather | solution.py:160
  9.2 10.6 %copy-start.4 = (s32[1,32]{1,0:T(1,128)S(1)}, s32[1,32]{1,0:T(1,128)}, u32[]{:S(2)}) copy-start(s32[1,32]{1,0:T(1,128)} %param.12) | copy-start | bytes 388
  9.2 11.3 %copy-start.3 = (s32[1,256,1]{1,2,0:T(1,128)S(1)}, s32[1,256,1]{1,2,0:T(1,128)}, u32[]{:S(2)}) copy-start(s32[1,256,1]{1,2,0:T(1,128)} %param.13) | copy-start | bytes 3076
  13.0 19.6 %copy-start.2 = (bf16[1,256,1024]{2,1,0:T(8,128)(2,1)S(1)}, bf16[1,256,1024]{2,1,0:T(8,128)(2,1)}, u32[]{:S(2)}) copy-start(bf16[1,256,1024]{2,1,0:T(8,128)(2,1)} %param.11) | copy-start | bytes 1572868
  13.9 8.3 %collective-permute-start = (bf16[15,1024]{1,0:T(8,128)(2,1)}, bf16[15,1024]{1,0:T(8,128)(2,1)}, u32[]{:S(2)}, u32[]{:S(2)}) collective-permute-start(bf16[15,1024]{1,0:T(8,128)(2,1)} %get-tuple-element.7), channel_id=1, source_target_pairs={{0,8},{8,16},{16,24},{24,32},{32,40},{40,48},{48,56},{56,64},{64,7... | collective-permute-start | bytes 92168 | tf_op jit(solution)/shard_map/ppermute | solution.py:67
  18.5 5.0 %collective-permute-start.1 = (bf16[15,1024]{1,0:T(8,128)(2,1)}, bf16[15,1024]{1,0:T(8,128)(2,1)}, u32[]{:S(2)}, u32[]{:S(2)}) collective-permute-start(bf16[15,1024]{1,0:T(8,128)(2,1)} %get-tuple-element.8), channel_id=1, source_target_pairs={{8,0},{16,8},{24,16},{32,24},{40,32},{48,40},{56,48},{64,56},{72,6... | collective-permute-start | bytes 92168 | tf_op jit(solution)/shard_map/ppermute | solution.py:69
  35.1 107.8 %copy-start.1 = (bf16[256,1024]{1,0:T(8,128)(2,1)}, bf16[256,1024]{1,0:T(8,128)(2,1)S(1)}, u32[]{:S(2)}) copy-start(bf16[256,1024]{1,0:T(8,128)(2,1)S(1)} %get-tuple-element.10) | copy-start | bytes 1572868
  81.5 111.5 %reduce-scatter.2.cloned.1.call-start = ((), (), s32[]{:S(2)}) async-start(), calls=%async_computation.3 | async-start | bytes 5242880 | tf_op jit(solution)/shard_map/reduce_scatter | solution.py:162
  143.0 60.6 %copy-start.5 = (bf16[1024,64]{0,1:T(8,128)(2,1)S(1)}, bf16[1024,64]{0,1:T(8,128)(2,1)}, u32[]{:S(2)}) copy-start(bf16[1024,64]{0,1:T(8,128)(2,1)} %param.19) | copy-start | bytes 393220
  192.9 38.7 %all-to-all-start.1 = ((bf16[64,8,1024]{2,1,0:T(8,128)(2,1)}), bf16[64,8,1024]{2,1,0:T(8,128)(2,1)S(1)}, u32[]{:S(2)}, u32[]{:S(2)}) async-start(bf16[64,8,1024]{2,1,0:T(8,128)(2,1)} %bitcast.83), calls=%async_computation.2 | async-start | bytes 2097152 | tf_op jit(solution)/shard_map/all_to_all | solution.py:163
Sparse Core Ops, SparseCore 0:
  81.6 48.2 all-gather.2
  143.1 49.7 reduce-scatter.1

commit v10 on v9

--- a/solution.py
+++ b/solution.py
@@ -10,15 +10,30 @@
 LANE_BLOCK = 512
 
 
-def depthwise_kernel(pad_ref, taps_ref, first_ref, last_ref, scale_ref, shift_ref, out_ref, shifted_ref):
+def depthwise_kernel(
+    gated_ref,
+    before_ref,
+    after_ref,
+    taps_ref,
+    first_ref,
+    last_ref,
+    scale_ref,
+    shift_ref,
+    out_ref,
+    wide_ref,
+    shifted_ref,
+):
     frame_count = out_ref.shape[0]
     tap_count = taps_ref.shape[0]
     half_span = (tap_count - 1) // 2
     phases = 8
     span = shifted_ref.shape[1]
+    wide_ref[:half_span, :] = before_ref[...].astype(jnp.float32)
+    wide_ref[half_span : half_span + frame_count, :] = gated_ref[...].astype(jnp.float32)
+    wide_ref[half_span + frame_count :, :] = after_ref[...].astype(jnp.float32)
     for phase in range(phases):
-        count = min(span, pad_ref.shape[0] - phase)
-        shifted_ref[phase, :count, :] = pad_ref[phase : phase + count, :].astype(jnp.float32)
+        count = min(span, wide_ref.shape[0] - phase)
+        shifted_ref[phase, :count, :] = wide_ref[phase : phase + count, :]
     for row in range(0, frame_count, ROW_BLOCK):
         first_rel = first_ref[row : row + ROW_BLOCK, :]
         last_rel = last_ref[row : row + ROW_BLOCK, :]
@@ -34,16 +49,19 @@
         out_ref[row : row + ROW_BLOCK, :] = (value * jax.nn.sigmoid(value)).astype(out_ref.dtype)
 
 
-def depthwise_silu(padded, taps, first_rel, last_rel, scale, shift):
-    rows, width = padded.shape
+def depthwise_silu(gated, before, after, taps, first_rel, last_rel, scale, shift):
+    frame_count, width = gated.shape
     tap_count = taps.shape[0]
-    frame_count = rows - (tap_count - 1)
+    half_span = (tap_count - 1) // 2
+    rows = frame_count + 2 * half_span
     span = frame_count + 24
     return pl.pallas_call(
         depthwise_kernel,
         grid=(width // LANE_BLOCK,),
         in_specs=[
-            pl.BlockSpec((rows, LANE_BLOCK), lambda c: (0, c)),
+            pl.BlockSpec((frame_count, LANE_BLOCK), lambda c: (0, c)),
+            pl.BlockSpec((half_span, LANE_BLOCK), lambda c: (0, c)),
+            pl.BlockSpec((half_span, LANE_BLOCK), lambda c: (0, c)),
             pl.BlockSpec((tap_count, LANE_BLOCK), lambda c: (0, c)),
             pl.BlockSpec((frame_count, 1), lambda c: (0, 0)),
             pl.BlockSpec((frame_count, 1), lambda c: (0, 0)),
@@ -52,25 +70,21 @@
         ],
         out_specs=pl.BlockSpec((frame_count, LANE_BLOCK), lambda c: (0, c)),
         out_shape=jax.ShapeDtypeStruct((frame_count, width), jnp.bfloat16),
-        scratch_shapes=[pltpu.VMEM((8, span, LANE_BLOCK), jnp.float32)],
-    )(padded, taps, first_rel, last_rel, scale.reshape(1, -1), shift.reshape(1, -1))
-
-
-def padded_2(cells, sides, width):
-    for axis, dim in sides:
-        count = lax.axis_size(axis)
-        ends = count - 1
-        head = lax.slice_in_dim(cells, 0, width, axis=dim)
-        tail = lax.slice_in_dim(cells, cells.shape[dim] - width, cells.shape[dim], axis=dim)
-        cells = jnp.concatenate(
-            [
-                lax.ppermute(tail, axis, [(i, (i + 1) % count) for i in range(ends)]),
-                cells,
-                lax.ppermute(head, axis, [((i + 1) % count, i) for i in range(ends)]),
-            ],
-            axis=dim,
-        )
-    return cells
+        scratch_shapes=[
+            pltpu.VMEM((rows, LANE_BLOCK), jnp.float32),
+            pltpu.VMEM((8, span, LANE_BLOCK), jnp.float32),
+        ],
+    )(gated, before, after, taps, first_rel, last_rel, scale.reshape(1, -1), shift.reshape(1, -1))
+
+
+def halo_pair(cells, axis, width):
+    count = lax.axis_size(axis)
+    ends = count - 1
+    head = cells[:width]
+    tail = cells[cells.shape[0] - width :]
+    before = lax.ppermute(tail, axis, [(i, (i + 1) % count) for i in range(ends)])
+    after = lax.ppermute(head, axis, [((i + 1) % count, i) for i in range(ends)])
+    return before, after
 
 
 def layer_norm(values):
@@ -111,7 +125,7 @@
     gated_act = (projected[:, :model_width] * jax.nn.sigmoid(projected[:, model_width:])).astype(
         jnp.bfloat16
     )
-    padded = padded_2(gated_act, ((("z", "y"), 0),), half_span)
+    before, after = halo_pair(gated_act, ("z", "y"), half_span)
     lengths = utt_lengths[0]
     utter_ends = jnp.cumsum(lengths, dtype=jnp.int32)
     utter_starts = utter_ends - lengths
@@ -122,7 +136,9 @@
     first_pos = jnp.sum(jnp.where(inside, utter_starts[None, :], 0), axis=1, dtype=jnp.int32)
     last_pos = jnp.sum(jnp.where(inside, utter_ends[None, :], 0), axis=1, dtype=jnp.int32)
     activated = depthwise_silu(
-        padded,
+        gated_act,
+        before,
+        after,
         depth_taps,
         (first_pos - position)[:, None],
         (last_pos - position)[:, None],

time: 243 us -> 242 us (level)
  no operation moved by 1% of the time
where the time goes in v10:
time: 242 us; the launch traced here: 241 us
  waiting for transfers between devices  126 us (52%)
  blocking collectives  43.2 us (18%)
  matrix products  20.7 us (9%)
  starting transfers between devices  16.8 us (7%)
  between operations  13.6 us (6%)
  other arithmetic  10.1 us (4%)
  Pallas kernels  7.55 us (3%)
  local copies, waits for them, and re-layouts  3.25 us (1%)
    reduce_scatter x1, waiting for transfers between devices, shards(): lax.psum_scatter(partial_out, 'y', scatter_dimension=0, tiled=False)  49.9 us
    all_gather x1, waiting for transfers between devices, shards(): gathered = lax.all_gather(by_member, 'y', axis=0, tiled=False)  48.2 us
    all_to_all x1, blocking collectives, shards(): lax.all_to_all(send_buffer, ('expert', 'z'), split_axis=0, concat_axis=0,...  43.2 us
    all_to_all x1, waiting for transfers between devices, shards(): lax.all_to_all(summed, ('expert', 'z'), split_axis=0, concat_axis=0, tile...  26.6 us
    dot_general x1, matrix products, expert_pass(): jnp.dot(hidden, w_out, preferred_element_type=jnp.float32)  13 us
    all_to_all x1, starting transfers between devices, shards(): lax.all_to_all(summed, ('expert', 'z'), split_axis=0, concat_axis=0, tile...  10.6 us
    pallas_call x1, Pallas kernels, depthwise_silu(): pl.pallas_call(depthwise_kernel, grid=(width // LANE_BLOCK,), in_specs=[p...  7.55 us
  transfers between devices with their start and end apart: 5, of which 4 were waited for; matrix products, arithmetic and copies ran while one was open for 2% of the time, Pallas kernels for 0%

profile of v10, /device:TPU:1, one launch (start us, length us, event | category | flops | bytes accessed | tf_op | source)
XLA Modules:
  0.0 241.2 jit_solution(13529042209160337040)
XLA Ops:
  6.5 0.0 copy-start
  6.5 0.0 all-gather.3.cloned.1.call-start
  6.5 1.3 convert_reduce_fusion.1
  7.9 1.3 fusion.20
  9.2 0.0 copy-start.5
  9.2 0.0 copy-start.4
  9.2 3.7 %fusion.29 = f32[256,2048]{1,0:T(8,128)S(1)} fusion(bf16[1024,2048]{1,0:T(8,128)(2,1)} %param.14, bf16[1,256,1024]{2,1,0:T(8,128)(2,1)} %param.11, f32[256]{0:T(256)S(1)} %add_rsqrt_fusion.1, f32[256]{0:T(256)S(1)} %broadcast_multiply_fusion.1), kind=kOutput, calls=%fused_computation.35 | convolution fusion | flops 1074790400 | bytes 6817792 | tf_op jit(solution)/shard_map/dot_general | solution.py:124
  13.0 0.0 copy-start.3
  13.0 0.3 fusion.27.gated_ref
  13.3 0.0 copy-start.2
  13.3 0.7 fusion.45
  14.0 4.6 %collective-permute-start = (bf16[15,1024]{1,0:T(8,128)(2,1)}, bf16[15,1024]{1,0:T(8,128)(2,1)}, u32[]{:S(2)}, u32[]{:S(2)}) collective-permute-start(bf16[15,1024]{1,0:T(8,128)(2,1)} %get-tuple-element.8), channel_id=1, source_target_pairs={{0,8},{8,16},{16,24},{24,32},{32,40},{40,48},{48,56},{56,64},{64,7... | collective-permute-start | bytes 92168 | tf_op jit(solution)/shard_map/ppermute | solution.py:85
  18.6 1.3 collective-permute-start.1
  19.9 0.0 copy-done.5
  19.9 0.1 copy.26
  20.0 0.1 reduce-window.10
  20.0 0.1 reduce.1
  20.2 0.1 select_reduce_fusion
  20.3 0.1 copy.28
  20.4 0.1 copy.29
  20.6 0.0 copy-done.4
  20.6 0.6 reduce-window.11
  21.2 0.2 slice_reduce_fusion
  21.4 0.7 fusion.35
  22.2 0.1 fusion.38
  22.3 0.0 collective-permute-done.before_ref
  22.3 1.3 collective-permute-done.1.after_ref
  23.6 0.0 copy-done.2
  23.6 7.5 %shard_map.109 = bf16[256,1024]{1,0:T(8,128)(2,1)} custom-call(bf16[256,1024]{1,0:T(8,128)(2,1)} %copy-done.2, bf16[15,1024]{1,0:T(8,128)(2,1)} %collective-permute-done.before_ref, bf16[15,1024]{1,0:T(8,128)(2,1)} %collective-permute-done.1.after_ref, f32[31,1024]{1,0:T(8,128)} %taps_ref.1, s32[256,1]{1,0:T(8,128)} %get-tuple-element.12.first_ref, ...), custom_call_target="tpu_custom_call" | custom-call | tf_op jit(solution)/shard_map/pallas_call | solution.py:58
  31.1 0.0 copy-done.3
  31.1 2.6 %convert_reduce_fusion = (f32[256]{0:T(256)S(1)}, bf16[256,1024]{1,0:T(8,128)(2,1)S(1)}) fusion(bf16[256,1024]{1,0:T(8,128)(2,1)} %shard_map.109, bf16[1024,1024]{1,0:T(8,128)(2,1)} %param.18, bf16[1,256,1024]{2,1,0:T(8,128)(2,1)S(1)} %copy-done.3), kind=kOutput, calls=%fused_computation.11 | convolution fusion | flops 538181376 | bytes 3671040 | tf_op jit(solution)/shard_map/dot_general | solution.py:150
  33.7 0.0 copy-start.1
  33.7 0.3 fusion.18
  34.0 2.8 %scatter_custom_fusion = bf16[512,1024]{1,0:T(8,128)(2,1)} fusion(s32[256]{0:T(256)S(1)} %bitcast.92, bf16[]{:T(256)} %constant.64.clone.1, bf16[256,1024]{1,0:T(8,128)(2,1)S(1)} %get-tuple-element.10, f32[256]{0:T(256)S(1)} %add_rsqrt_fusion, f32[256]{0:T(256)S(1)} %broadcast_multiply_fusion), kind=kCustom, calls=%fused_computation.36 | custom fusion | flops 1048576 | bytes 1574914 | tf_op jit(solution)/shard_map/scatter | solution.py:170
  36.8 43.2 %all_to_all.10 = bf16[64,8,1024]{2,1,0:T(8,128)(2,1)} all-to-all(bf16[64,8,1024]{2,1,0:T(8,128)(2,1)} %bitcast.82), channel_id=1, replica_groups=mesh['z'=8,'y'=4,'expert'=8] {'expert','z'}, dimensions={0} | all-to-all | bytes 2097152 | tf_op jit(solution)/shard_map/all_to_all | solution.py:175
  80.0 0.0 all-gather.3.cloned.1.call-update
  80.1 0.2 reduce-scatter.2.cloned.1.call-start
  80.3 48.2 %all-gather.3.cloned.1.call-done = bf16[256,8,1024]{2,1,0:T(8,128)(2,1)} async-done(((bf16[64,8,1024]{2,1,0:T(8,128)(2,1)}), bf16[256,8,1024]{2,1,0:T(8,128)(2,1)}) %all-gather.3.cloned.1.call-update) | async-done | bytes 4194320 | tf_op jit(solution)/shard_map/all_gather | solution.py:176
  128.5 0.0 copy-done
  128.5 13.0 %fusion.3 = bf16[2048,1024]{1,0:T(8,128)(2,1)} fusion(bf16[256,8,1024]{2,1,0:T(8,128)(2,1)} %all-gather.3.cloned.1.call-done, bf16[1,1,1024,1024]{3,2,1,0:T(8,128)(2,1)S(1)} %copy-done, bf16[1,1,1024,1024]{3,2,1,0:T(8,128)(2,1)} %param.20), kind=kOutput, calls=%fused_computation.6 | convolution fusion | flops 8602517504 | bytes 12582912 | tf_op jit(solution)/shard_map/dot_general | solution.py:102
  141.5 0.0 copy-done.1
  141.5 0.0 copy-start.6
  141.5 0.0 reduce-scatter.2.cloned.1.call-update
  141.6 49.9 %reduce-scatter.2.cloned.1.call-done = bf16[1,64,8,1024]{3,2,1,0:T(8,128)(2,1)} async-done(((bf16[4,64,8,1024]{3,2,1,0:T(8,128)(2,1)}), bf16[1,64,8,1024]{3,2,1,0:T(8,128)(2,1)}) %reduce-scatter.2.cloned.1.call-update) | async-done | bytes 1048592 | tf_op jit(solution)/shard_map/reduce_scatter | solution.py:178
  191.5 10.6 %all-to-all-start.1 = ((bf16[64,8,1024]{2,1,0:T(8,128)(2,1)}), bf16[64,8,1024]{2,1,0:T(8,128)(2,1)S(1)}, u32[]{:S(2)}, u32[]{:S(2)}) async-start(bf16[64,8,1024]{2,1,0:T(8,128)(2,1)} %bitcast.83), calls=%async_computation.2 | async-start | bytes 2097152 | tf_op jit(solution)/shard_map/all_to_all | solution.py:179
  202.1 0.0 copy-done.6
  202.1 1.4 fusion.17
  203.6 26.6 %all-to-all-done.1 = bf16[64,8,1024]{2,1,0:T(8,128)(2,1)S(1)} async-done(((bf16[64,8,1024]{2,1,0:T(8,128)(2,1)}), bf16[64,8,1024]{2,1,0:T(8,128)(2,1)S(1)}, u32[]{:S(2)}, u32[]{:S(2)}) %all-to-all-start.1) | async-done | bytes 1048608 | tf_op jit(solution)/shard_map/all_to_all | solution.py:179
  230.2 2.0 gather_fusion
  232.2 2.2 fusion.28
  (12 shorter events, 0.1 us)
Async XLA Ops:
  6.5 121.9 %copy-start = (bf16[1,1,1024,1024]{3,2,1,0:T(8,128)(2,1)S(1)}, bf16[1,1,1024,1024]{3,2,1,0:T(8,128)(2,1)}, u32[]{:S(2)}) copy-start(bf16[1,1,1024,1024]{3,2,1,0:T(8,128)(2,1)} %param.21) | copy-start | bytes 6291460
  6.5 121.9 %all-gather.3.cloned.1.call-start = ((), (), s32[]{:S(2)}) async-start(), calls=%async_computation.4 | async-start | bytes 5242880 | tf_op jit(solution)/shard_map/all_gather | solution.py:176
  9.2 10.7 %copy-start.5 = (s32[1,32]{1,0:T(1,128)S(1)}, s32[1,32]{1,0:T(1,128)}, u32[]{:S(2)}) copy-start(s32[1,32]{1,0:T(1,128)} %param.12) | copy-start | bytes 388
  9.2 11.3 %copy-start.4 = (s32[1,256,1]{1,2,0:T(1,128)S(1)}, s32[1,256,1]{1,2,0:T(1,128)}, u32[]{:S(2)}) copy-start(s32[1,256,1]{1,2,0:T(1,128)} %param.13) | copy-start | bytes 3076
  13.0 18.1 %copy-start.3 = (bf16[1,256,1024]{2,1,0:T(8,128)(2,1)S(1)}, bf16[1,256,1024]{2,1,0:T(8,128)(2,1)}, u32[]{:S(2)}) copy-start(bf16[1,256,1024]{2,1,0:T(8,128)(2,1)} %param.11) | copy-start | bytes 1572868
  13.3 10.3 %copy-start.2 = (bf16[256,1024]{1,0:T(8,128)(2,1)}, bf16[256,1024]{1,0:T(8,128)(2,1)S(1)}, u32[]{:S(2)}) copy-start(bf16[256,1024]{1,0:T(8,128)(2,1)S(1)} %fusion.27.gated_ref) | copy-start | bytes 1572868
  14.0 8.3 %collective-permute-start = (bf16[15,1024]{1,0:T(8,128)(2,1)}, bf16[15,1024]{1,0:T(8,128)(2,1)}, u32[]{:S(2)}, u32[]{:S(2)}) collective-permute-start(bf16[15,1024]{1,0:T(8,128)(2,1)} %get-tuple-element.8), channel_id=1, source_target_pairs={{0,8},{8,16},{16,24},{24,32},{32,40},{40,48},{48,56},{56,64},{64,7... | collective-permute-start | bytes 92168 | tf_op jit(solution)/shard_map/ppermute | solution.py:85
  18.6 5.0 %collective-permute-start.1 = (bf16[15,1024]{1,0:T(8,128)(2,1)}, bf16[15,1024]{1,0:T(8,128)(2,1)}, u32[]{:S(2)}, u32[]{:S(2)}) collective-permute-start(bf16[15,1024]{1,0:T(8,128)(2,1)} %get-tuple-element.7), channel_id=1, source_target_pairs={{8,0},{16,8},{24,16},{32,24},{40,32},{48,40},{56,48},{64,56},{72,6... | collective-permute-start | bytes 92168 | tf_op jit(solution)/shard_map/ppermute | solution.py:86
  33.7 107.9 %copy-start.1 = (bf16[256,1024]{1,0:T(8,128)(2,1)}, bf16[256,1024]{1,0:T(8,128)(2,1)S(1)}, u32[]{:S(2)}) copy-start(bf16[256,1024]{1,0:T(8,128)(2,1)S(1)} %get-tuple-element.10) | copy-start | bytes 1572868
  80.1 111.4 %reduce-scatter.2.cloned.1.call-start = ((), (), s32[]{:S(2)}) async-start(), calls=%async_computation.3 | async-start | bytes 5242880 | tf_op jit(solution)/shard_map/reduce_scatter | solution.py:178
  141.5 60.6 %copy-start.6 = (bf16[1024,64]{0,1:T(8,128)(2,1)S(1)}, bf16[1024,64]{0,1:T(8,128)(2,1)}, u32[]{:S(2)}) copy-start(bf16[1024,64]{0,1:T(8,128)(2,1)} %param.19) | copy-start | bytes 393220
  191.5 38.7 %all-to-all-start.1 = ((bf16[64,8,1024]{2,1,0:T(8,128)(2,1)}), bf16[64,8,1024]{2,1,0:T(8,128)(2,1)S(1)}, u32[]{:S(2)}, u32[]{:S(2)}) async-start(bf16[64,8,1024]{2,1,0:T(8,128)(2,1)} %bitcast.83), calls=%async_computation.2 | async-start | bytes 2097152 | tf_op jit(solution)/shard_map/all_to_all | solution.py:179
Sparse Core Ops, SparseCore 0:
  80.2 48.2 all-gather.2
  141.7 49.7 reduce-scatter.1

commit v11 on v10

--- a/solution.py
+++ b/solution.py
@@ -164,11 +164,13 @@
     owner_group = route_ids // per_owner
     member = route_ids % per_owner
     slot_index = (owner_group * per_owner + member) * capacity + rank_in
-    send_buffer = (
-        jnp.zeros((per_owner * owners * capacity, model_width), jnp.bfloat16)
-        .at[slot_index]
-        .set(moe_in)
-    )
+    slot_count = per_owner * owners * capacity
+    placing = (slot_index[:, None] == jnp.arange(slot_count, dtype=jnp.int32)[None, :]).astype(
+        jnp.bfloat16
+    )
+    send_buffer = lax.dot_general(
+        placing, moe_in, (((0,), (0,)), ((), ())), preferred_element_type=jnp.float32
+    ).astype(jnp.bfloat16)
     send_buffer = send_buffer.reshape(owners * per_owner, capacity, model_width)
     w_in = expert_in[0, 0]
     w_out = expert_out[0, 0]
@@ -177,7 +179,9 @@
     partial_out = expert_pass(gathered, w_in, w_out)
     summed = lax.psum_scatter(partial_out, "y", scatter_dimension=0, tiled=False)
     results = lax.all_to_all(summed, ("expert", "z"), split_axis=0, concat_axis=0, tiled=True)
-    frame_moe = results.reshape(-1, model_width)[slot_index]
+    frame_moe = jnp.dot(
+        placing, results.reshape(-1, model_width), preferred_element_type=jnp.float32
+    )
     layer_out = mixed_res.astype(jnp.float32) + gate_value[:, None] * frame_moe.astype(jnp.float32)
     return layer_out.astype(jnp.bfloat16)[None]
 

time: 242 us -> 238 us (0.983)
  other arithmetic: 10.1 us -> 5.04 us
  blocking collectives: 43.2 us -> 46.4 us
    all_to_all x1, blocking collectives: 43.2 us -> 46.4 us  [shards(): lax.all_to_all(send_buffer, ('expert', 'z'), split_axis=0, concat_axis=0,...]
    dot_general x0 -> x2, matrix products: none -> 3.13 us  [the longest x1 2.51 us: shards(): jnp.dot(placing, results.reshape(-1, model_width), preferred_element_type...]
    scatter x1 -> x0, other arithmetic: 2.84 us -> none  [shards(): send_buffer = jnp.zeros((per_owner * owners * capacity, model_width), jnp...]
  transfers between devices with their start and end apart: 5 -> 5, of which waited for: 4 -> 3; matrix products, arithmetic and copies ran while one was open for 2% -> 1% of each run, Pallas kernels for 0% -> 0%
where the time goes in v11:
time: 238 us
  waiting for transfers between devices  124 us (52%)
  blocking collectives  46.4 us (19%)
  matrix products  22.8 us (10%)
  starting transfers between devices  16.8 us (7%)
  between operations  13.6 us (6%)
  Pallas kernels  7.54 us (3%)
  other arithmetic  5.04 us (2%)
    reduce_scatter x1, waiting for transfers between devices, shards(): lax.psum_scatter(partial_out, 'y', scatter_dimension=0, tiled=False)  49.9 us
    all_to_all x1, blocking collectives, shards(): lax.all_to_all(send_buffer, ('expert', 'z'), split_axis=0, concat_axis=0,...  46.4 us
    all_gather x1, waiting for transfers between devices, shards(): gathered = lax.all_gather(by_member, 'y', axis=0, tiled=False)  46 us
    all_to_all x1, waiting for transfers between devices, shards(): lax.all_to_all(summed, ('expert', 'z'), split_axis=0, concat_axis=0, tile...  27.6 us
    dot_general x1, matrix products, expert_pass(): jnp.dot(hidden, w_out, preferred_element_type=jnp.float32)  13.1 us
    all_to_all x1, starting transfers between devices, shards(): lax.all_to_all(summed, ('expert', 'z'), split_axis=0, concat_axis=0, tile...  10.8 us
    pallas_call x1, Pallas kernels, depthwise_silu(): pl.pallas_call(depthwise_kernel, grid=(width // LANE_BLOCK,), in_specs=[p...  7.54 us
  transfers between devices with their start and end apart: 5, of which 3 were waited for; matrix products, arithmetic and copies ran while one was open for 1% of the time, Pallas kernels for 0%

profile of v11, /device:TPU:1, one launch (start us, length us, event | category | flops | bytes accessed | tf_op | source)
XLA Modules:
  0.0 237.6 jit_solution(3963463945004671961)
XLA Ops:
  6.5 0.0 copy-start
  6.5 0.0 all-gather.3.cloned.1.call-start
  6.5 1.3 convert_reduce_fusion.1
  7.9 1.3 fusion.23
  9.2 0.0 copy-start.6
  9.2 0.0 copy-start.5
  9.2 3.7 %fusion.31 = f32[256,2048]{1,0:T(8,128)S(1)} fusion(bf16[1024,2048]{1,0:T(8,128)(2,1)} %param.14, bf16[1,256,1024]{2,1,0:T(8,128)(2,1)} %param.11, f32[256]{0:T(256)S(1)} %add_rsqrt_fusion.1, f32[256]{0:T(256)S(1)} %broadcast_multiply_fusion.1), kind=kOutput, calls=%fused_computation.37 | convolution fusion | flops 1074790400 | bytes 6817792 | tf_op jit(solution)/shard_map/dot_general | solution.py:124
  13.0 0.0 copy-start.2
  13.0 0.3 fusion.30.gated_ref
  13.3 0.0 copy-start.1
  13.3 0.7 fusion.47
  14.0 1.3 collective-permute-start.1
  15.3 4.7 %collective-permute-start = (bf16[15,1024]{1,0:T(8,128)(2,1)}, bf16[15,1024]{1,0:T(8,128)(2,1)S(1)}, u32[]{:S(2)}, u32[]{:S(2)}) collective-permute-start(bf16[15,1024]{1,0:T(8,128)(2,1)} %get-tuple-element.8), channel_id=1, source_target_pairs={{0,8},{8,16},{16,24},{24,32},{32,40},{40,48},{48,56},{56,64},{64,7... | collective-permute-start | bytes 92168 | tf_op jit(solution)/shard_map/ppermute | solution.py:85
  19.9 0.0 copy-done.6
  20.0 0.1 copy.26
  20.0 0.1 reduce-window.10
  20.1 0.1 reduce.1
  20.2 0.0 copy-done.5
  20.2 0.6 reduce-window.11
  20.9 0.2 slice_reduce_fusion
  21.1 0.1 select_reduce_fusion
  21.2 0.1 copy.28
  21.3 0.1 copy.29
  21.5 0.1 fusion.40
  21.6 0.7 fusion.37
  22.3 0.0 collective-permute-done.1.after_ref
  22.3 0.0 copy-start.3
  22.3 0.0 collective-permute-done.before_ref
  22.4 0.0 copy-start.4
  22.4 0.0 copy-done.1
  22.4 0.6 copy-done.3
  22.9 0.0 copy-done.4
  23.0 7.5 %shard_map.109 = bf16[256,1024]{1,0:T(8,128)(2,1)} custom-call(bf16[256,1024]{1,0:T(8,128)(2,1)} %copy-done.1, bf16[15,1024]{1,0:T(8,128)(2,1)} %copy-done.4, bf16[15,1024]{1,0:T(8,128)(2,1)} %copy-done.3, f32[31,1024]{1,0:T(8,128)} %taps_ref.1, s32[256,1]{1,0:T(8,128)} %get-tuple-element.12.first_ref, s32[256,1]{1,0:T(8,128)} %get-tuple-element.11.last_ref, ...), custom_call_target="tpu_custom_call" | custom-call | tf_op jit(solution)/shard_map/pallas_call | solution.py:58
  30.5 0.0 copy-done.2
  30.5 2.6 %convert_reduce_fusion = (f32[256]{0:T(256)S(1)}, bf16[256,1024]{1,0:T(8,128)(2,1)S(1)}) fusion(bf16[256,1024]{1,0:T(8,128)(2,1)} %shard_map.109, bf16[1024,1024]{1,0:T(8,128)(2,1)} %param.18, bf16[1,256,1024]{2,1,0:T(8,128)(2,1)S(1)} %copy-done.2), kind=kOutput, calls=%fused_computation.9 | convolution fusion | flops 538181376 | bytes 3671040 | tf_op jit(solution)/shard_map/dot_general | solution.py:150
  33.1 0.3 fusion.21
  33.4 0.6 fusion.11
  34.0 46.4 %all_to_all.10 = bf16[64,8,1024]{2,1,0:T(8,128)(2,1)} all-to-all(bf16[64,8,1024]{2,1,0:T(8,128)(2,1)S(1)} %fusion.11), channel_id=1, replica_groups=mesh['z'=8,'y'=4,'expert'=8] {'expert','z'}, dimensions={0} | all-to-all | bytes 2097152 | tf_op jit(solution)/shard_map/all_to_all | solution.py:177
  80.4 0.0 all-gather.3.cloned.1.call-update
  80.4 0.0 reduce-scatter.2.cloned.1.call-start
  80.5 46.0 %all-gather.3.cloned.1.call-done = bf16[256,8,1024]{2,1,0:T(8,128)(2,1)} async-done(((bf16[64,8,1024]{2,1,0:T(8,128)(2,1)}), bf16[256,8,1024]{2,1,0:T(8,128)(2,1)}) %all-gather.3.cloned.1.call-update) | async-done | bytes 4194320 | tf_op jit(solution)/shard_map/all_gather | solution.py:178
  126.4 0.0 copy-done
  126.4 13.1 %fusion.3 = bf16[2048,1024]{1,0:T(8,128)(2,1)} fusion(bf16[256,8,1024]{2,1,0:T(8,128)(2,1)} %all-gather.3.cloned.1.call-done, bf16[1,1,1024,1024]{3,2,1,0:T(8,128)(2,1)S(1)} %copy-done, bf16[1,1,1024,1024]{3,2,1,0:T(8,128)(2,1)} %param.20), kind=kOutput, calls=%fused_computation.4 | convolution fusion | flops 8602517504 | bytes 12582912 | tf_op jit(solution)/shard_map/dot_general | solution.py:102
  139.5 0.0 copy-start.7
  139.5 0.0 reduce-scatter.2.cloned.1.call-update
  139.5 49.9 %reduce-scatter.2.cloned.1.call-done = bf16[1,64,8,1024]{3,2,1,0:T(8,128)(2,1)} async-done(((bf16[4,64,8,1024]{3,2,1,0:T(8,128)(2,1)}), bf16[1,64,8,1024]{3,2,1,0:T(8,128)(2,1)}) %reduce-scatter.2.cloned.1.call-update) | async-done | bytes 1048592 | tf_op jit(solution)/shard_map/reduce_scatter | solution.py:180
  189.5 10.8 %all-to-all-start.1 = ((bf16[64,8,1024]{2,1,0:T(8,128)(2,1)}), bf16[64,8,1024]{2,1,0:T(8,128)(2,1)}, u32[]{:S(2)}, u32[]{:S(2)}) async-start(bf16[64,8,1024]{2,1,0:T(8,128)(2,1)} %bitcast.69), calls=%async_computation.2 | async-start | bytes 2097152 | tf_op jit(solution)/shard_map/all_to_all | solution.py:181
  200.3 0.0 copy-done.7
  200.3 0.4 fusion.20
  200.7 27.6 %all-to-all-done.1 = bf16[64,8,1024]{2,1,0:T(8,128)(2,1)} async-done(((bf16[64,8,1024]{2,1,0:T(8,128)(2,1)}), bf16[64,8,1024]{2,1,0:T(8,128)(2,1)}, u32[]{:S(2)}, u32[]{:S(2)}) %all-to-all-start.1) | async-done | bytes 1048608 | tf_op jit(solution)/shard_map/all_to_all | solution.py:181
  228.2 2.5 %fusion.19 = bf16[1,256,1024]{2,1,0:T(8,128)(2,1)} fusion(bf16[256,1024]{1,0:T(8,128)(2,1)S(1)} %get-tuple-element.10, bf16[64,8,1024]{2,1,0:T(8,128)(2,1)} %all-to-all-done.1, f32[256]{0:T(256)S(1)} %add_divide_fusion, s32[256]{0:T(256)S(1)} %multiply_add_fusion), kind=kOutput, calls=%fused_computation.23 | convolution fusion | flops 269615104 | bytes 2099200 | tf_op jit(solution)/shard_map/dot_general | solution.py:182
  (11 shorter events, 0.1 us)
Async XLA Ops:
  6.5 119.9 %copy-start = (bf16[1,1,1024,1024]{3,2,1,0:T(8,128)(2,1)S(1)}, bf16[1,1,1024,1024]{3,2,1,0:T(8,128)(2,1)}, u32[]{:S(2)}) copy-start(bf16[1,1,1024,1024]{3,2,1,0:T(8,128)(2,1)} %param.21) | copy-start | bytes 6291460
  6.5 119.9 %all-gather.3.cloned.1.call-start = ((), (), s32[]{:S(2)}) async-start(), calls=%async_computation.4 | async-start | bytes 5242880 | tf_op jit(solution)/shard_map/all_gather | solution.py:178
  9.2 10.7 %copy-start.6 = (s32[1,32]{1,0:T(1,128)S(1)}, s32[1,32]{1,0:T(1,128)}, u32[]{:S(2)}) copy-start(s32[1,32]{1,0:T(1,128)} %param.12) | copy-start | bytes 388
  9.2 11.0 %copy-start.5 = (s32[1,256,1]{1,2,0:T(1,128)S(1)}, s32[1,256,1]{1,2,0:T(1,128)}, u32[]{:S(2)}) copy-start(s32[1,256,1]{1,2,0:T(1,128)} %param.13) | copy-start | bytes 3076
  13.0 17.5 %copy-start.2 = (bf16[1,256,1024]{2,1,0:T(8,128)(2,1)S(1)}, bf16[1,256,1024]{2,1,0:T(8,128)(2,1)}, u32[]{:S(2)}) copy-start(bf16[1,256,1024]{2,1,0:T(8,128)(2,1)} %param.11) | copy-start | bytes 1572868
  13.3 9.1 %copy-start.1 = (bf16[256,1024]{1,0:T(8,128)(2,1)}, bf16[256,1024]{1,0:T(8,128)(2,1)S(1)}, u32[]{:S(2)}) copy-start(bf16[256,1024]{1,0:T(8,128)(2,1)S(1)} %fusion.30.gated_ref) | copy-start | bytes 1572868
  14.0 8.4 %collective-permute-start.1 = (bf16[15,1024]{1,0:T(8,128)(2,1)}, bf16[15,1024]{1,0:T(8,128)(2,1)S(1)}, u32[]{:S(2)}, u32[]{:S(2)}) collective-permute-start(bf16[15,1024]{1,0:T(8,128)(2,1)} %get-tuple-element.7), channel_id=1, source_target_pairs={{8,0},{16,8},{24,16},{32,24},{40,32},{48,40},{56,48},{64,56},{72,6... | collective-permute-start | bytes 92168 | tf_op jit(solution)/shard_map/ppermute | solution.py:86
  15.3 7.1 %collective-permute-start = (bf16[15,1024]{1,0:T(8,128)(2,1)}, bf16[15,1024]{1,0:T(8,128)(2,1)S(1)}, u32[]{:S(2)}, u32[]{:S(2)}) collective-permute-start(bf16[15,1024]{1,0:T(8,128)(2,1)} %get-tuple-element.8), channel_id=1, source_target_pairs={{0,8},{8,16},{16,24},{24,32},{32,40},{40,48},{48,56},{56,64},{64,7... | collective-permute-start | bytes 92168 | tf_op jit(solution)/shard_map/ppermute | solution.py:85
  22.3 0.6 copy-start.3
  22.4 0.6 copy-start.4
  80.4 109.0 %reduce-scatter.2.cloned.1.call-start = ((), (), s32[]{:S(2)}) async-start(), calls=%async_computation.3 | async-start | bytes 5242880 | tf_op jit(solution)/shard_map/reduce_scatter | solution.py:180
  139.5 60.8 %copy-start.7 = (bf16[1024,64]{0,1:T(8,128)(2,1)S(1)}, bf16[1024,64]{0,1:T(8,128)(2,1)}, u32[]{:S(2)}) copy-start(bf16[1024,64]{0,1:T(8,128)(2,1)} %param.19) | copy-start | bytes 393220
  189.5 38.8 %all-to-all-start.1 = ((bf16[64,8,1024]{2,1,0:T(8,128)(2,1)}), bf16[64,8,1024]{2,1,0:T(8,128)(2,1)}, u32[]{:S(2)}, u32[]{:S(2)}) async-start(bf16[64,8,1024]{2,1,0:T(8,128)(2,1)} %bitcast.69), calls=%async_computation.2 | async-start | bytes 2097152 | tf_op jit(solution)/shard_map/all_to_all | solution.py:181
Sparse Core Ops, SparseCore 0:
  80.5 45.8 all-gather.2
  139.6 49.7 reduce-scatter.1

commit v12 on v11

--- a/solution.py
+++ b/solution.py
@@ -8,6 +8,7 @@
 QUARTERS = 4
 ROW_BLOCK = 32
 LANE_BLOCK = 512
+ROW_TILE = 512
 
 
 def depthwise_kernel(
@@ -94,12 +95,30 @@
     return center * lax.rsqrt(variance + 1e-05)
 
 
+def expert_kernel(rows_ref, w_in_ref, w_out_ref, out_ref):
+    hidden = jnp.dot(rows_ref[...], w_in_ref[...], preferred_element_type=jnp.float32)
+    hidden = (hidden * jax.nn.sigmoid(hidden)).astype(jnp.bfloat16)
+    out_ref[...] = jnp.dot(hidden, w_out_ref[...], preferred_element_type=jnp.float32).astype(
+        out_ref.dtype
+    )
+
+
 def expert_pass(slot_block, w_in, w_out):
     slot_rows = slot_block.reshape(-1, slot_block.shape[-1])
-    hidden = jax.nn.silu(jnp.dot(slot_rows, w_in, preferred_element_type=jnp.float32)).astype(
-        jnp.bfloat16
-    )
-    partial_out = jnp.dot(hidden, w_out, preferred_element_type=jnp.float32).astype(jnp.bfloat16)
+    row_count, model_width = slot_rows.shape
+    hidden_width = w_in.shape[1]
+    tile = min(ROW_TILE, row_count)
+    partial_out = pl.pallas_call(
+        expert_kernel,
+        grid=(row_count // tile,),
+        in_specs=[
+            pl.BlockSpec((tile, model_width), lambda r: (r, 0)),
+            pl.BlockSpec((model_width, hidden_width), lambda r: (0, 0)),
+            pl.BlockSpec((hidden_width, model_width), lambda r: (0, 0)),
+        ],
+        out_specs=pl.BlockSpec((tile, model_width), lambda r: (r, 0)),
+        out_shape=jax.ShapeDtypeStruct((row_count, model_width), jnp.bfloat16),
+    )(slot_rows, w_in, w_out)
     return partial_out.reshape(slot_block.shape)
 
 

time: 238 us -> 237 us (level)
  matrix products: 22.8 us -> 9.06 us
  Pallas kernels: 7.54 us -> 20.5 us
    dot_general x1 -> x0, matrix products: 13.1 us -> none  [expert_pass(): jnp.dot(hidden, w_out, preferred_element_type=jnp.float32)]
    pallas_call x0 -> x1, Pallas kernels: none -> 13 us  [expert_pass(): pl.pallas_call(expert_kernel, grid=(row_count // tile,), in_specs=[pl.Blo...]
where the time goes in v12:
time: 237 us
  waiting for transfers between devices  124 us (52%)
  blocking collectives  46.4 us (20%)
  Pallas kernels  20.5 us (9%)
  starting transfers between devices  16.8 us (7%)
  between operations  13.6 us (6%)
  matrix products  9.06 us (4%)
  other arithmetic  5.04 us (2%)
    reduce_scatter x1, waiting for transfers between devices, shards(): lax.psum_scatter(partial_out, 'y', scatter_dimension=0, tiled=False)  49.9 us
    all_to_all x1, blocking collectives, shards(): lax.all_to_all(send_buffer, ('expert', 'z'), split_axis=0, concat_axis=0,...  46.4 us
    all_gather x1, waiting for transfers between devices, shards(): gathered = lax.all_gather(by_member, 'y', axis=0, tiled=False)  46 us
    all_to_all x1, waiting for transfers between devices, shards(): lax.all_to_all(summed, ('expert', 'z'), split_axis=0, concat_axis=0, tile...  27.6 us
    pallas_call x1, Pallas kernels, expert_pass(): pl.pallas_call(expert_kernel, grid=(row_count // tile,), in_specs=[pl.Blo...  13 us
    all_to_all x1, starting transfers between devices, shards(): lax.all_to_all(summed, ('expert', 'z'), split_axis=0, concat_axis=0, tile...  10.8 us
    pallas_call x1, Pallas kernels, depthwise_silu(): pl.pallas_call(depthwise_kernel, grid=(width // LANE_BLOCK,), in_specs=[p...  7.54 us
  transfers between devices with their start and end apart: 5, of which 3 were waited for; matrix products, arithmetic and copies ran while one was open for 1% of the time, Pallas kernels for 0%

profile of v12, /device:TPU:1, one launch (start us, length us, event | category | flops | bytes accessed | tf_op | source)
XLA Modules:
  0.0 236.7 jit_solution(8801832990777619561)
XLA Ops:
  6.5 0.0 copy-start
  6.5 0.0 all-gather.3.cloned.1.call-start
  6.5 1.3 convert_reduce_fusion.1
  7.9 1.3 fusion.12
  9.2 3.7 %fusion.20 = f32[256,2048]{1,0:T(8,128)S(1)} fusion(bf16[1024,2048]{1,0:T(8,128)(2,1)} %param.14, bf16[1,256,1024]{2,1,0:T(8,128)(2,1)} %param.11, f32[256]{0:T(256)S(1)} %add_rsqrt_fusion.1, f32[256]{0:T(256)S(1)} %broadcast_multiply_fusion.1), kind=kOutput, calls=%fused_computation.30 | convolution fusion | flops 1074790400 | bytes 6817792 | tf_op jit(solution)/shard_map/dot_general | solution.py:143
  12.9 0.0 copy-start.6
  12.9 0.0 copy-start.5
  12.9 0.3 fusion.19.gated_ref
  13.2 0.0 copy-start.1
  13.3 0.0 copy-start.2
  13.3 0.6 fusion.35
  13.9 1.3 collective-permute-start.1
  15.2 4.7 %collective-permute-start = (bf16[15,1024]{1,0:T(8,128)(2,1)}, bf16[15,1024]{1,0:T(8,128)(2,1)S(1)}, u32[]{:S(2)}, u32[]{:S(2)}) collective-permute-start(bf16[15,1024]{1,0:T(8,128)(2,1)} %get-tuple-element.8), channel_id=1, source_target_pairs={{0,8},{8,16},{16,24},{24,32},{32,40},{40,48},{48,56},{56,64},{64,7... | collective-permute-start | bytes 92168 | tf_op jit(solution)/shard_map/ppermute | solution.py:86
  19.9 0.0 copy-done.6
  19.9 0.1 copy.26
  20.0 0.1 reduce-window.10
  20.0 0.1 reduce.1
  20.1 0.0 copy-done.5
  20.2 0.6 reduce-window.11
  20.8 0.2 slice_reduce_fusion
  21.0 0.1 select_reduce_fusion
  21.1 0.1 copy.28
  21.2 0.1 copy.29
  21.4 0.1 fusion.29
  21.5 0.7 fusion.26
  22.2 0.0 collective-permute-done.1.after_ref
  22.3 0.0 copy-start.3
  22.3 0.0 collective-permute-done.before_ref
  22.3 0.0 copy-start.4
  22.3 0.0 copy-done.1
  22.3 0.6 copy-done.3
  22.9 0.0 copy-done.4
  22.9 7.5 %shard_map.109 = bf16[256,1024]{1,0:T(8,128)(2,1)} custom-call(bf16[256,1024]{1,0:T(8,128)(2,1)} %copy-done.1, bf16[15,1024]{1,0:T(8,128)(2,1)} %copy-done.4, bf16[15,1024]{1,0:T(8,128)(2,1)} %copy-done.3, f32[31,1024]{1,0:T(8,128)} %taps_ref.1, s32[256,1]{1,0:T(8,128)} %get-tuple-element.12.first_ref, s32[256,1]{1,0:T(8,128)} %get-tuple-element.11.last_ref, ...), custom_call_target="tpu_custom_call" | custom-call | tf_op jit(solution)/shard_map/pallas_call | solution.py:59
  30.4 0.0 copy-done
  30.4 0.0 copy-done.2
  30.4 1.8 convert_reduce_fusion
  32.3 0.3 fusion.10
  32.6 0.6 fusion
  33.2 46.4 %all_to_all.10 = bf16[64,8,1024]{2,1,0:T(8,128)(2,1)} all-to-all(bf16[64,8,1024]{2,1,0:T(8,128)(2,1)S(1)} %fusion), channel_id=1, replica_groups=mesh['z'=8,'y'=4,'expert'=8] {'expert','z'}, dimensions={0} | all-to-all | bytes 2097152 | tf_op jit(solution)/shard_map/all_to_all | solution.py:196
  79.6 0.0 all-gather.3.cloned.1.call-update
  79.6 0.0 reduce-scatter.2.cloned.1.call-start
  79.7 46.0 %all-gather.3.cloned.1.call-done = bf16[256,8,1024]{2,1,0:T(8,128)(2,1)} async-done(((bf16[64,8,1024]{2,1,0:T(8,128)(2,1)}), bf16[256,8,1024]{2,1,0:T(8,128)(2,1)}) %all-gather.3.cloned.1.call-update) | async-done | bytes 4194320 | tf_op jit(solution)/shard_map/all_gather | solution.py:197
  125.6 13.0 %shard_map.110 = bf16[2048,1024]{1,0:T(8,128)(2,1)} custom-call(bf16[2048,1024]{1,0:T(8,128)(2,1)} %bitcast.58, bf16[1024,1024]{1,0:T(8,128)(2,1)} %bitcast.59, bf16[1024,1024]{1,0:T(8,128)(2,1)} %bitcast.60), custom_call_target="tpu_custom_call" | custom-call | tf_op jit(solution)/shard_map/pallas_call | solution.py:111
  138.6 0.0 reduce-scatter.2.cloned.1.call-update
  138.6 0.0 copy-start.7
  138.6 49.9 %reduce-scatter.2.cloned.1.call-done = bf16[1,64,8,1024]{3,2,1,0:T(8,128)(2,1)} async-done(((bf16[4,64,8,1024]{3,2,1,0:T(8,128)(2,1)}), bf16[1,64,8,1024]{3,2,1,0:T(8,128)(2,1)}) %reduce-scatter.2.cloned.1.call-update) | async-done | bytes 1048592 | tf_op jit(solution)/shard_map/reduce_scatter | solution.py:199
  188.6 10.8 %all-to-all-start.1 = ((bf16[64,8,1024]{2,1,0:T(8,128)(2,1)}), bf16[64,8,1024]{2,1,0:T(8,128)(2,1)}, u32[]{:S(2)}, u32[]{:S(2)}) async-start(bf16[64,8,1024]{2,1,0:T(8,128)(2,1)} %bitcast.61), calls=%async_computation.2 | async-start | bytes 2097152 | tf_op jit(solution)/shard_map/all_to_all | solution.py:200
  199.4 0.0 copy-done.7
  199.4 0.4 fusion.9
  199.8 27.6 %all-to-all-done.1 = bf16[64,8,1024]{2,1,0:T(8,128)(2,1)} async-done(((bf16[64,8,1024]{2,1,0:T(8,128)(2,1)}), bf16[64,8,1024]{2,1,0:T(8,128)(2,1)}, u32[]{:S(2)}, u32[]{:S(2)}) %all-to-all-start.1) | async-done | bytes 1048608 | tf_op jit(solution)/shard_map/all_to_all | solution.py:200
  227.4 2.5 %fusion.8 = bf16[1,256,1024]{2,1,0:T(8,128)(2,1)} fusion(bf16[256,1024]{1,0:T(8,128)(2,1)S(1)} %get-tuple-element.10, bf16[64,8,1024]{2,1,0:T(8,128)(2,1)} %all-to-all-done.1, f32[256]{0:T(256)S(1)} %add_divide_fusion, s32[256]{0:T(256)S(1)} %multiply_add_fusion), kind=kOutput, calls=%fused_computation.16 | convolution fusion | flops 269615104 | bytes 2099200 | tf_op jit(solution)/shard_map/dot_general | solution.py:201
  (11 shorter events, 0.1 us)
Async XLA Ops:
  6.5 23.9 %copy-start = (bf16[1024,1024]{1,0:T(8,128)(2,1)S(1)}, bf16[1024,1024]{1,0:T(8,128)(2,1)}, u32[]{:S(2)}) copy-start(bf16[1024,1024]{1,0:T(8,128)(2,1)} %param.18) | copy-start | bytes 6291460
  6.5 119.1 %all-gather.3.cloned.1.call-start = ((), (), s32[]{:S(2)}) async-start(), calls=%async_computation.4 | async-start | bytes 5242880 | tf_op jit(solution)/shard_map/all_gather | solution.py:197
  12.9 6.9 %copy-start.6 = (s32[1,32]{1,0:T(1,128)S(1)}, s32[1,32]{1,0:T(1,128)}, u32[]{:S(2)}) copy-start(s32[1,32]{1,0:T(1,128)} %param.12) | copy-start | bytes 388
  12.9 7.2 %copy-start.5 = (s32[1,256,1]{1,2,0:T(1,128)S(1)}, s32[1,256,1]{1,2,0:T(1,128)}, u32[]{:S(2)}) copy-start(s32[1,256,1]{1,2,0:T(1,128)} %param.13) | copy-start | bytes 3076
  13.2 9.0 %copy-start.1 = (bf16[256,1024]{1,0:T(8,128)(2,1)}, bf16[256,1024]{1,0:T(8,128)(2,1)S(1)}, u32[]{:S(2)}) copy-start(bf16[256,1024]{1,0:T(8,128)(2,1)S(1)} %fusion.19.gated_ref) | copy-start | bytes 1572868
  13.3 17.2 %copy-start.2 = (bf16[1,256,1024]{2,1,0:T(8,128)(2,1)S(1)}, bf16[1,256,1024]{2,1,0:T(8,128)(2,1)}, u32[]{:S(2)}) copy-start(bf16[1,256,1024]{2,1,0:T(8,128)(2,1)} %param.11) | copy-start | bytes 1572868
  13.9 8.4 %collective-permute-start.1 = (bf16[15,1024]{1,0:T(8,128)(2,1)}, bf16[15,1024]{1,0:T(8,128)(2,1)S(1)}, u32[]{:S(2)}, u32[]{:S(2)}) collective-permute-start(bf16[15,1024]{1,0:T(8,128)(2,1)} %get-tuple-element.7), channel_id=1, source_target_pairs={{8,0},{16,8},{24,16},{32,24},{40,32},{48,40},{56,48},{64,56},{72,6... | collective-permute-start | bytes 92168 | tf_op jit(solution)/shard_map/ppermute | solution.py:87
  15.2 7.1 %collective-permute-start = (bf16[15,1024]{1,0:T(8,128)(2,1)}, bf16[15,1024]{1,0:T(8,128)(2,1)S(1)}, u32[]{:S(2)}, u32[]{:S(2)}) collective-permute-start(bf16[15,1024]{1,0:T(8,128)(2,1)} %get-tuple-element.8), channel_id=1, source_target_pairs={{0,8},{8,16},{16,24},{24,32},{32,40},{40,48},{48,56},{56,64},{64,7... | collective-permute-start | bytes 92168 | tf_op jit(solution)/shard_map/ppermute | solution.py:86
  22.3 0.6 copy-start.3
  22.3 0.6 copy-start.4
  79.6 108.9 %reduce-scatter.2.cloned.1.call-start = ((), (), s32[]{:S(2)}) async-start(), calls=%async_computation.3 | async-start | bytes 5242880 | tf_op jit(solution)/shard_map/reduce_scatter | solution.py:199
  138.6 60.7 %copy-start.7 = (bf16[1024,64]{0,1:T(8,128)(2,1)S(1)}, bf16[1024,64]{0,1:T(8,128)(2,1)}, u32[]{:S(2)}) copy-start(bf16[1024,64]{0,1:T(8,128)(2,1)} %param.19) | copy-start | bytes 393220
  188.6 38.8 %all-to-all-start.1 = ((bf16[64,8,1024]{2,1,0:T(8,128)(2,1)}), bf16[64,8,1024]{2,1,0:T(8,128)(2,1)}, u32[]{:S(2)}, u32[]{:S(2)}) async-start(bf16[64,8,1024]{2,1,0:T(8,128)(2,1)} %bitcast.61), calls=%async_computation.2 | async-start | bytes 2097152 | tf_op jit(solution)/shard_map/all_to_all | solution.py:200
Sparse Core Ops, SparseCore 0:
  79.7 45.8 all-gather.2
  138.8 49.7 reduce-scatter.1

commit v13 on v12

--- a/solution.py
+++ b/solution.py
@@ -182,7 +182,7 @@
     gate_value = jax.nn.sigmoid(jnp.sum(logits * onehot.astype(jnp.float32), axis=1))
     owner_group = route_ids // per_owner
     member = route_ids % per_owner
-    slot_index = (owner_group * per_owner + member) * capacity + rank_in
+    slot_index = (member * owners + owner_group) * capacity + rank_in
     slot_count = per_owner * owners * capacity
     placing = (slot_index[:, None] == jnp.arange(slot_count, dtype=jnp.int32)[None, :]).astype(
         jnp.bfloat16
@@ -193,11 +193,11 @@
     send_buffer = send_buffer.reshape(owners * per_owner, capacity, model_width)
     w_in = expert_in[0, 0]
     w_out = expert_out[0, 0]
-    by_member = lax.all_to_all(send_buffer, ("expert", "z"), split_axis=0, concat_axis=0, tiled=True)
+    by_member = lax.all_to_all(send_buffer, ("z", "expert"), split_axis=0, concat_axis=0, tiled=True)
     gathered = lax.all_gather(by_member, "y", axis=0, tiled=False)
     partial_out = expert_pass(gathered, w_in, w_out)
     summed = lax.psum_scatter(partial_out, "y", scatter_dimension=0, tiled=False)
-    results = lax.all_to_all(summed, ("expert", "z"), split_axis=0, concat_axis=0, tiled=True)
+    results = lax.all_to_all(summed, ("z", "expert"), split_axis=0, concat_axis=0, tiled=True)
     frame_moe = jnp.dot(
         placing, results.reshape(-1, model_width), preferred_element_type=jnp.float32
     )

time: 237 us -> 237 us (level)
  no operation moved by 1% of the time
where the time goes in v13:
time: 237 us; the launch traced here: 236 us
  waiting for transfers between devices  123 us (52%)
  blocking collectives  46.3 us (20%)
  Pallas kernels  20.5 us (9%)
  starting transfers between devices  16.8 us (7%)
  between operations  13.6 us (6%)
  matrix products  9.06 us (4%)
  other arithmetic  5.04 us (2%)
    reduce_scatter x1, waiting for transfers between devices, shards(): lax.psum_scatter(partial_out, 'y', scatter_dimension=0, tiled=False)  49.9 us
    all_to_all x1, blocking collectives, shards(): lax.all_to_all(send_buffer, ('z', 'expert'), split_axis=0, concat_axis=0,...  46.3 us
    all_gather x1, waiting for transfers between devices, shards(): gathered = lax.all_gather(by_member, 'y', axis=0, tiled=False)  45.6 us
    all_to_all x1, waiting for transfers between devices, shards(): lax.all_to_all(summed, ('z', 'expert'), split_axis=0, concat_axis=0, tile...  27.5 us
    pallas_call x1, Pallas kernels, expert_pass(): pl.pallas_call(expert_kernel, grid=(row_count // tile,), in_specs=[pl.Blo...  13 us
    all_to_all x1, starting transfers between devices, shards(): lax.all_to_all(summed, ('z', 'expert'), split_axis=0, concat_axis=0, tile...  10.8 us
    pallas_call x1, Pallas kernels, depthwise_silu(): pl.pallas_call(depthwise_kernel, grid=(width // LANE_BLOCK,), in_specs=[p...  7.54 us
  transfers between devices with their start and end apart: 5, of which 3 were waited for; matrix products, arithmetic and copies ran while one was open for 1% of the time, Pallas kernels for 0%

profile of v13, /device:TPU:1, one launch (start us, length us, event | category | flops | bytes accessed | tf_op | source)
XLA Modules:
  0.0 236.1 jit_solution(14382926159593454613)
XLA Ops:
  6.5 0.0 copy-start
  6.5 0.0 all-gather.3.cloned.1.call-start
  6.5 1.3 convert_reduce_fusion.1
  7.9 1.3 fusion.12
  9.2 3.7 %fusion.20 = f32[256,2048]{1,0:T(8,128)S(1)} fusion(bf16[1024,2048]{1,0:T(8,128)(2,1)} %param.14, bf16[1,256,1024]{2,1,0:T(8,128)(2,1)} %param.11, f32[256]{0:T(256)S(1)} %add_rsqrt_fusion.1, f32[256]{0:T(256)S(1)} %broadcast_multiply_fusion.1), kind=kOutput, calls=%fused_computation.30 | convolution fusion | flops 1074790400 | bytes 6817792 | tf_op jit(solution)/shard_map/dot_general | solution.py:143
  12.9 0.0 copy-start.6
  12.9 0.0 copy-start.5
  12.9 0.3 fusion.19.gated_ref
  13.2 0.0 copy-start.1
  13.3 0.0 copy-start.2
  13.3 0.6 fusion.36
  13.9 1.3 collective-permute-start.1
  15.2 4.7 %collective-permute-start = (bf16[15,1024]{1,0:T(8,128)(2,1)}, bf16[15,1024]{1,0:T(8,128)(2,1)S(1)}, u32[]{:S(2)}, u32[]{:S(2)}) collective-permute-start(bf16[15,1024]{1,0:T(8,128)(2,1)} %get-tuple-element.8), channel_id=1, source_target_pairs={{0,8},{8,16},{16,24},{24,32},{32,40},{40,48},{48,56},{56,64},{64,7... | collective-permute-start | bytes 92168 | tf_op jit(solution)/shard_map/ppermute | solution.py:86
  19.9 0.0 copy-done.6
  19.9 0.1 copy.26
  20.0 0.1 reduce-window.10
  20.0 0.1 reduce.1
  20.1 0.0 copy-done.5
  20.2 0.6 reduce-window.11
  20.8 0.2 slice_reduce_fusion
  21.0 0.1 select_reduce_fusion
  21.1 0.1 copy.28
  21.2 0.1 copy.29
  21.4 0.1 fusion.29
  21.5 0.7 fusion.26
  22.2 0.0 collective-permute-done.1.after_ref
  22.3 0.0 copy-start.3
  22.3 0.0 collective-permute-done.before_ref
  22.3 0.0 copy-start.4
  22.3 0.0 copy-done.1
  22.3 0.6 copy-done.3
  22.9 0.0 copy-done.4
  22.9 7.5 %shard_map.109 = bf16[256,1024]{1,0:T(8,128)(2,1)} custom-call(bf16[256,1024]{1,0:T(8,128)(2,1)} %copy-done.1, bf16[15,1024]{1,0:T(8,128)(2,1)} %copy-done.4, bf16[15,1024]{1,0:T(8,128)(2,1)} %copy-done.3, f32[31,1024]{1,0:T(8,128)} %taps_ref.1, s32[256,1]{1,0:T(8,128)} %get-tuple-element.12.first_ref, s32[256,1]{1,0:T(8,128)} %get-tuple-element.11.last_ref, ...), custom_call_target="tpu_custom_call" | custom-call | tf_op jit(solution)/shard_map/pallas_call | solution.py:59
  30.4 0.0 copy-done
  30.4 0.0 copy-done.2
  30.4 1.8 convert_reduce_fusion
  32.3 0.3 fusion.10
  32.6 0.6 fusion
  33.2 46.3 %all_to_all.10 = bf16[64,8,1024]{2,1,0:T(8,128)(2,1)} all-to-all(bf16[64,8,1024]{2,1,0:T(8,128)(2,1)S(1)} %fusion), channel_id=1, replica_groups=mesh['z'=8,'y'=4,'expert'=8] {'z','expert'}, dimensions={0} | all-to-all | bytes 2097152 | tf_op jit(solution)/shard_map/all_to_all | solution.py:196
  79.5 0.0 all-gather.3.cloned.1.call-update
  79.5 0.0 reduce-scatter.2.cloned.1.call-start
  79.6 45.6 %all-gather.3.cloned.1.call-done = bf16[256,8,1024]{2,1,0:T(8,128)(2,1)} async-done(((bf16[64,8,1024]{2,1,0:T(8,128)(2,1)}), bf16[256,8,1024]{2,1,0:T(8,128)(2,1)}) %all-gather.3.cloned.1.call-update) | async-done | bytes 4194320 | tf_op jit(solution)/shard_map/all_gather | solution.py:197
  125.2 13.0 %shard_map.110 = bf16[2048,1024]{1,0:T(8,128)(2,1)} custom-call(bf16[2048,1024]{1,0:T(8,128)(2,1)} %bitcast.58, bf16[1024,1024]{1,0:T(8,128)(2,1)} %bitcast.59, bf16[1024,1024]{1,0:T(8,128)(2,1)} %bitcast.60), custom_call_target="tpu_custom_call" | custom-call | tf_op jit(solution)/shard_map/pallas_call | solution.py:111
  138.1 0.0 reduce-scatter.2.cloned.1.call-update
  138.2 0.0 copy-start.7
  138.2 49.9 %reduce-scatter.2.cloned.1.call-done = bf16[1,64,8,1024]{3,2,1,0:T(8,128)(2,1)} async-done(((bf16[4,64,8,1024]{3,2,1,0:T(8,128)(2,1)}), bf16[1,64,8,1024]{3,2,1,0:T(8,128)(2,1)}) %reduce-scatter.2.cloned.1.call-update) | async-done | bytes 1048592 | tf_op jit(solution)/shard_map/reduce_scatter | solution.py:199
  188.1 10.8 %all-to-all-start.1 = ((bf16[64,8,1024]{2,1,0:T(8,128)(2,1)}), bf16[64,8,1024]{2,1,0:T(8,128)(2,1)}, u32[]{:S(2)}, u32[]{:S(2)}) async-start(bf16[64,8,1024]{2,1,0:T(8,128)(2,1)} %bitcast.61), calls=%async_computation.2 | async-start | bytes 2097152 | tf_op jit(solution)/shard_map/all_to_all | solution.py:200
  198.9 0.0 copy-done.7
  198.9 0.4 fusion.9
  199.3 27.5 %all-to-all-done.1 = bf16[64,8,1024]{2,1,0:T(8,128)(2,1)} async-done(((bf16[64,8,1024]{2,1,0:T(8,128)(2,1)}), bf16[64,8,1024]{2,1,0:T(8,128)(2,1)}, u32[]{:S(2)}, u32[]{:S(2)}) %all-to-all-start.1) | async-done | bytes 1048608 | tf_op jit(solution)/shard_map/all_to_all | solution.py:200
  226.8 2.5 %fusion.8 = bf16[1,256,1024]{2,1,0:T(8,128)(2,1)} fusion(bf16[256,1024]{1,0:T(8,128)(2,1)S(1)} %get-tuple-element.10, bf16[64,8,1024]{2,1,0:T(8,128)(2,1)} %all-to-all-done.1, f32[256]{0:T(256)S(1)} %add_divide_fusion, s32[256]{0:T(256)S(1)} %multiply_add_fusion), kind=kOutput, calls=%fused_computation.16 | convolution fusion | flops 269615104 | bytes 2099200 | tf_op jit(solution)/shard_map/dot_general | solution.py:201
  (11 shorter events, 0.1 us)
Async XLA Ops:
  6.5 23.9 %copy-start = (bf16[1024,1024]{1,0:T(8,128)(2,1)S(1)}, bf16[1024,1024]{1,0:T(8,128)(2,1)}, u32[]{:S(2)}) copy-start(bf16[1024,1024]{1,0:T(8,128)(2,1)} %param.18) | copy-start | bytes 6291460
  6.5 118.6 %all-gather.3.cloned.1.call-start = ((), (), s32[]{:S(2)}) async-start(), calls=%async_computation.4 | async-start | bytes 5242880 | tf_op jit(solution)/shard_map/all_gather | solution.py:197
  12.9 6.9 %copy-start.6 = (s32[1,32]{1,0:T(1,128)S(1)}, s32[1,32]{1,0:T(1,128)}, u32[]{:S(2)}) copy-start(s32[1,32]{1,0:T(1,128)} %param.12) | copy-start | bytes 388
  12.9 7.2 %copy-start.5 = (s32[1,256,1]{1,2,0:T(1,128)S(1)}, s32[1,256,1]{1,2,0:T(1,128)}, u32[]{:S(2)}) copy-start(s32[1,256,1]{1,2,0:T(1,128)} %param.13) | copy-start | bytes 3076
  13.2 9.0 %copy-start.1 = (bf16[256,1024]{1,0:T(8,128)(2,1)}, bf16[256,1024]{1,0:T(8,128)(2,1)S(1)}, u32[]{:S(2)}) copy-start(bf16[256,1024]{1,0:T(8,128)(2,1)S(1)} %fusion.19.gated_ref) | copy-start | bytes 1572868
  13.3 17.2 %copy-start.2 = (bf16[1,256,1024]{2,1,0:T(8,128)(2,1)S(1)}, bf16[1,256,1024]{2,1,0:T(8,128)(2,1)}, u32[]{:S(2)}) copy-start(bf16[1,256,1024]{2,1,0:T(8,128)(2,1)} %param.11) | copy-start | bytes 1572868
  13.9 8.4 %collective-permute-start.1 = (bf16[15,1024]{1,0:T(8,128)(2,1)}, bf16[15,1024]{1,0:T(8,128)(2,1)S(1)}, u32[]{:S(2)}, u32[]{:S(2)}) collective-permute-start(bf16[15,1024]{1,0:T(8,128)(2,1)} %get-tuple-element.7), channel_id=1, source_target_pairs={{8,0},{16,8},{24,16},{32,24},{40,32},{48,40},{56,48},{64,56},{72,6... | collective-permute-start | bytes 92168 | tf_op jit(solution)/shard_map/ppermute | solution.py:87
  15.2 7.1 %collective-permute-start = (bf16[15,1024]{1,0:T(8,128)(2,1)}, bf16[15,1024]{1,0:T(8,128)(2,1)S(1)}, u32[]{:S(2)}, u32[]{:S(2)}) collective-permute-start(bf16[15,1024]{1,0:T(8,128)(2,1)} %get-tuple-element.8), channel_id=1, source_target_pairs={{0,8},{8,16},{16,24},{24,32},{32,40},{40,48},{48,56},{56,64},{64,7... | collective-permute-start | bytes 92168 | tf_op jit(solution)/shard_map/ppermute | solution.py:86
  22.3 0.6 copy-start.3
  22.3 0.6 copy-start.4
  79.5 108.6 %reduce-scatter.2.cloned.1.call-start = ((), (), s32[]{:S(2)}) async-start(), calls=%async_computation.3 | async-start | bytes 5242880 | tf_op jit(solution)/shard_map/reduce_scatter | solution.py:199
  138.2 60.7 %copy-start.7 = (bf16[1024,64]{0,1:T(8,128)(2,1)S(1)}, bf16[1024,64]{0,1:T(8,128)(2,1)}, u32[]{:S(2)}) copy-start(bf16[1024,64]{0,1:T(8,128)(2,1)} %param.19) | copy-start | bytes 393220
  188.1 38.7 %all-to-all-start.1 = ((bf16[64,8,1024]{2,1,0:T(8,128)(2,1)}), bf16[64,8,1024]{2,1,0:T(8,128)(2,1)}, u32[]{:S(2)}, u32[]{:S(2)}) async-start(bf16[64,8,1024]{2,1,0:T(8,128)(2,1)} %bitcast.61), calls=%async_computation.2 | async-start | bytes 2097152 | tf_op jit(solution)/shard_map/all_to_all | solution.py:200
Sparse Core Ops, SparseCore 0:
  79.6 45.4 all-gather.2
  138.3 49.7 reduce-scatter.1

commit v14 on v13

--- a/solution.py
+++ b/solution.py
@@ -122,6 +122,44 @@
     return partial_out.reshape(slot_block.shape)
 
 
+def others_kernel(own_ref, rows_ref, own_part_ref, w_in_ref, w_out_ref, out_ref):
+    mine = pl.program_id(0) == own_ref[0]
+
+    @pl.when(mine)
+    def _():
+        out_ref[...] = own_part_ref[...]
+
+    @pl.when(jnp.logical_not(mine))
+    def _():
+        expert_kernel(rows_ref, w_in_ref, w_out_ref, out_ref)
+
+
+def expert_pass_others(gathered, own_partial, own_index, w_in, w_out):
+    blocks = gathered.shape[0]
+    model_width = gathered.shape[-1]
+    slot_rows = gathered.reshape(-1, model_width)
+    row_count = slot_rows.shape[0]
+    tile = row_count // blocks
+    hidden_width = w_in.shape[1]
+    own_rows = own_partial.reshape(-1, model_width)
+    partial_out = pl.pallas_call(
+        others_kernel,
+        grid_spec=pltpu.PrefetchScalarGridSpec(
+            num_scalar_prefetch=1,
+            grid=(blocks,),
+            in_specs=[
+                pl.BlockSpec((tile, model_width), lambda r, own: (r, 0)),
+                pl.BlockSpec((tile, model_width), lambda r, own: (0, 0)),
+                pl.BlockSpec((model_width, hidden_width), lambda r, own: (0, 0)),
+                pl.BlockSpec((hidden_width, model_width), lambda r, own: (0, 0)),
+            ],
+            out_specs=pl.BlockSpec((tile, model_width), lambda r, own: (r, 0)),
+        ),
+        out_shape=jax.ShapeDtypeStruct((row_count, model_width), jnp.bfloat16),
+    )(own_index, slot_rows, own_rows, w_in, w_out)
+    return partial_out.reshape(gathered.shape)
+
+
 def shards(
     frames,
     utt_lengths,
@@ -194,8 +232,10 @@
     w_in = expert_in[0, 0]
     w_out = expert_out[0, 0]
     by_member = lax.all_to_all(send_buffer, ("z", "expert"), split_axis=0, concat_axis=0, tiled=True)
+    own_partial = expert_pass(by_member, w_in, w_out)
     gathered = lax.all_gather(by_member, "y", axis=0, tiled=False)
-    partial_out = expert_pass(gathered, w_in, w_out)
+    own_index = lax.axis_index("y").astype(jnp.int32).reshape(1)
+    partial_out = expert_pass_others(gathered, own_partial, own_index, w_in, w_out)
     summed = lax.psum_scatter(partial_out, "y", scatter_dimension=0, tiled=False)
     results = lax.all_to_all(summed, ("z", "expert"), split_axis=0, concat_axis=0, tiled=True)
     frame_moe = jnp.dot(

time: 237 us -> 237 us (level)
  Pallas kernels: 20.5 us -> 24.7 us
  waiting for transfers between devices: 123 us -> 119 us
    pallas_call x0 -> x1, Pallas kernels: none -> 11.2 us  [expert_pass_others(): pl.pallas_call(others_kernel, grid_spec=pltpu.PrefetchScalarGridSpec(num_...]
    pallas_call x1, Pallas kernels: 13 us -> 5.95 us  [expert_pass(): pl.pallas_call(expert_kernel, grid=(row_count // tile,), in_specs=[pl.Blo...]
    all_gather x1, waiting for transfers between devices: 45.6 us -> 39.6 us  [shards(): gathered = lax.all_gather(by_member, 'y', axis=0, tiled=False)]
  transfers between devices with their start and end apart: 5 -> 5, of which waited for: 3 -> 3; matrix products, arithmetic and copies ran while one was open for 1% -> 1% of each run, Pallas kernels for 0% -> 3%
where the time goes in v14:
time: 237 us; the launch traced here: 236 us
  waiting for transfers between devices  119 us (50%)
  blocking collectives  46.3 us (20%)
  Pallas kernels  24.7 us (10%)
  starting transfers between devices  16.8 us (7%)
  between operations  13.6 us (6%)
  matrix products  9.06 us (4%)
  other arithmetic  5.04 us (2%)
    reduce_scatter x1, waiting for transfers between devices, shards(): lax.psum_scatter(partial_out, 'y', scatter_dimension=0, tiled=False)  51.7 us
    all_to_all x1, blocking collectives, shards(): lax.all_to_all(send_buffer, ('z', 'expert'), split_axis=0, concat_axis=0,...  46.3 us
    all_gather x1, waiting for transfers between devices, shards(): gathered = lax.all_gather(by_member, 'y', axis=0, tiled=False)  39.6 us
    all_to_all x1, waiting for transfers between devices, shards(): lax.all_to_all(summed, ('z', 'expert'), split_axis=0, concat_axis=0, tile...  27.5 us
    pallas_call x1, Pallas kernels, expert_pass_others(): pl.pallas_call(others_kernel, grid_spec=pltpu.PrefetchScalarGridSpec(num_...  11.2 us
    all_to_all x1, starting transfers between devices, shards(): lax.all_to_all(summed, ('z', 'expert'), split_axis=0, concat_axis=0, tile...  10.8 us
    pallas_call x1, Pallas kernels, depthwise_silu(): pl.pallas_call(depthwise_kernel, grid=(width // LANE_BLOCK,), in_specs=[p...  7.54 us
    pallas_call x1, Pallas kernels, expert_pass(): pl.pallas_call(expert_kernel, grid=(row_count // tile,), in_specs=[pl.Blo...  5.95 us
  transfers between devices with their start and end apart: 5, of which 3 were waited for; matrix products, arithmetic and copies ran while one was open for 1% of the time, Pallas kernels for 3%

profile of v14, /device:TPU:1, one launch (start us, length us, event | category | flops | bytes accessed | tf_op | source)
XLA Modules:
  0.0 236.1 jit_solution(7993654672379574016)
XLA Ops:
  6.5 0.0 copy-start
  6.5 0.0 all-gather.3.cloned.1.call-start
  6.5 1.3 convert_reduce_fusion.1
  7.9 1.3 fusion.12
  9.2 3.7 %fusion.20 = f32[256,2048]{1,0:T(8,128)S(1)} fusion(bf16[1024,2048]{1,0:T(8,128)(2,1)} %param.14, bf16[1,256,1024]{2,1,0:T(8,128)(2,1)} %param.11, f32[256]{0:T(256)S(1)} %add_rsqrt_fusion.1, f32[256]{0:T(256)S(1)} %broadcast_multiply_fusion.1), kind=kOutput, calls=%fused_computation.30 | convolution fusion | flops 1074790400 | bytes 6817792 | tf_op jit(solution)/shard_map/dot_general | solution.py:181
  12.9 0.0 copy-start.6
  12.9 0.0 copy-start.5
  12.9 0.3 fusion.19.gated_ref
  13.2 0.0 copy-start.1
  13.2 0.0 copy-start.2
  13.3 0.6 fusion.36
  13.9 1.3 collective-permute-start.1
  15.2 4.7 %collective-permute-start = (bf16[15,1024]{1,0:T(8,128)(2,1)}, bf16[15,1024]{1,0:T(8,128)(2,1)S(1)}, u32[]{:S(2)}, u32[]{:S(2)}) collective-permute-start(bf16[15,1024]{1,0:T(8,128)(2,1)} %get-tuple-element.8), channel_id=1, source_target_pairs={{0,8},{8,16},{16,24},{24,32},{32,40},{40,48},{48,56},{56,64},{64,7... | collective-permute-start | bytes 92168 | tf_op jit(solution)/shard_map/ppermute | solution.py:86
  19.9 0.0 copy-done.6
  19.9 0.1 copy.26
  20.0 0.1 reduce-window.10
  20.0 0.1 reduce.1
  20.1 0.0 copy-done.5
  20.2 0.6 reduce-window.11
  20.8 0.2 slice_reduce_fusion
  21.0 0.1 select_reduce_fusion
  21.1 0.1 copy.28
  21.2 0.1 copy.29
  21.4 0.1 fusion.29
  21.5 0.7 fusion.26
  22.2 0.0 collective-permute-done.1.after_ref
  22.3 0.0 copy-start.3
  22.3 0.0 collective-permute-done.before_ref
  22.3 0.0 copy-start.4
  22.3 0.0 copy-done.1
  22.3 0.6 copy-done.3
  22.9 0.0 copy-done.4
  22.9 7.5 %shard_map.109 = bf16[256,1024]{1,0:T(8,128)(2,1)} custom-call(bf16[256,1024]{1,0:T(8,128)(2,1)} %copy-done.1, bf16[15,1024]{1,0:T(8,128)(2,1)} %copy-done.4, bf16[15,1024]{1,0:T(8,128)(2,1)} %copy-done.3, f32[31,1024]{1,0:T(8,128)} %taps_ref.1, s32[256,1]{1,0:T(8,128)} %get-tuple-element.12.first_ref, s32[256,1]{1,0:T(8,128)} %get-tuple-element.11.last_ref, ...), custom_call_target="tpu_custom_call" | custom-call | tf_op jit(solution)/shard_map/pallas_call | solution.py:59
  30.4 0.0 copy-done
  30.4 0.0 copy-done.2
  30.4 1.8 convert_reduce_fusion
  32.3 0.3 fusion.10
  32.6 0.6 fusion
  33.2 46.3 %all_to_all.10 = bf16[64,8,1024]{2,1,0:T(8,128)(2,1)} all-to-all(bf16[64,8,1024]{2,1,0:T(8,128)(2,1)S(1)} %fusion), channel_id=1, replica_groups=mesh['z'=8,'y'=4,'expert'=8] {'z','expert'}, dimensions={0} | all-to-all | bytes 2097152 | tf_op jit(solution)/shard_map/all_to_all | solution.py:234
  79.5 0.0 all-gather.3.cloned.1.call-update
  79.5 0.0 reduce-scatter.2.cloned.1.call-start
  79.6 6.0 %shard_map.110.own_part_ref = bf16[512,1024]{1,0:T(8,128)(2,1)} custom-call(bf16[512,1024]{1,0:T(8,128)(2,1)} %bitcast.60, bf16[1024,1024]{1,0:T(8,128)(2,1)} %bitcast.61, bf16[1024,1024]{1,0:T(8,128)(2,1)} %bitcast.63), custom_call_target="tpu_custom_call" | custom-call | tf_op jit(solution)/shard_map/pallas_call | solution.py:111
  85.5 39.6 %all-gather.3.cloned.1.call-done = bf16[256,8,1024]{2,1,0:T(8,128)(2,1)} async-done(((bf16[64,8,1024]{2,1,0:T(8,128)(2,1)}), bf16[256,8,1024]{2,1,0:T(8,128)(2,1)}) %all-gather.3.cloned.1.call-update) | async-done | bytes 4194320 | tf_op jit(solution)/shard_map/all_gather | solution.py:236
  125.2 11.2 %shard_map.111 = bf16[2048,1024]{1,0:T(8,128)(2,1)} custom-call(s32[1]{0:T(128)} %bitcast.10.own_ref, bf16[2048,1024]{1,0:T(8,128)(2,1)} %bitcast.65, bf16[512,1024]{1,0:T(8,128)(2,1)} %shard_map.110.own_part_ref, bf16[1024,1024]{1,0:T(8,128)(2,1)} %bitcast.62, bf16[1024,1024]{1,0:T(8,128)(2,1)} %bitcast.64), custom_call_target="tpu_custom_call" | custom-call | tf_op jit(solution)/shard_map/pallas_call | solution.py:145
  136.3 0.0 reduce-scatter.2.cloned.1.call-update
  136.4 0.0 copy-start.7
  136.4 51.7 %reduce-scatter.2.cloned.1.call-done = bf16[1,64,8,1024]{3,2,1,0:T(8,128)(2,1)} async-done(((bf16[4,64,8,1024]{3,2,1,0:T(8,128)(2,1)}), bf16[1,64,8,1024]{3,2,1,0:T(8,128)(2,1)}) %reduce-scatter.2.cloned.1.call-update) | async-done | bytes 1048592 | tf_op jit(solution)/shard_map/reduce_scatter | solution.py:239
  188.0 10.8 %all-to-all-start.1 = ((bf16[64,8,1024]{2,1,0:T(8,128)(2,1)}), bf16[64,8,1024]{2,1,0:T(8,128)(2,1)}, u32[]{:S(2)}, u32[]{:S(2)}) async-start(bf16[64,8,1024]{2,1,0:T(8,128)(2,1)} %bitcast.66), calls=%async_computation.2 | async-start | bytes 2097152 | tf_op jit(solution)/shard_map/all_to_all | solution.py:240
  198.9 0.0 copy-done.7
  198.9 0.4 fusion.9
  199.3 27.5 %all-to-all-done.1 = bf16[64,8,1024]{2,1,0:T(8,128)(2,1)} async-done(((bf16[64,8,1024]{2,1,0:T(8,128)(2,1)}), bf16[64,8,1024]{2,1,0:T(8,128)(2,1)}, u32[]{:S(2)}, u32[]{:S(2)}) %all-to-all-start.1) | async-done | bytes 1048608 | tf_op jit(solution)/shard_map/all_to_all | solution.py:240
  226.8 2.5 %fusion.8 = bf16[1,256,1024]{2,1,0:T(8,128)(2,1)} fusion(bf16[256,1024]{1,0:T(8,128)(2,1)S(1)} %get-tuple-element.10, bf16[64,8,1024]{2,1,0:T(8,128)(2,1)} %all-to-all-done.1, f32[256]{0:T(256)S(1)} %add_divide_fusion, s32[256]{0:T(256)S(1)} %multiply_add_fusion), kind=kOutput, calls=%fused_computation.16 | convolution fusion | flops 269615104 | bytes 2099200 | tf_op jit(solution)/shard_map/dot_general | solution.py:241
  (11 shorter events, 0.1 us)
Async XLA Ops:
  6.5 23.9 %copy-start = (bf16[1024,1024]{1,0:T(8,128)(2,1)S(1)}, bf16[1024,1024]{1,0:T(8,128)(2,1)}, u32[]{:S(2)}) copy-start(bf16[1024,1024]{1,0:T(8,128)(2,1)} %param.18) | copy-start | bytes 6291460
  6.5 118.6 %all-gather.3.cloned.1.call-start = ((), (), s32[]{:S(2)}) async-start(), calls=%async_computation.4 | async-start | bytes 5242880 | tf_op jit(solution)/shard_map/all_gather | solution.py:236
  12.9 6.9 %copy-start.6 = (s32[1,32]{1,0:T(1,128)S(1)}, s32[1,32]{1,0:T(1,128)}, u32[]{:S(2)}) copy-start(s32[1,32]{1,0:T(1,128)} %param.12) | copy-start | bytes 388
  12.9 7.2 %copy-start.5 = (s32[1,256,1]{1,2,0:T(1,128)S(1)}, s32[1,256,1]{1,2,0:T(1,128)}, u32[]{:S(2)}) copy-start(s32[1,256,1]{1,2,0:T(1,128)} %param.13) | copy-start | bytes 3076
  13.2 9.0 %copy-start.1 = (bf16[256,1024]{1,0:T(8,128)(2,1)}, bf16[256,1024]{1,0:T(8,128)(2,1)S(1)}, u32[]{:S(2)}) copy-start(bf16[256,1024]{1,0:T(8,128)(2,1)S(1)} %fusion.19.gated_ref) | copy-start | bytes 1572868
  13.2 17.2 %copy-start.2 = (bf16[1,256,1024]{2,1,0:T(8,128)(2,1)S(1)}, bf16[1,256,1024]{2,1,0:T(8,128)(2,1)}, u32[]{:S(2)}) copy-start(bf16[1,256,1024]{2,1,0:T(8,128)(2,1)} %param.11) | copy-start | bytes 1572868
  13.9 8.4 %collective-permute-start.1 = (bf16[15,1024]{1,0:T(8,128)(2,1)}, bf16[15,1024]{1,0:T(8,128)(2,1)S(1)}, u32[]{:S(2)}, u32[]{:S(2)}) collective-permute-start(bf16[15,1024]{1,0:T(8,128)(2,1)} %get-tuple-element.7), channel_id=1, source_target_pairs={{8,0},{16,8},{24,16},{32,24},{40,32},{48,40},{56,48},{64,56},{72,6... | collective-permute-start | bytes 92168 | tf_op jit(solution)/shard_map/ppermute | solution.py:87
  15.2 7.1 %collective-permute-start = (bf16[15,1024]{1,0:T(8,128)(2,1)}, bf16[15,1024]{1,0:T(8,128)(2,1)S(1)}, u32[]{:S(2)}, u32[]{:S(2)}) collective-permute-start(bf16[15,1024]{1,0:T(8,128)(2,1)} %get-tuple-element.8), channel_id=1, source_target_pairs={{0,8},{8,16},{16,24},{24,32},{32,40},{40,48},{48,56},{56,64},{64,7... | collective-permute-start | bytes 92168 | tf_op jit(solution)/shard_map/ppermute | solution.py:86
  22.3 0.6 copy-start.3
  22.3 0.6 copy-start.4
  79.5 108.5 %reduce-scatter.2.cloned.1.call-start = ((), (), s32[]{:S(2)}) async-start(), calls=%async_computation.3 | async-start | bytes 5242880 | tf_op jit(solution)/shard_map/reduce_scatter | solution.py:239
  136.4 62.5 %copy-start.7 = (bf16[1024,64]{0,1:T(8,128)(2,1)S(1)}, bf16[1024,64]{0,1:T(8,128)(2,1)}, u32[]{:S(2)}) copy-start(bf16[1024,64]{0,1:T(8,128)(2,1)} %param.19) | copy-start | bytes 393220
  188.0 38.7 %all-to-all-start.1 = ((bf16[64,8,1024]{2,1,0:T(8,128)(2,1)}), bf16[64,8,1024]{2,1,0:T(8,128)(2,1)}, u32[]{:S(2)}, u32[]{:S(2)}) async-start(bf16[64,8,1024]{2,1,0:T(8,128)(2,1)} %bitcast.66), calls=%async_computation.2 | async-start | bytes 2097152 | tf_op jit(solution)/shard_map/all_to_all | solution.py:240
Sparse Core Ops, SparseCore 0:
  79.6 45.4 all-gather.2
  136.5 51.4 reduce-scatter.1

commit v15 on v13

--- a/solution.py
+++ b/solution.py
@@ -8,7 +8,7 @@
 QUARTERS = 4
 ROW_BLOCK = 32
 LANE_BLOCK = 512
-ROW_TILE = 512
+ROW_TILE = 1024
 
 
 def depthwise_kernel(

time: 237 us -> 237 us (level)
  no operation moved by 1% of the time
where the time goes in v15:
time: 237 us; the launch traced here: 236 us
  waiting for transfers between devices  123 us (52%)
  blocking collectives  46.3 us (20%)
  Pallas kernels  20.8 us (9%)
  starting transfers between devices  16.8 us (7%)
  between operations  13.6 us (6%)
  matrix products  9.06 us (4%)
  other arithmetic  5.04 us (2%)
    reduce_scatter x1, waiting for transfers between devices, shards(): lax.psum_scatter(partial_out, 'y', scatter_dimension=0, tiled=False)  49.9 us
    all_to_all x1, blocking collectives, shards(): lax.all_to_all(send_buffer, ('z', 'expert'), split_axis=0, concat_axis=0,...  46.3 us
    all_gather x1, waiting for transfers between devices, shards(): gathered = lax.all_gather(by_member, 'y', axis=0, tiled=False)  45.6 us
    all_to_all x1, waiting for transfers between devices, shards(): lax.all_to_all(summed, ('z', 'expert'), split_axis=0, concat_axis=0, tile...  27.5 us
    pallas_call x1, Pallas kernels, expert_pass(): pl.pallas_call(expert_kernel, grid=(row_count // tile,), in_specs=[pl.Blo...  13.2 us
    all_to_all x1, starting transfers between devices, shards(): lax.all_to_all(summed, ('z', 'expert'), split_axis=0, concat_axis=0, tile...  10.8 us
    pallas_call x1, Pallas kernels, depthwise_silu(): pl.pallas_call(depthwise_kernel, grid=(width // LANE_BLOCK,), in_specs=[p...  7.54 us
  transfers between devices with their start and end apart: 5, of which 3 were waited for; matrix products, arithmetic and copies ran while one was open for 1% of the time, Pallas kernels for 0%

profile of v15, /device:TPU:1, one launch (start us, length us, event | category | flops | bytes accessed | tf_op | source)
XLA Modules:
  0.0 236.4 jit_solution(14837152144206164102)
XLA Ops:
  6.5 0.0 copy-start
  6.5 0.0 all-gather.3.cloned.1.call-start
  6.5 1.3 convert_reduce_fusion.1
  7.9 1.3 fusion.12
  9.2 3.7 %fusion.20 = f32[256,2048]{1,0:T(8,128)S(1)} fusion(bf16[1024,2048]{1,0:T(8,128)(2,1)} %param.14, bf16[1,256,1024]{2,1,0:T(8,128)(2,1)} %param.11, f32[256]{0:T(256)S(1)} %add_rsqrt_fusion.1, f32[256]{0:T(256)S(1)} %broadcast_multiply_fusion.1), kind=kOutput, calls=%fused_computation.30 | convolution fusion | flops 1074790400 | bytes 6817792 | tf_op jit(solution)/shard_map/dot_general | solution.py:143
  12.9 0.0 copy-start.6
  12.9 0.0 copy-start.5
  12.9 0.3 fusion.19.gated_ref
  13.2 0.0 copy-start.1
  13.3 0.0 copy-start.2
  13.3 0.6 fusion.36
  13.9 1.3 collective-permute-start.1
  15.2 4.7 %collective-permute-start = (bf16[15,1024]{1,0:T(8,128)(2,1)}, bf16[15,1024]{1,0:T(8,128)(2,1)S(1)}, u32[]{:S(2)}, u32[]{:S(2)}) collective-permute-start(bf16[15,1024]{1,0:T(8,128)(2,1)} %get-tuple-element.8), channel_id=1, source_target_pairs={{0,8},{8,16},{16,24},{24,32},{32,40},{40,48},{48,56},{56,64},{64,7... | collective-permute-start | bytes 92168 | tf_op jit(solution)/shard_map/ppermute | solution.py:86
  19.9 0.0 copy-done.6
  19.9 0.1 copy.26
  20.0 0.1 reduce-window.10
  20.0 0.1 reduce.1
  20.1 0.0 copy-done.5
  20.2 0.6 reduce-window.11
  20.8 0.2 slice_reduce_fusion
  21.0 0.1 select_reduce_fusion
  21.1 0.1 copy.28
  21.2 0.1 copy.29
  21.4 0.1 fusion.29
  21.5 0.7 fusion.26
  22.2 0.0 collective-permute-done.1.after_ref
  22.3 0.0 copy-start.3
  22.3 0.0 collective-permute-done.before_ref
  22.3 0.0 copy-start.4
  22.3 0.0 copy-done.1
  22.3 0.6 copy-done.3
  22.9 0.0 copy-done.4
  22.9 7.5 %shard_map.109 = bf16[256,1024]{1,0:T(8,128)(2,1)} custom-call(bf16[256,1024]{1,0:T(8,128)(2,1)} %copy-done.1, bf16[15,1024]{1,0:T(8,128)(2,1)} %copy-done.4, bf16[15,1024]{1,0:T(8,128)(2,1)} %copy-done.3, f32[31,1024]{1,0:T(8,128)} %taps_ref.1, s32[256,1]{1,0:T(8,128)} %get-tuple-element.12.first_ref, s32[256,1]{1,0:T(8,128)} %get-tuple-element.11.last_ref, ...), custom_call_target="tpu_custom_call" | custom-call | tf_op jit(solution)/shard_map/pallas_call | solution.py:59
  30.4 0.0 copy-done
  30.4 0.0 copy-done.2
  30.4 1.8 convert_reduce_fusion
  32.3 0.3 fusion.10
  32.6 0.6 fusion
  33.2 46.3 %all_to_all.10 = bf16[64,8,1024]{2,1,0:T(8,128)(2,1)} all-to-all(bf16[64,8,1024]{2,1,0:T(8,128)(2,1)S(1)} %fusion), channel_id=1, replica_groups=mesh['z'=8,'y'=4,'expert'=8] {'z','expert'}, dimensions={0} | all-to-all | bytes 2097152 | tf_op jit(solution)/shard_map/all_to_all | solution.py:196
  79.5 0.0 all-gather.3.cloned.1.call-update
  79.5 0.0 reduce-scatter.2.cloned.1.call-start
  79.6 45.6 %all-gather.3.cloned.1.call-done = bf16[256,8,1024]{2,1,0:T(8,128)(2,1)} async-done(((bf16[64,8,1024]{2,1,0:T(8,128)(2,1)}), bf16[256,8,1024]{2,1,0:T(8,128)(2,1)}) %all-gather.3.cloned.1.call-update) | async-done | bytes 4194320 | tf_op jit(solution)/shard_map/all_gather | solution.py:197
  125.2 13.2 %shard_map.110 = bf16[2048,1024]{1,0:T(8,128)(2,1)} custom-call(bf16[2048,1024]{1,0:T(8,128)(2,1)} %bitcast.58, bf16[1024,1024]{1,0:T(8,128)(2,1)} %bitcast.59, bf16[1024,1024]{1,0:T(8,128)(2,1)} %bitcast.60), custom_call_target="tpu_custom_call" | custom-call | tf_op jit(solution)/shard_map/pallas_call | solution.py:111
  138.4 0.0 reduce-scatter.2.cloned.1.call-update
  138.4 0.0 copy-start.7
  138.4 49.9 %reduce-scatter.2.cloned.1.call-done = bf16[1,64,8,1024]{3,2,1,0:T(8,128)(2,1)} async-done(((bf16[4,64,8,1024]{3,2,1,0:T(8,128)(2,1)}), bf16[1,64,8,1024]{3,2,1,0:T(8,128)(2,1)}) %reduce-scatter.2.cloned.1.call-update) | async-done | bytes 1048592 | tf_op jit(solution)/shard_map/reduce_scatter | solution.py:199
  188.3 10.8 %all-to-all-start.1 = ((bf16[64,8,1024]{2,1,0:T(8,128)(2,1)}), bf16[64,8,1024]{2,1,0:T(8,128)(2,1)}, u32[]{:S(2)}, u32[]{:S(2)}) async-start(bf16[64,8,1024]{2,1,0:T(8,128)(2,1)} %bitcast.61), calls=%async_computation.2 | async-start | bytes 2097152 | tf_op jit(solution)/shard_map/all_to_all | solution.py:200
  199.1 0.0 copy-done.7
  199.1 0.4 fusion.9
  199.6 27.5 %all-to-all-done.1 = bf16[64,8,1024]{2,1,0:T(8,128)(2,1)} async-done(((bf16[64,8,1024]{2,1,0:T(8,128)(2,1)}), bf16[64,8,1024]{2,1,0:T(8,128)(2,1)}, u32[]{:S(2)}, u32[]{:S(2)}) %all-to-all-start.1) | async-done | bytes 1048608 | tf_op jit(solution)/shard_map/all_to_all | solution.py:200
  227.0 2.5 %fusion.8 = bf16[1,256,1024]{2,1,0:T(8,128)(2,1)} fusion(bf16[256,1024]{1,0:T(8,128)(2,1)S(1)} %get-tuple-element.10, bf16[64,8,1024]{2,1,0:T(8,128)(2,1)} %all-to-all-done.1, f32[256]{0:T(256)S(1)} %add_divide_fusion, s32[256]{0:T(256)S(1)} %multiply_add_fusion), kind=kOutput, calls=%fused_computation.16 | convolution fusion | flops 269615104 | bytes 2099200 | tf_op jit(solution)/shard_map/dot_general | solution.py:201
  (11 shorter events, 0.1 us)
Async XLA Ops:
  6.5 23.9 %copy-start = (bf16[1024,1024]{1,0:T(8,128)(2,1)S(1)}, bf16[1024,1024]{1,0:T(8,128)(2,1)}, u32[]{:S(2)}) copy-start(bf16[1024,1024]{1,0:T(8,128)(2,1)} %param.18) | copy-start | bytes 6291460
  6.5 118.6 %all-gather.3.cloned.1.call-start = ((), (), s32[]{:S(2)}) async-start(), calls=%async_computation.4 | async-start | bytes 5242880 | tf_op jit(solution)/shard_map/all_gather | solution.py:197
  12.9 6.9 %copy-start.6 = (s32[1,32]{1,0:T(1,128)S(1)}, s32[1,32]{1,0:T(1,128)}, u32[]{:S(2)}) copy-start(s32[1,32]{1,0:T(1,128)} %param.12) | copy-start | bytes 388
  12.9 7.2 %copy-start.5 = (s32[1,256,1]{1,2,0:T(1,128)S(1)}, s32[1,256,1]{1,2,0:T(1,128)}, u32[]{:S(2)}) copy-start(s32[1,256,1]{1,2,0:T(1,128)} %param.13) | copy-start | bytes 3076
  13.2 9.0 %copy-start.1 = (bf16[256,1024]{1,0:T(8,128)(2,1)}, bf16[256,1024]{1,0:T(8,128)(2,1)S(1)}, u32[]{:S(2)}) copy-start(bf16[256,1024]{1,0:T(8,128)(2,1)S(1)} %fusion.19.gated_ref) | copy-start | bytes 1572868
  13.3 17.2 %copy-start.2 = (bf16[1,256,1024]{2,1,0:T(8,128)(2,1)S(1)}, bf16[1,256,1024]{2,1,0:T(8,128)(2,1)}, u32[]{:S(2)}) copy-start(bf16[1,256,1024]{2,1,0:T(8,128)(2,1)} %param.11) | copy-start | bytes 1572868
  13.9 8.4 %collective-permute-start.1 = (bf16[15,1024]{1,0:T(8,128)(2,1)}, bf16[15,1024]{1,0:T(8,128)(2,1)S(1)}, u32[]{:S(2)}, u32[]{:S(2)}) collective-permute-start(bf16[15,1024]{1,0:T(8,128)(2,1)} %get-tuple-element.7), channel_id=1, source_target_pairs={{8,0},{16,8},{24,16},{32,24},{40,32},{48,40},{56,48},{64,56},{72,6... | collective-permute-start | bytes 92168 | tf_op jit(solution)/shard_map/ppermute | solution.py:87
  15.2 7.1 %collective-permute-start = (bf16[15,1024]{1,0:T(8,128)(2,1)}, bf16[15,1024]{1,0:T(8,128)(2,1)S(1)}, u32[]{:S(2)}, u32[]{:S(2)}) collective-permute-start(bf16[15,1024]{1,0:T(8,128)(2,1)} %get-tuple-element.8), channel_id=1, source_target_pairs={{0,8},{8,16},{16,24},{24,32},{32,40},{40,48},{48,56},{56,64},{64,7... | collective-permute-start | bytes 92168 | tf_op jit(solution)/shard_map/ppermute | solution.py:86
  22.3 0.6 copy-start.3
  22.3 0.6 copy-start.4
  79.5 108.8 %reduce-scatter.2.cloned.1.call-start = ((), (), s32[]{:S(2)}) async-start(), calls=%async_computation.3 | async-start | bytes 5242880 | tf_op jit(solution)/shard_map/reduce_scatter | solution.py:199
  138.4 60.7 %copy-start.7 = (bf16[1024,64]{0,1:T(8,128)(2,1)S(1)}, bf16[1024,64]{0,1:T(8,128)(2,1)}, u32[]{:S(2)}) copy-start(bf16[1024,64]{0,1:T(8,128)(2,1)} %param.19) | copy-start | bytes 393220
  188.3 38.7 %all-to-all-start.1 = ((bf16[64,8,1024]{2,1,0:T(8,128)(2,1)}), bf16[64,8,1024]{2,1,0:T(8,128)(2,1)}, u32[]{:S(2)}, u32[]{:S(2)}) async-start(bf16[64,8,1024]{2,1,0:T(8,128)(2,1)} %bitcast.61), calls=%async_computation.2 | async-start | bytes 2097152 | tf_op jit(solution)/shard_map/all_to_all | solution.py:200
Sparse Core Ops, SparseCore 0:
  79.6 45.4 all-gather.2
  138.5 49.7 reduce-scatter.1

commit v16 on v13

--- a/solution.py
+++ b/solution.py
@@ -6,8 +6,8 @@
 from jax.sharding import Mesh, PartitionSpec as P
 
 QUARTERS = 4
-ROW_BLOCK = 32
-LANE_BLOCK = 512
+ROW_BLOCK = 16
+LANE_BLOCK = 1024
 ROW_TILE = 512
 
 

time: 237 us -> 237 us (level)
  no operation moved by 1% of the time
where the time goes in v16:
time: 237 us; the launch traced here: 236 us
  waiting for transfers between devices  123 us (52%)
  blocking collectives  46.3 us (20%)
  Pallas kernels  20.7 us (9%)
  starting transfers between devices  17 us (7%)
  between operations  13.6 us (6%)
  matrix products  9.06 us (4%)
  other arithmetic  5.04 us (2%)
    reduce_scatter x1, waiting for transfers between devices, shards(): lax.psum_scatter(partial_out, 'y', scatter_dimension=0, tiled=False)  49.9 us
    all_to_all x1, blocking collectives, shards(): lax.all_to_all(send_buffer, ('z', 'expert'), split_axis=0, concat_axis=0,...  46.3 us
    all_gather x1, waiting for transfers between devices, shards(): gathered = lax.all_gather(by_member, 'y', axis=0, tiled=False)  45.4 us
    all_to_all x1, waiting for transfers between devices, shards(): lax.all_to_all(summed, ('z', 'expert'), split_axis=0, concat_axis=0, tile...  27.5 us
    pallas_call x1, Pallas kernels, expert_pass(): pl.pallas_call(expert_kernel, grid=(row_count // tile,), in_specs=[pl.Blo...  13 us
    all_to_all x1, starting transfers between devices, shards(): lax.all_to_all(summed, ('z', 'expert'), split_axis=0, concat_axis=0, tile...  10.8 us
    pallas_call x1, Pallas kernels, depthwise_silu(): pl.pallas_call(depthwise_kernel, grid=(width // LANE_BLOCK,), in_specs=[p...  7.7 us
  transfers between devices with their start and end apart: 5, of which 3 were waited for; matrix products, arithmetic and copies ran while one was open for 1% of the time, Pallas kernels for 0%

profile of v16, /device:TPU:1, one launch (start us, length us, event | category | flops | bytes accessed | tf_op | source)
XLA Modules:
  0.0 236.3 jit_solution(4701881654222849176)
XLA Ops:
  6.5 0.0 copy-start
  6.5 0.0 all-gather.3.cloned.1.call-start
  6.5 1.3 convert_reduce_fusion.1
  7.9 1.3 fusion.12
  9.2 3.7 %fusion.20 = f32[256,2048]{1,0:T(8,128)S(1)} fusion(bf16[1024,2048]{1,0:T(8,128)(2,1)} %param.14, bf16[1,256,1024]{2,1,0:T(8,128)(2,1)} %param.11, f32[256]{0:T(256)S(1)} %add_rsqrt_fusion.1, f32[256]{0:T(256)S(1)} %broadcast_multiply_fusion.1), kind=kOutput, calls=%fused_computation.30 | convolution fusion | flops 1074790400 | bytes 6817792 | tf_op jit(solution)/shard_map/dot_general | solution.py:143
  12.9 0.0 copy-start.6
  12.9 0.0 copy-start.5
  13.0 0.3 fusion.19.gated_ref
  13.2 0.0 copy-start.1
  13.3 0.0 copy-start.2
  13.3 0.6 fusion.36
  13.9 1.3 collective-permute-start.1
  15.2 4.7 %collective-permute-start = (bf16[15,1024]{1,0:T(8,128)(2,1)}, bf16[15,1024]{1,0:T(8,128)(2,1)S(1)}, u32[]{:S(2)}, u32[]{:S(2)}) collective-permute-start(bf16[15,1024]{1,0:T(8,128)(2,1)} %get-tuple-element.8), channel_id=1, source_target_pairs={{0,8},{8,16},{16,24},{24,32},{32,40},{40,48},{48,56},{56,64},{64,7... | collective-permute-start | bytes 92168 | tf_op jit(solution)/shard_map/ppermute | solution.py:86
  19.9 0.0 copy-done.6
  19.9 0.1 copy.26
  20.0 0.1 reduce-window.10
  20.0 0.1 reduce.1
  20.1 0.0 copy-done.5
  20.2 0.6 reduce-window.11
  20.8 0.2 slice_reduce_fusion
  21.0 0.1 select_reduce_fusion
  21.1 0.1 copy.28
  21.2 0.1 copy.29
  21.4 0.1 fusion.29
  21.5 0.7 fusion.26
  22.2 0.0 collective-permute-done.1.after_ref
  22.2 0.0 copy-start.3
  22.3 0.0 collective-permute-done.before_ref
  22.3 0.0 copy-start.4
  22.3 0.0 copy-done.1
  22.3 0.6 copy-done.3
  22.9 0.0 copy-done.4
  22.9 7.7 %shard_map.109 = bf16[256,1024]{1,0:T(8,128)(2,1)} custom-call(bf16[256,1024]{1,0:T(8,128)(2,1)} %copy-done.1, bf16[15,1024]{1,0:T(8,128)(2,1)} %copy-done.4, bf16[15,1024]{1,0:T(8,128)(2,1)} %copy-done.3, f32[31,1024]{1,0:T(8,128)} %taps_ref.1, s32[256,1]{1,0:T(8,128)} %get-tuple-element.12.first_ref, s32[256,1]{1,0:T(8,128)} %get-tuple-element.11.last_ref, ...), custom_call_target="tpu_custom_call" | custom-call | tf_op jit(solution)/shard_map/pallas_call | solution.py:59
  30.6 0.0 copy-done
  30.6 0.0 copy-done.2
  30.6 1.8 convert_reduce_fusion
  32.4 0.3 fusion.10
  32.7 0.6 fusion
  33.4 46.3 %all_to_all.10 = bf16[64,8,1024]{2,1,0:T(8,128)(2,1)} all-to-all(bf16[64,8,1024]{2,1,0:T(8,128)(2,1)S(1)} %fusion), channel_id=1, replica_groups=mesh['z'=8,'y'=4,'expert'=8] {'z','expert'}, dimensions={0} | all-to-all | bytes 2097152 | tf_op jit(solution)/shard_map/all_to_all | solution.py:196
  79.7 0.0 all-gather.3.cloned.1.call-update
  79.7 0.2 reduce-scatter.2.cloned.1.call-start
  79.9 45.4 %all-gather.3.cloned.1.call-done = bf16[256,8,1024]{2,1,0:T(8,128)(2,1)} async-done(((bf16[64,8,1024]{2,1,0:T(8,128)(2,1)}), bf16[256,8,1024]{2,1,0:T(8,128)(2,1)}) %all-gather.3.cloned.1.call-update) | async-done | bytes 4194320 | tf_op jit(solution)/shard_map/all_gather | solution.py:197
  125.3 13.0 %shard_map.110 = bf16[2048,1024]{1,0:T(8,128)(2,1)} custom-call(bf16[2048,1024]{1,0:T(8,128)(2,1)} %bitcast.58, bf16[1024,1024]{1,0:T(8,128)(2,1)} %bitcast.59, bf16[1024,1024]{1,0:T(8,128)(2,1)} %bitcast.60), custom_call_target="tpu_custom_call" | custom-call | tf_op jit(solution)/shard_map/pallas_call | solution.py:111
  138.3 0.0 reduce-scatter.2.cloned.1.call-update
  138.3 0.0 copy-start.7
  138.3 49.9 %reduce-scatter.2.cloned.1.call-done = bf16[1,64,8,1024]{3,2,1,0:T(8,128)(2,1)} async-done(((bf16[4,64,8,1024]{3,2,1,0:T(8,128)(2,1)}), bf16[1,64,8,1024]{3,2,1,0:T(8,128)(2,1)}) %reduce-scatter.2.cloned.1.call-update) | async-done | bytes 1048592 | tf_op jit(solution)/shard_map/reduce_scatter | solution.py:199
  188.3 10.8 %all-to-all-start.1 = ((bf16[64,8,1024]{2,1,0:T(8,128)(2,1)}), bf16[64,8,1024]{2,1,0:T(8,128)(2,1)}, u32[]{:S(2)}, u32[]{:S(2)}) async-start(bf16[64,8,1024]{2,1,0:T(8,128)(2,1)} %bitcast.61), calls=%async_computation.2 | async-start | bytes 2097152 | tf_op jit(solution)/shard_map/all_to_all | solution.py:200
  199.1 0.0 copy-done.7
  199.1 0.4 fusion.9
  199.5 27.5 %all-to-all-done.1 = bf16[64,8,1024]{2,1,0:T(8,128)(2,1)} async-done(((bf16[64,8,1024]{2,1,0:T(8,128)(2,1)}), bf16[64,8,1024]{2,1,0:T(8,128)(2,1)}, u32[]{:S(2)}, u32[]{:S(2)}) %all-to-all-start.1) | async-done | bytes 1048608 | tf_op jit(solution)/shard_map/all_to_all | solution.py:200
  227.0 2.5 %fusion.8 = bf16[1,256,1024]{2,1,0:T(8,128)(2,1)} fusion(bf16[256,1024]{1,0:T(8,128)(2,1)S(1)} %get-tuple-element.10, bf16[64,8,1024]{2,1,0:T(8,128)(2,1)} %all-to-all-done.1, f32[256]{0:T(256)S(1)} %add_divide_fusion, s32[256]{0:T(256)S(1)} %multiply_add_fusion), kind=kOutput, calls=%fused_computation.16 | convolution fusion | flops 269615104 | bytes 2099200 | tf_op jit(solution)/shard_map/dot_general | solution.py:201
  (11 shorter events, 0.1 us)
Async XLA Ops:
  6.5 24.0 %copy-start = (bf16[1024,1024]{1,0:T(8,128)(2,1)S(1)}, bf16[1024,1024]{1,0:T(8,128)(2,1)}, u32[]{:S(2)}) copy-start(bf16[1024,1024]{1,0:T(8,128)(2,1)} %param.18) | copy-start | bytes 6291460
  6.5 118.8 %all-gather.3.cloned.1.call-start = ((), (), s32[]{:S(2)}) async-start(), calls=%async_computation.4 | async-start | bytes 5242880 | tf_op jit(solution)/shard_map/all_gather | solution.py:197
  12.9 6.9 %copy-start.6 = (s32[1,32]{1,0:T(1,128)S(1)}, s32[1,32]{1,0:T(1,128)}, u32[]{:S(2)}) copy-start(s32[1,32]{1,0:T(1,128)} %param.12) | copy-start | bytes 388
  12.9 7.2 %copy-start.5 = (s32[1,256,1]{1,2,0:T(1,128)S(1)}, s32[1,256,1]{1,2,0:T(1,128)}, u32[]{:S(2)}) copy-start(s32[1,256,1]{1,2,0:T(1,128)} %param.13) | copy-start | bytes 3076
  13.2 9.0 %copy-start.1 = (bf16[256,1024]{1,0:T(8,128)(2,1)}, bf16[256,1024]{1,0:T(8,128)(2,1)S(1)}, u32[]{:S(2)}) copy-start(bf16[256,1024]{1,0:T(8,128)(2,1)S(1)} %fusion.19.gated_ref) | copy-start | bytes 1572868
  13.3 17.3 %copy-start.2 = (bf16[1,256,1024]{2,1,0:T(8,128)(2,1)S(1)}, bf16[1,256,1024]{2,1,0:T(8,128)(2,1)}, u32[]{:S(2)}) copy-start(bf16[1,256,1024]{2,1,0:T(8,128)(2,1)} %param.11) | copy-start | bytes 1572868
  13.9 8.4 %collective-permute-start.1 = (bf16[15,1024]{1,0:T(8,128)(2,1)}, bf16[15,1024]{1,0:T(8,128)(2,1)S(1)}, u32[]{:S(2)}, u32[]{:S(2)}) collective-permute-start(bf16[15,1024]{1,0:T(8,128)(2,1)} %get-tuple-element.7), channel_id=1, source_target_pairs={{8,0},{16,8},{24,16},{32,24},{40,32},{48,40},{56,48},{64,56},{72,6... | collective-permute-start | bytes 92168 | tf_op jit(solution)/shard_map/ppermute | solution.py:87
  15.2 7.1 %collective-permute-start = (bf16[15,1024]{1,0:T(8,128)(2,1)}, bf16[15,1024]{1,0:T(8,128)(2,1)S(1)}, u32[]{:S(2)}, u32[]{:S(2)}) collective-permute-start(bf16[15,1024]{1,0:T(8,128)(2,1)} %get-tuple-element.8), channel_id=1, source_target_pairs={{0,8},{8,16},{16,24},{24,32},{32,40},{40,48},{48,56},{56,64},{64,7... | collective-permute-start | bytes 92168 | tf_op jit(solution)/shard_map/ppermute | solution.py:86
  22.2 0.6 copy-start.3
  22.3 0.6 copy-start.4
  79.7 108.6 %reduce-scatter.2.cloned.1.call-start = ((), (), s32[]{:S(2)}) async-start(), calls=%async_computation.3 | async-start | bytes 5242880 | tf_op jit(solution)/shard_map/reduce_scatter | solution.py:199
  138.3 60.7 %copy-start.7 = (bf16[1024,64]{0,1:T(8,128)(2,1)S(1)}, bf16[1024,64]{0,1:T(8,128)(2,1)}, u32[]{:S(2)}) copy-start(bf16[1024,64]{0,1:T(8,128)(2,1)} %param.19) | copy-start | bytes 393220
  188.3 38.7 %all-to-all-start.1 = ((bf16[64,8,1024]{2,1,0:T(8,128)(2,1)}), bf16[64,8,1024]{2,1,0:T(8,128)(2,1)}, u32[]{:S(2)}, u32[]{:S(2)}) async-start(bf16[64,8,1024]{2,1,0:T(8,128)(2,1)} %bitcast.61), calls=%async_computation.2 | async-start | bytes 2097152 | tf_op jit(solution)/shard_map/all_to_all | solution.py:200
Sparse Core Ops, SparseCore 0:
  79.8 45.4 all-gather.2
  138.4 49.7 reduce-scatter.1
